TPU v7x, 256 devices: a whole 4x4x8 slice. The times are simulated.
256 devices in a mesh: gx: 8 (over y_hi, x), gy: 32 (over z, y_lo, core).
Axes of the slice: x: 4, y: 4 (y_hi: 2, y_lo: 2; y = y_hi * 2 + y_lo), z: 8, core: 2. Of those that a mesh axis runs over, the one named last changes fastest.
Arguments:
- f_start: float32 [19, 4, 1024, 1024], P(None, None, 'gy', 'gx'), may hold values from 0.022 to 0.4, as said below
- cotangent: bfloat16 [19, 4, 1024, 1024], P(None, None, 'gy', 'gx'), may hold values from -6 to 6
- porosity: float32 [8, 32, 16], P('gx', 'gy'), may hold values from 0.1 to 0.9
- brick_ids: int32 [8, 32, 64], P('gx', 'gy'), may hold values from 0 to 127, as said below
- brick_slot: int32 [8, 32, 64], P('gx', 'gy'), may hold values from 0 to 15
Outputs:
- start_grad: float32 [19, 4, 1024, 1024], P(None, None, 'gy', 'gx')
- porosity_grad: float32 [8, 32, 16], P('gx', 'gy')
Inputs may be any that keep to these rules, and one draw needn't show every extreme that they name: `f_start`: each population is w_q times a factor between 0.8 and 1.2, w_q the weight of its direction. `brick_ids`: each device lists 64 distinct bricks of its own block; brick b covers layer b // 32, row b % 32 and all 128 cells along x of that block; device (0, 0) lists the last brick and device (0, 1) the first.
All inputs are finite; a program needn't handle non-finite values.
Results may differ from a plain program's by a relative error of at most 0.0003.
Values sent between devices are 32-bit elements; how exact they have to be, the bound alone decides.
No kernel may reach another device: no remote copies, remote signals or barrier semaphores. Data moves between devices by JAX's collectives and lax.ppermute only.
A program may use at most 64 MiB of HBM per device.

v0:
```python
import jax
import jax.numpy as jnp
import numpy as np
from jax import lax
from jax.sharding import PartitionSpec as P

DIR_X = np.array([0, 1, -1, 0, 0, 0, 0, 1, -1, 1, -1, 1, -1, 1, -1, 0, 0, 0, 0])
DIR_Y = np.array([0, 0, 0, 1, -1, 0, 0, 1, 1, -1, -1, 0, 0, 0, 0, 1, -1, 1, -1])
DIR_Z = np.array([0, 0, 0, 0, 0, 1, -1, 0, 0, 0, 0, 1, 1, -1, -1, 1, 1, -1, -1])
WEIGHTS = np.array([1.0 / 3.0] + [1.0 / 18.0] * 6 + [1.0 / 36.0] * 12)
RELAX_RATE = 0.8


def extended(array, sides, width):
    for axis, dim in sides:
        devices, length = (lax.axis_size(axis), array.shape[dim])
        up = [(i, (i + 1) % devices) for i in range(devices)]
        down = [(j, i) for i, j in up]
        last = lax.slice_in_dim(array, length - width, length, axis=dim)
        leading = lax.slice_in_dim(array, 0, width, axis=dim)
        before = lax.ppermute(last, axis, up)
        after = lax.ppermute(leading, axis, down)
        array = jnp.concatenate([before, array, after], axis=dim)
    return array


def column(values):
    return np.asarray(values, np.float32)[:, None, None, None]


def collide(field, solid):
    density = jnp.sum(field, axis=0)
    inverse = (1.0 - solid) / density
    vel_x = jnp.sum(field * column(DIR_X), axis=0) * inverse
    vel_y = jnp.sum(field * column(DIR_Y), axis=0) * inverse
    vel_z = jnp.sum(field * column(DIR_Z), axis=0) * inverse
    along = column(DIR_X) * vel_x + column(DIR_Y) * vel_y + column(DIR_Z) * vel_z
    square = vel_x * vel_x + vel_y * vel_y + vel_z * vel_z
    balance = column(WEIGHTS) * density * (1.0 + 3.0 * along + 4.5 * along * along - 1.5 * square)
    return field - RELAX_RATE * (field - balance)


def pull(padded, sign):
    height = padded.shape[2] - 2
    width = padded.shape[3] - 2
    moved = []
    for lane in range(19):
        row_start = 1 - sign * int(DIR_Y[lane])
        col_start = 1 - sign * int(DIR_X[lane])
        piece = padded[lane, :, row_start : row_start + height, col_start : col_start + width]
        moved.append(jnp.roll(piece, sign * int(DIR_Z[lane]), axis=0))
    return jnp.stack(moved)


def extend(field):
    return extended(field, (("gx", 3), ("gy", 2)), 1)


def on_device(f_start, cotangent, porosity, brick_ids, brick_slot):
    layers_dev = f_start.shape[1]
    rows_dev = f_start.shape[2]
    cols_dev = f_start.shape[3]
    tile_count = cols_dev // 128
    brick_count = layers_dev * rows_dev * tile_count
    listed = brick_ids.reshape(-1)
    slots_of = brick_slot.reshape(-1)
    slot_table = porosity.reshape(-1)
    brick_hit = (listed[:, None] == jnp.arange(brick_count, dtype=jnp.int32)[None, :]).astype(
        jnp.float32
    )
    slot_hit = (
        slots_of[:, None] == jnp.arange(slot_table.shape[0], dtype=jnp.int32)[None, :]
    ).astype(jnp.float32)
    brick_value = jnp.sum(slot_hit * slot_table[None, :], axis=1)
    tile_value = jnp.sum(brick_hit * brick_value[:, None], axis=0)
    solid = jnp.broadcast_to(
        tile_value.reshape(layers_dev, rows_dev, tile_count, 1),
        (layers_dev, rows_dev, tile_count, 128),
    ).reshape(layers_dev, rows_dev, cols_dev)
    back_last = cotangent.astype(jnp.float32)
    after_one = pull(extend(collide(f_start, solid)), 1)
    back_two = pull(extend(back_last), -1)
    ignored, undo_two = jax.vjp(collide, after_one, solid)
    back_one, solid_bar_two = undo_two(back_two)
    back_one_pulled = pull(extend(back_one), -1)
    ignored_first, undo_one = jax.vjp(collide, f_start, solid)
    start_grad, solid_bar_one = undo_one(back_one_pulled)
    solid_bar = solid_bar_one + solid_bar_two
    tile_sums = jnp.sum(solid_bar.reshape(brick_count, 128), axis=1)
    brick_sum = jnp.sum(brick_hit * tile_sums[None, :], axis=1)
    slot_grad = jnp.sum(slot_hit * brick_sum[:, None], axis=0)
    return (start_grad, slot_grad.reshape(porosity.shape))


def solution(mesh):
    return jax.shard_map(
        on_device,
        mesh=mesh,
        in_specs=(
            P(None, None, "gy", "gx"),
            P(None, None, "gy", "gx"),
            P("gx", "gy", None),
            P("gx", "gy", None),
            P("gx", "gy", None),
        ),
        out_specs=(P(None, None, "gy", "gx"), P("gx", "gy", None)),
        check_vma=False,
    )
```

profile of v0, /device:TPU:0, one launch (start us, length us, event | category | flops | bytes accessed | tf_op | source)
XLA Modules:
  0.0 89.8 jit_solution(18099506679010283507)
XLA Ops:
  0.7 0.9 select_reduce_fusion.3
  1.6 0.7 select_reduce_fusion.1
  2.4 1.7 %multiply_reduce_fusion.12 = (f32[4,32,128]{2,1,0:T(8,128)S(1)}, f32[4,32,128]{2,1,0:T(8,128)S(1)}, f32[4,32,128]{2,1,0:T(8,128)S(1)}, f32[4,32,128]{2,1,0:T(8,128)S(1)}) fusion(f32[19,4,32,128]{3,2,1,0:T(8,128)} %param.26, f32[19]{0:T(128)} %constant.33, f32[19]{0:T(128)} %constant.34, f32[19]{0:T(128)} %constant.35), kind=kLoop, calls=%fused_computation.39 | loop fusion | flops 2113536 | bytes 1507556 | tf_op jit(solution)/shard_map/reduce_sum | solution.py:34
  4.3 0.5 copy-done.13
  4.8 1.3 %fusion.2 = f32[19,4,32,128]{3,2,1,0:T(8,128)S(1)} fusion(f32[19,4,32,128]{3,2,1,0:T(8,128)S(1)} %copy-done.11, f32[4,32,128]{2,1,0:T(8,128)S(1)} %get-tuple-element.52, f32[4,32,128]{2,1,0:T(8,128)S(1)} %get-tuple-element.55, f32[19]{0:T(128)S(1)} %copy-done.20, f32[4,32,128]{2,1,0:T(8,128)S(1)} %get-tuple-element.54, f32[19]{0:T(128)S(1)} %copy-done.19, ...), kind=kLoop, calls=%fused_computation.8 | loop fusion | flops 4980736 | bytes 2818352 | tf_op jit(solution)/shard_map/sub | solution.py:40
  6.1 1.5 %fusion.63 = (f32[19,4,32,1]{3,2,1,0:T(8,128)S(1)}, f32[19,4,32,1]{3,2,1,0:T(8,128)}) fusion(f32[19,4,32,128]{3,2,1,0:T(8,128)S(1)} %fusion.2), kind=kLoop, calls=%fused_computation.305 | loop fusion | bytes 38912 | tf_op jit(solution)/shard_map/slice | solution.py:20
  7.6 2.5 %copy.122 = f32[19,4,32,1]{2,1,3,0:T(4,128)} copy(f32[19,4,32,1]{3,2,1,0:T(8,128)} %get-tuple-element.131) | data formatting | bytes 19456 | tf_op jit(solution)/shard_map/slice | solution.py:19
  10.1 1.1 %copy.124 = f32[19,4,32,1]{2,1,3,0:T(4,128)} copy(f32[19,4,32,1]{3,2,1,0:T(8,128)S(1)} %get-tuple-element.130) | data formatting | bytes 19456 | tf_op jit(solution)/shard_map/slice | solution.py:20
  11.2 5.6 %collective-permute-start.5 = (f32[19,4,32,1]{2,1,3,0:T(4,128)}, f32[19,4,32,1]{2,1,3,0:T(4,128)}, u32[]{:S(2)}, u32[]{:S(2)}) collective-permute-start(f32[19,4,32,1]{2,1,3,0:T(4,128)} %copy.124), channel_id=1, source_target_pairs={{32,0},{64,32},{96,64},{128,96},{160,128},{192,160},{224,192},{0,2... | collective-permute-start | bytes 29192 | tf_op jit(solution)/shard_map/ppermute | solution.py:22
  16.8 1.4 %fusion.64 = (f32[19,4,32,1]{3,2,1,0:T(8,128)S(1)}, f32[19,4,32,1]{3,2,1,0:T(8,128)}) fusion(bf16[19,4,32,128]{3,2,1,0:T(8,128)(2,1)S(1)} %copy-done.7), kind=kLoop, calls=%fused_computation.306 | loop fusion | bytes 38912 | tf_op jit(solution)/shard_map/slice | solution.py:19
  18.2 2.4 %copy.116 = f32[19,4,32,1]{2,1,3,0:T(4,128)} copy(f32[19,4,32,1]{3,2,1,0:T(8,128)} %get-tuple-element.139) | data formatting | bytes 19456 | tf_op jit(solution)/shard_map/slice | solution.py:20
  20.7 1.1 %copy.118 = f32[19,4,32,1]{2,1,3,0:T(4,128)} copy(f32[19,4,32,1]{3,2,1,0:T(8,128)S(1)} %get-tuple-element.138) | data formatting | bytes 19456 | tf_op jit(solution)/shard_map/slice | solution.py:19
  21.8 2.0 %collective-permute-start.1 = (f32[19,4,32,1]{2,1,3,0:T(4,128)}, f32[19,4,32,1]{2,1,3,0:T(4,128)}, u32[]{:S(2)}, u32[]{:S(2)}) collective-permute-start(f32[19,4,32,1]{2,1,3,0:T(4,128)} %copy.118), channel_id=1, source_target_pairs={{0,32},{32,64},{64,96},{96,128},{128,160},{160,192},{192,224},{224... | collective-permute-start | bytes 29192 | tf_op jit(solution)/shard_map/ppermute | solution.py:21
  23.8 0.6 constant_dynamic-update-slice_fusion.37
  24.4 0.1 convert_element_type.2
  24.6 0.6 constant_dynamic-update-slice_fusion.18
  25.2 2.3 %copy.123 = f32[19,4,32,1]{3,2,1,0:T(8,128)} copy(f32[19,4,32,1]{2,1,3,0:T(4,128)} %collective-permute-done.4) | data formatting | bytes 19456 | tf_op jit(solution)/shard_map/ppermute | solution.py:21
  27.6 2.4 %copy.125 = f32[19,4,32,1]{3,2,1,0:T(8,128)} copy(f32[19,4,32,1]{2,1,3,0:T(4,128)} %collective-permute-done.5) | data formatting | bytes 19456 | tf_op jit(solution)/shard_map/ppermute | solution.py:22
  29.9 1.1 %maximum_bitcast_fusion.28 = (f32[3,32,128]{2,1,0:T(8,128)S(1)}, f32[3,32,128]{2,1,0:T(8,128)S(1)}, f32[3,32,128]{2,1,0:T(8,128)S(1)}, f32[3,32,128]{2,1,0:T(8,128)S(1)}) fusion(f32[19,4,32,1]{3,2,1,0:T(8,128)} %copy.125, f32[19,4,32,128]{3,2,1,0:T(8,128)S(1)} %fusion.2, f32[19,4,32,1]{3,2,1,0:T(8,128)} %copy.123), kind=kLoop, calls=%fused_computation.220 | loop fusion | flops 36864 | bytes 1510400 | tf_op jit(solution)/shard_map/jit(_roll_static)/slice | solution.py:51
  31.1 0.2 copy-done.2
  31.3 0.4 copy-done.4
  31.8 0.5 pad_maximum_fusion.3
  32.3 2.4 %copy.117 = f32[19,4,32,1]{3,2,1,0:T(8,128)} copy(f32[19,4,32,1]{2,1,3,0:T(4,128)} %collective-permute-done) | data formatting | bytes 19456 | tf_op jit(solution)/shard_map/ppermute | solution.py:22
  34.7 2.3 %copy.119 = f32[19,4,32,1]{3,2,1,0:T(8,128)} copy(f32[19,4,32,1]{2,1,3,0:T(4,128)} %collective-permute-done.1) | data formatting | bytes 19456 | tf_op jit(solution)/shard_map/ppermute | solution.py:21
  37.0 2.0 %pad_maximum_fusion.6 = (f32[19,4,1,130]{3,2,1,0:T(1,128)S(1)}, f32[19,4,1,130]{3,2,1,0:T(1,128)S(1)}) fusion(f32[19,4,32,1]{3,2,1,0:T(8,128)} %copy.117, f32[19,4,32,128]{3,2,1,0:T(8,128)S(1)} %convert_element_type.2, f32[19,4,32,1]{3,2,1,0:T(8,128)} %copy.119), kind=kLoop, calls=%fused_computation.107 | loop fusion | flops 39520 | bytes 1343680 | tf_op jit(solution)/shard_map/concatenate | solution.py:23
  39.1 0.1 fusion.41
  39.4 3.8 %collective-permute-start.7 = (f32[19,4,1,130]{3,2,1,0:T(1,128)S(1)}, f32[19,4,1,130]{3,2,1,0:T(1,128)S(1)}, u32[]{:S(2)}, u32[]{:S(2)}) collective-permute-start(f32[19,4,1,130]{3,2,1,0:T(1,128)S(1)} %get-tuple-element.90), channel_id=1, source_target_pairs={{1,0},{2,1},{3,2},{4,3},{5,4},{6,5},{7,6},{8,7},{9,8},{10,9},{11,1... | collective-permute-start | bytes 118568 | tf_op jit(solution)/shard_map/ppermute | solution.py:22
  43.5 1.2 %copy-done.8 = f32[19,4,32,128]{3,2,1,0:T(8,128)S(1)} copy-done((f32[19,4,32,128]{3,2,1,0:T(8,128)S(1)}, f32[19,4,32,128]{3,2,1,0:T(8,128)}, u32[]{:S(2)}) %copy-start.8) | copy-done | bytes 1245208
  44.9 1.6 %collective-permute-start.2 = (f32[19,4,1,130]{3,2,1,0:T(1,128)S(1)}, f32[19,4,1,130]{3,2,1,0:T(1,128)S(1)}, u32[]{:S(2)}, u32[]{:S(2)}) collective-permute-start(f32[19,4,1,130]{3,2,1,0:T(1,128)S(1)} %get-tuple-element.97), channel_id=1, source_target_pairs={{1,0},{2,1},{3,2},{4,3},{5,4},{6,5},{7,6},{8,7},{9,8},{10,9},{11,1... | collective-permute-start | bytes 118568 | tf_op jit(solution)/shard_map/ppermute | solution.py:22
  46.7 0.1 maximum_bitcast_fusion.24
  47.1 0.1 constant_dynamic-update-slice_fusion.29
  47.3 0.1 constant_dynamic-update-slice_fusion.27
  47.5 0.3 multiply_reduce_fusion.9
  47.9 0.1 fusion.45
  48.1 0.4 collective-permute-done.2
  48.6 3.8 %collective-permute-done.3 = f32[19,4,1,130]{3,2,1,0:T(1,128)S(1)} collective-permute-done((f32[19,4,1,130]{3,2,1,0:T(1,128)S(1)}, f32[19,4,1,130]{3,2,1,0:T(1,128)S(1)}, u32[]{:S(2)}, u32[]{:S(2)}) %collective-permute-start.3) | collective-permute-done | bytes 39552 | tf_op jit(solution)/shard_map/ppermute | solution.py:21
  52.6 0.1 fusion.38
  52.8 0.1 constant_dynamic-update-slice_fusion.11
  53.4 0.4 copy-done.22
  53.8 1.3 %fusion.16 = (f32[4,32,128]{2,1,0:T(8,128)S(1)}, f32[4,32,128]{2,1,0:T(8,128)S(1)}, f32[4,32,128]{2,1,0:T(8,128)S(1)}, f32[4,32,128]{2,1,0:T(8,128)S(1)}, f32[4,32,128]{2,1,0:T(8,128)S(1)}) fusion(f32[19,4,32,128]{3,2,1,0:T(8,128)S(1)} %constant_dynamic-update-slice_fusion, f32[4,32,128]{2,1,0:T(8,128)S(1)} %bitcast.338, f32[19]{0:T(128)S(1)} %copy-done.22, ...), kind=kLoop, calls=%fused_computation.42 | loop fusion | flops 9879552 | bytes 1900848 | tf_op jit(solution)/shard_map/transpose(jvp())/reduce_sum | solution.py:39
  55.3 0.7 negate_add_fusion.1
  56.0 0.5 add_add_fusion.1
  56.5 1.5 %fusion.62 = (f32[19,4,32,1]{3,2,1,0:T(8,128)S(1)}, f32[19,4,32,1]{3,2,1,0:T(8,128)}) fusion(f32[19,4,32,128]{3,2,1,0:T(8,128)S(1)} %add_add_fusion.1), kind=kLoop, calls=%fused_computation.304 | loop fusion | bytes 38912 | tf_op jit(solution)/shard_map/slice | solution.py:19
  58.0 1.8 %copy.128 = f32[19,4,32,1]{2,1,3,0:T(4,128)S(1)} copy(f32[19,4,32,1]{3,2,1,0:T(8,128)} %get-tuple-element.123) | data formatting | bytes 19456 | tf_op jit(solution)/shard_map/slice | solution.py:20
  59.8 5.2 %collective-permute-start.8 = (f32[19,4,32,1]{2,1,3,0:T(4,128)S(1)}, f32[19,4,32,1]{2,1,3,0:T(4,128)S(1)}, u32[]{:S(2)}, u32[]{:S(2)}) collective-permute-start(f32[19,4,32,1]{2,1,3,0:T(4,128)S(1)} %copy.128), channel_id=1, source_target_pairs={{32,0},{64,32},{96,64},{128,96},{160,128},{192,160},{224,192},{0,2... | collective-permute-start | bytes 29192 | tf_op jit(solution)/shard_map/ppermute | solution.py:22
  65.0 0.5 copy.130
  65.6 0.6 constant_dynamic-update-slice_fusion.56
  66.2 0.4 collective-permute-done.8
  66.6 0.5 copy.129
  67.2 6.0 %collective-permute-done.9 = f32[19,4,32,1]{2,1,3,0:T(4,128)S(1)} collective-permute-done((f32[19,4,32,1]{2,1,3,0:T(4,128)S(1)}, f32[19,4,32,1]{2,1,3,0:T(4,128)S(1)}, u32[]{:S(2)}, u32[]{:S(2)}) %collective-permute-start.9) | collective-permute-done | bytes 9760 | tf_op jit(solution)/shard_map/ppermute | solution.py:21
  73.1 1.6 %copy.131 = f32[19,4,32,1]{3,2,1,0:T(8,128)} copy(f32[19,4,32,1]{2,1,3,0:T(4,128)S(1)} %collective-permute-done.9) | data formatting | bytes 19456 | tf_op jit(solution)/shard_map/ppermute | solution.py:21
  74.7 1.7 %pad_maximum_fusion = (f32[19,4,1,130]{3,2,1,0:T(1,128)S(1)}, f32[19,4,1,130]{3,2,1,0:T(1,128)S(1)}) fusion(f32[19,4,32,1]{3,2,1,0:T(8,128)S(1)} %copy.129, f32[19,4,32,128]{3,2,1,0:T(8,128)S(1)} %add_add_fusion.1, f32[19,4,32,1]{3,2,1,0:T(8,128)} %copy.131), kind=kLoop, calls=%fused_computation.101 | loop fusion | flops 39520 | bytes 1343680 | tf_op jit(solution)/shard_map/concatenate | solution.py:23
  76.4 0.1 fusion.37
  76.8 0.5 collective-permute-start.11
  77.3 0.6 copy-done.9
  78.1 0.7 collective-permute-done.10
  78.9 3.9 %collective-permute-done.11 = f32[19,4,1,130]{3,2,1,0:T(1,128)S(1)} collective-permute-done((f32[19,4,1,130]{3,2,1,0:T(1,128)S(1)}, f32[19,4,1,130]{3,2,1,0:T(1,128)S(1)}, u32[]{:S(2)}, u32[]{:S(2)}) %collective-permute-start.11) | collective-permute-done | bytes 39552 | tf_op jit(solution)/shard_map/ppermute | solution.py:21
  83.0 0.1 fusion.34
  83.8 0.6 copy-done.16
  84.4 1.3 %fusion.17 = (f32[4,32,128]{2,1,0:T(8,128)S(1)}, f32[4,32,128]{2,1,0:T(8,128)S(1)}, f32[4,32,128]{2,1,0:T(8,128)S(1)}, f32[4,32,128]{2,1,0:T(8,128)S(1)}, f32[4,32,128]{2,1,0:T(8,128)S(1)}) fusion(f32[19,4,32,128]{3,2,1,0:T(8,128)S(1)} %constant_dynamic-update-slice_fusion.38, f32[4,32,128]{2,1,0:T(8,128)S(1)} %get-tuple-element.19, f32[19]{0:T(128)S(1)} %copy-done.22, ...), kind=kLoop, calls=%fused_computation.43 | loop fusion | flops 9879552 | bytes 1900848 | tf_op jit(solution)/shard_map/transpose(jvp())/reduce_sum | solution.py:39
  85.7 0.2 add_reduce_fusion
  86.0 0.2 select_reduce_fusion
  86.2 0.6 select_reduce_fusion.2
  86.9 2.8 %add_add_fusion = f32[19,4,32,128]{3,2,1,0:T(8,128)} fusion(f32[19,4,32,128]{3,2,1,0:T(8,128)} %copy-done.10, f32[4,32,128]{2,1,0:T(8,128)S(1)} %negate_add_fusion, f32[4,32,128]{2,1,0:T(8,128)S(1)} %get-tuple-element.144, f32[4,32,128]{2,1,0:T(8,128)S(1)} %get-tuple-element.143, f32[4,32,128]{2,1,0:T(8,128)S(1)} %get-tuple-element.142, ...), kind=kLoop, calls=%fused_computation.21 | loop fusion | flops 3112960 | bytes 2752740 | tf_op jit(solution)/shard_map/transpose(jvp())/add_any | solution.py:32
  (119 shorter events, 3.8 us)
Async XLA Ops:
  0.6 4.1 %copy-start.18 = (f32[19]{0:T(128)S(1)}, f32[19]{0:T(128)}, u32[]{:S(2)}) copy-start(f32[19]{0:T(128)} %constant.33) | copy-start | bytes 232
  0.6 4.1 %copy-start.19 = (f32[19]{0:T(128)S(1)}, f32[19]{0:T(128)}, u32[]{:S(2)}) copy-start(f32[19]{0:T(128)} %constant.34) | copy-start | bytes 232
  0.7 4.1 %copy-start.20 = (f32[19]{0:T(128)S(1)}, f32[19]{0:T(128)}, u32[]{:S(2)}) copy-start(f32[19]{0:T(128)} %constant.35) | copy-start | bytes 232
  0.7 4.1 %copy-start.21 = (f32[19]{0:T(128)S(1)}, f32[19]{0:T(128)}, u32[]{:S(2)}) copy-start(f32[19]{0:T(128)} %constant.32) | copy-start | bytes 232
  0.7 4.1 %copy-start.11 = (f32[19,4,32,128]{3,2,1,0:T(8,128)S(1)}, f32[19,4,32,128]{3,2,1,0:T(8,128)}, u32[]{:S(2)}) copy-start(f32[19,4,32,128]{3,2,1,0:T(8,128)} %param.26) | copy-start | bytes 3735556
  4.1 0.6 copy-start.13
  4.3 1.8 %copy-start.15 = (f32[4,32,128]{2,1,0:T(8,128)}, f32[4,32,128]{2,1,0:T(8,128)S(1)}, u32[]{:S(2)}) copy-start(f32[4,32,128]{2,1,0:T(8,128)S(1)} %get-tuple-element.52) | copy-start | bytes 196612
  7.6 9.2 %copy-start.7 = (bf16[19,4,32,128]{3,2,1,0:T(8,128)(2,1)S(1)}, bf16[19,4,32,128]{3,2,1,0:T(8,128)(2,1)}, u32[]{:S(2)}) copy-start(bf16[19,4,32,128]{3,2,1,0:T(8,128)(2,1)} %param.27) | copy-start | bytes 1867780
  10.1 15.1 %collective-permute-start.4 = (f32[19,4,32,1]{2,1,3,0:T(4,128)}, f32[19,4,32,1]{2,1,3,0:T(4,128)}, u32[]{:S(2)}, u32[]{:S(2)}) collective-permute-start(f32[19,4,32,1]{2,1,3,0:T(4,128)} %copy.122), channel_id=1, source_target_pairs={{0,32},{32,64},{64,96},{96,128},{128,160},{160,192},{192,224},{224... | collective-permute-start | bytes 29192 | tf_op jit(solution)/shard_map/ppermute | solution.py:21
  11.2 16.4 %collective-permute-start.5 = (f32[19,4,32,1]{2,1,3,0:T(4,128)}, f32[19,4,32,1]{2,1,3,0:T(4,128)}, u32[]{:S(2)}, u32[]{:S(2)}) collective-permute-start(f32[19,4,32,1]{2,1,3,0:T(4,128)} %copy.124), channel_id=1, source_target_pairs={{32,0},{64,32},{96,64},{128,96},{160,128},{192,160},{224,192},{0,2... | collective-permute-start | bytes 29192 | tf_op jit(solution)/shard_map/ppermute | solution.py:22
  20.6 11.7 %collective-permute-start = (f32[19,4,32,1]{2,1,3,0:T(4,128)}, f32[19,4,32,1]{2,1,3,0:T(4,128)}, u32[]{:S(2)}, u32[]{:S(2)}) collective-permute-start(f32[19,4,32,1]{2,1,3,0:T(4,128)} %copy.116), channel_id=1, source_target_pairs={{32,0},{64,32},{96,64},{128,96},{160,128},{192,160},{224,192},{0,2... | collective-permute-start | bytes 29192 | tf_op jit(solution)/shard_map/ppermute | solution.py:22
  21.8 12.8 %collective-permute-start.1 = (f32[19,4,32,1]{2,1,3,0:T(4,128)}, f32[19,4,32,1]{2,1,3,0:T(4,128)}, u32[]{:S(2)}, u32[]{:S(2)}) collective-permute-start(f32[19,4,32,1]{2,1,3,0:T(4,128)} %copy.118), channel_id=1, source_target_pairs={{0,32},{32,64},{64,96},{96,128},{128,160},{160,192},{192,224},{224... | collective-permute-start | bytes 29192 | tf_op jit(solution)/shard_map/ppermute | solution.py:21
  29.9 1.4 %copy-start.2 = (f32[19,4,32,1]{3,2,1,0:T(8,128)S(1)}, f32[19,4,32,1]{3,2,1,0:T(8,128)}, u32[]{:S(2)}) copy-start(f32[19,4,32,1]{3,2,1,0:T(8,128)} %copy.123) | copy-start | bytes 29188
  29.9 1.7 %copy-start.4 = (f32[19,4,32,1]{3,2,1,0:T(8,128)S(1)}, f32[19,4,32,1]{3,2,1,0:T(8,128)}, u32[]{:S(2)}) copy-start(f32[19,4,32,1]{3,2,1,0:T(8,128)} %copy.125) | copy-start | bytes 29188
  37.0 2.0 %copy-start = (f32[19,4,32,1]{3,2,1,0:T(8,128)S(1)}, f32[19,4,32,1]{3,2,1,0:T(8,128)}, u32[]{:S(2)}) copy-start(f32[19,4,32,1]{3,2,1,0:T(8,128)} %copy.117) | copy-start | bytes 29188
  37.0 2.1 %copy-start.1 = (f32[19,4,32,1]{3,2,1,0:T(8,128)S(1)}, f32[19,4,32,1]{3,2,1,0:T(8,128)}, u32[]{:S(2)}) copy-start(f32[19,4,32,1]{3,2,1,0:T(8,128)} %copy.119) | copy-start | bytes 29188
  39.2 4.1 %copy-start.3 = (f32[19,4,32,1]{3,2,1,0:T(8,128)S(1)}, f32[19,4,32,1]{3,2,1,0:T(8,128)}, u32[]{:S(2)}) copy-start(f32[19,4,32,1]{3,2,1,0:T(8,128)} %copy.123) | copy-start | bytes 29188
  39.2 4.0 %copy-start.12 = (f32[19,4,32,128]{3,2,1,0:T(8,128)S(1)}, f32[19,4,32,128]{3,2,1,0:T(8,128)}, u32[]{:S(2)}) copy-start(f32[19,4,32,128]{3,2,1,0:T(8,128)} %constant_dynamic-update-slice_fusion.37) | copy-start | bytes 3735556
  39.3 7.1 %collective-permute-start.6 = (f32[19,4,1,130]{3,2,1,0:T(1,128)S(1)}, f32[19,4,1,130]{3,2,1,0:T(1,128)S(1)}, u32[]{:S(2)}, u32[]{:S(2)}) collective-permute-start(f32[19,4,1,130]{3,2,1,0:T(1,128)S(1)} %get-tuple-element.91), channel_id=1, source_target_pairs={{0,1},{1,2},{2,3},{3,4},{4,5},{5,6},{6,7},{7,8},{8,9},{9,10},{10,1... | collective-permute-start | bytes 118568 | tf_op jit(solution)/shard_map/ppermute | solution.py:21
  39.4 3.9 %copy-start.5 = (f32[19,4,32,1]{3,2,1,0:T(8,128)S(1)}, f32[19,4,32,1]{3,2,1,0:T(8,128)}, u32[]{:S(2)}) copy-start(f32[19,4,32,1]{3,2,1,0:T(8,128)} %copy.125) | copy-start | bytes 29188
  39.4 7.1 %collective-permute-start.7 = (f32[19,4,1,130]{3,2,1,0:T(1,128)S(1)}, f32[19,4,1,130]{3,2,1,0:T(1,128)S(1)}, u32[]{:S(2)}, u32[]{:S(2)}) collective-permute-start(f32[19,4,1,130]{3,2,1,0:T(1,128)S(1)} %get-tuple-element.90), channel_id=1, source_target_pairs={{1,0},{2,1},{3,2},{4,3},{5,4},{6,5},{7,6},{8,7},{9,8},{10,9},{11,1... | collective-permute-start | bytes 118568 | tf_op jit(solution)/shard_map/ppermute | solution.py:22
  43.4 1.3 %copy-start.8 = (f32[19,4,32,128]{3,2,1,0:T(8,128)S(1)}, f32[19,4,32,128]{3,2,1,0:T(8,128)}, u32[]{:S(2)}) copy-start(f32[19,4,32,128]{3,2,1,0:T(8,128)} %constant_dynamic-update-slice_fusion.18) | copy-start | bytes 3735556
  44.9 3.6 %collective-permute-start.2 = (f32[19,4,1,130]{3,2,1,0:T(1,128)S(1)}, f32[19,4,1,130]{3,2,1,0:T(1,128)S(1)}, u32[]{:S(2)}, u32[]{:S(2)}) collective-permute-start(f32[19,4,1,130]{3,2,1,0:T(1,128)S(1)} %get-tuple-element.97), channel_id=1, source_target_pairs={{1,0},{2,1},{3,2},{4,3},{5,4},{6,5},{7,6},{8,7},{9,8},{10,9},{11,1... | collective-permute-start | bytes 118568 | tf_op jit(solution)/shard_map/ppermute | solution.py:22
  46.5 5.9 %collective-permute-start.3 = (f32[19,4,1,130]{3,2,1,0:T(1,128)S(1)}, f32[19,4,1,130]{3,2,1,0:T(1,128)S(1)}, u32[]{:S(2)}, u32[]{:S(2)}) collective-permute-start(f32[19,4,1,130]{3,2,1,0:T(1,128)S(1)} %get-tuple-element.96), channel_id=1, source_target_pairs={{0,1},{1,2},{2,3},{3,4},{4,5},{5,6},{6,7},{7,8},{8,9},{9,10},{10,1... | collective-permute-start | bytes 118568 | tf_op jit(solution)/shard_map/ppermute | solution.py:21
  53.1 0.7 copy-start.22
  59.8 6.8 %collective-permute-start.8 = (f32[19,4,32,1]{2,1,3,0:T(4,128)S(1)}, f32[19,4,32,1]{2,1,3,0:T(4,128)S(1)}, u32[]{:S(2)}, u32[]{:S(2)}) collective-permute-start(f32[19,4,32,1]{2,1,3,0:T(4,128)S(1)} %copy.128), channel_id=1, source_target_pairs={{32,0},{64,32},{96,64},{128,96},{160,128},{192,160},{224,192},{0,2... | collective-permute-start | bytes 29192 | tf_op jit(solution)/shard_map/ppermute | solution.py:22
  65.5 7.7 %collective-permute-start.9 = (f32[19,4,32,1]{2,1,3,0:T(4,128)S(1)}, f32[19,4,32,1]{2,1,3,0:T(4,128)S(1)}, u32[]{:S(2)}, u32[]{:S(2)}) collective-permute-start(f32[19,4,32,1]{2,1,3,0:T(4,128)S(1)} %copy.130), channel_id=1, source_target_pairs={{0,32},{32,64},{64,96},{96,128},{128,160},{160,192},{192,224},{224... | collective-permute-start | bytes 29192 | tf_op jit(solution)/shard_map/ppermute | solution.py:21
  74.7 1.7 %copy-start.6 = (f32[19,4,32,1]{3,2,1,0:T(8,128)S(1)}, f32[19,4,32,1]{3,2,1,0:T(8,128)}, u32[]{:S(2)}) copy-start(f32[19,4,32,1]{3,2,1,0:T(8,128)} %copy.131) | copy-start | bytes 29188
  76.6 1.3 %copy-start.9 = (f32[19,4,32,128]{3,2,1,0:T(8,128)S(1)}, f32[19,4,32,128]{3,2,1,0:T(8,128)}, u32[]{:S(2)}) copy-start(f32[19,4,32,128]{3,2,1,0:T(8,128)} %constant_dynamic-update-slice_fusion.56) | copy-start | bytes 3735556
  76.7 2.1 %collective-permute-start.10 = (f32[19,4,1,130]{3,2,1,0:T(1,128)S(1)}, f32[19,4,1,130]{3,2,1,0:T(1,128)S(1)}, u32[]{:S(2)}, u32[]{:S(2)}) collective-permute-start(f32[19,4,1,130]{3,2,1,0:T(1,128)S(1)} %get-tuple-element.85), channel_id=1, source_target_pairs={{1,0},{2,1},{3,2},{4,3},{5,4},{6,5},{7,6},{8,7},{9,8},{10,9},{11,1... | collective-permute-start | bytes 118568 | tf_op jit(solution)/shard_map/ppermute | solution.py:22
  76.8 6.0 %collective-permute-start.11 = (f32[19,4,1,130]{3,2,1,0:T(1,128)S(1)}, f32[19,4,1,130]{3,2,1,0:T(1,128)S(1)}, u32[]{:S(2)}, u32[]{:S(2)}) collective-permute-start(f32[19,4,1,130]{3,2,1,0:T(1,128)S(1)} %get-tuple-element.84), channel_id=1, source_target_pairs={{0,1},{1,2},{2,3},{3,4},{4,5},{5,6},{6,7},{7,8},{8,9},{9,10},{10,1... | collective-permute-start | bytes 118568 | tf_op jit(solution)/shard_map/ppermute | solution.py:21
  83.5 0.8 copy-start.16
  83.7 2.0 %copy-start.14 = (f32[4,32,128]{2,1,0:T(8,128)S(1)}, f32[4,32,128]{2,1,0:T(8,128)}, u32[]{:S(2)}) copy-start(f32[4,32,128]{2,1,0:T(8,128)} %copy-done.13) | copy-start | bytes 196612
  83.7 2.0 %copy-start.17 = (f32[4,32,128]{2,1,0:T(8,128)S(1)}, f32[4,32,128]{2,1,0:T(8,128)}, u32[]{:S(2)}) copy-start(f32[4,32,128]{2,1,0:T(8,128)} %get-tuple-element.32) | copy-start | bytes 196612
  84.4 1.6 %copy-start.10 = (f32[19,4,32,128]{3,2,1,0:T(8,128)}, f32[19,4,32,128]{3,2,1,0:T(8,128)S(1)}, u32[]{:S(2)}) copy-start(f32[19,4,32,128]{3,2,1,0:T(8,128)S(1)} %constant_dynamic-update-slice_fusion.38) | copy-start | bytes 3735556
  84.4 1.6 %copy-start.23 = (s32[1,1,64]{2,1,0:T(1,128)S(1)}, s32[1,1,64]{2,1,0:T(1,128)}, u32[]{:S(2)}) copy-start(s32[1,1,64]{2,1,0:T(1,128)} %param.29) | copy-start | bytes 772
  84.4 1.8 %copy-start.24 = (s32[1,1,64]{2,1,0:T(1,128)S(1)}, s32[1,1,64]{2,1,0:T(1,128)}, u32[]{:S(2)}) copy-start(s32[1,1,64]{2,1,0:T(1,128)} %param.30) | copy-start | bytes 772
where the time goes:
time: 90.5 us; the launch traced here: 89.8 us
  local copies, waits for them, and re-layouts  31.5 us (35%)
  other arithmetic  22.6 us (25%)
  starting transfers between devices  19 us (21%)
  waiting for transfers between devices  15.2 us (17%)
  between operations  1.48 us (2%)
    ppermute x6, starting transfers between devices, extended(): after = lax.ppermute(leading, axis, down)  16.4 us
    ppermute x6, waiting for transfers between devices, extended(): before = lax.ppermute(last, axis, up)  13.7 us
    slice x5, local copies, waits for them, and re-layouts, extended(): last = lax.slice_in_dim(array, length - width, length, axis=dim)  7 us
    slice x4, local copies, waits for them, and re-layouts, extended(): leading = lax.slice_in_dim(array, 0, width, axis=dim)  6.84 us
    ppermute x3, local copies, waits for them, and re-layouts, extended(): before = lax.ppermute(last, axis, up)  6.26 us
    unnamed x53, local copies, waits for them, and re-layouts  5.98 us
    ppermute x3, local copies, waits for them, and re-layouts, extended(): after = lax.ppermute(leading, axis, down)  5.24 us
    concatenate x3, other arithmetic, extended(): array = jnp.concatenate([before, array, after], axis=dim)  4.22 us
  transfers between devices with their start and end apart: 12, of which 6 were waited for; matrix products, arithmetic and copies ran while one was open for 22% of the time, Pallas kernels for 0%

commit v1 on v0

--- a/solution.py
+++ b/solution.py
@@ -9,19 +9,7 @@
 DIR_Z = np.array([0, 0, 0, 0, 0, 1, -1, 0, 0, 0, 0, 1, 1, -1, -1, 1, 1, -1, -1])
 WEIGHTS = np.array([1.0 / 3.0] + [1.0 / 18.0] * 6 + [1.0 / 36.0] * 12)
 RELAX_RATE = 0.8
-
-
-def extended(array, sides, width):
-    for axis, dim in sides:
-        devices, length = (lax.axis_size(axis), array.shape[dim])
-        up = [(i, (i + 1) % devices) for i in range(devices)]
-        down = [(j, i) for i, j in up]
-        last = lax.slice_in_dim(array, length - width, length, axis=dim)
-        leading = lax.slice_in_dim(array, 0, width, axis=dim)
-        before = lax.ppermute(last, axis, up)
-        after = lax.ppermute(leading, axis, down)
-        array = jnp.concatenate([before, array, after], axis=dim)
-    return array
+HI = lax.Precision.HIGHEST
 
 
 def column(values):
@@ -52,8 +40,72 @@
     return jnp.stack(moved)
 
 
-def extend(field):
-    return extended(field, (("gx", 3), ("gy", 2)), 1)
+def one_hot(rows, width, lanes):
+    table = np.zeros((rows, width), np.float32)
+    for k, lane in enumerate(lanes):
+        table[k, lane] = 1.0
+    return table
+
+
+def exchange(fields):
+    nx = lax.axis_size("gx")
+    ny = lax.axis_size("gy")
+    count = len(fields)
+    q, layers, height, width = fields[0].shape
+    rows = q * layers * height
+    pick = jnp.asarray(one_hot(2, width, (0, width - 1)))
+    packed = [
+        jnp.einsum("kx,nx->kn", pick, g.reshape(rows, width), precision=HI,
+                   preferred_element_type=jnp.float32)
+        for g in fields
+    ]
+    first_col = jnp.stack([p[0] for p in packed])
+    last_col = jnp.stack([p[1] for p in packed])
+    first_row = jnp.stack([g[:, :, 0, :] for g in fields])
+    last_row = jnp.stack([g[:, :, height - 1, :] for g in fields])
+    cols3 = [p.reshape(2, q, layers, height) for p in packed]
+    c00 = jnp.stack([c[0, :, :, 0] for c in cols3])
+    c0l = jnp.stack([c[1, :, :, 0] for c in cols3])
+    cl0 = jnp.stack([c[0, :, :, height - 1] for c in cols3])
+    cll = jnp.stack([c[1, :, :, height - 1] for c in cols3])
+
+    def lin(i, j):
+        return i * ny + j
+
+    def shift_x(value, step):
+        return lax.ppermute(value, "gx", [(i, (i + step) % nx) for i in range(nx)])
+
+    def shift_y(value, step):
+        return lax.ppermute(value, "gy", [(j, (j + step) % ny) for j in range(ny)])
+
+    def shift_xy(value, sx, sy):
+        pairs = [(lin(i, j), lin((i + sx) % nx, (j + sy) % ny)) for i in range(nx) for j in range(ny)]
+        return lax.ppermute(value, ("gx", "gy"), pairs)
+
+    before_x = shift_x(last_col, 1)
+    after_x = shift_x(first_col, -1)
+    before_y = shift_y(last_row, 1)
+    after_y = shift_y(first_row, -1)
+    corner_bb = shift_xy(cll, 1, 1)
+    corner_ba = shift_xy(cl0, -1, 1)
+    corner_ab = shift_xy(c0l, 1, -1)
+    corner_aa = shift_xy(c00, -1, -1)
+
+    place = jnp.asarray(one_hot(2, width + 2, (0, width + 1)))
+    out = []
+    for n, g in enumerate(fields):
+        halo_cols = jnp.stack([before_x[n], after_x[n]])
+        sides = jnp.einsum("kn,kx->nx", halo_cols, place, precision=HI,
+                           preferred_element_type=jnp.float32).reshape(q, layers, height, width + 2)
+        middle = jnp.pad(g, ((0, 0), (0, 0), (0, 0), (1, 1))) + sides
+        top = jnp.concatenate(
+            [corner_bb[n][:, :, None], before_y[n], corner_ba[n][:, :, None]], axis=2
+        )[:, :, None, :]
+        bottom = jnp.concatenate(
+            [corner_ab[n][:, :, None], after_y[n], corner_aa[n][:, :, None]], axis=2
+        )[:, :, None, :]
+        out.append(jnp.concatenate([top, middle, bottom], axis=2))
+    return out
 
 
 def on_device(f_start, cotangent, porosity, brick_ids, brick_slot):
@@ -78,11 +130,13 @@
         (layers_dev, rows_dev, tile_count, 128),
     ).reshape(layers_dev, rows_dev, cols_dev)
     back_last = cotangent.astype(jnp.float32)
-    after_one = pull(extend(collide(f_start, solid)), 1)
-    back_two = pull(extend(back_last), -1)
+    collided, cot_ext = exchange([collide(f_start, solid), back_last])
+    after_one = pull(collided, 1)
+    back_two = pull(cot_ext, -1)
     ignored, undo_two = jax.vjp(collide, after_one, solid)
     back_one, solid_bar_two = undo_two(back_two)
-    back_one_pulled = pull(extend(back_one), -1)
+    (back_one_ext,) = exchange([back_one])
+    back_one_pulled = pull(back_one_ext, -1)
     ignored_first, undo_one = jax.vjp(collide, f_start, solid)
     start_grad, solid_bar_one = undo_one(back_one_pulled)
     solid_bar = solid_bar_one + solid_bar_two

time: 90.5 us -> 94 us (1.039)
  the two profiles are of different devices: /device:TPU:0 before, /device:TPU:121 now
where the time goes in v1:
time: 94 us; the launch traced here: 93.3 us
  starting transfers between devices  35.6 us (38%)
  other arithmetic  24.1 us (26%)
  local copies, waits for them, and re-layouts  15.9 us (17%)
  waiting for transfers between devices  13.1 us (14%)
  matrix products  2.96 us (3%)
  between operations  1.7 us (2%)
    ppermute x8, starting transfers between devices, shift_xy(): return lax.ppermute(value, ('gx', 'gy'), pairs)  19.9 us
    ppermute x4, starting transfers between devices, shift_x(): return lax.ppermute(value, 'gx', [(i, (i + step) % nx) for i in range(nx)])  10.2 us
    ppermute x8, waiting for transfers between devices, shift_xy(): return lax.ppermute(value, ('gx', 'gy'), pairs)  9.78 us
    unnamed x66, local copies, waits for them, and re-layouts  7.72 us
    ppermute x4, starting transfers between devices, shift_y(): return lax.ppermute(value, 'gy', [(j, (j + step) % ny) for j in range(ny)])  5.52 us
    ppermute x4, waiting for transfers between devices, shift_y(): return lax.ppermute(value, 'gy', [(j, (j + step) % ny) for j in range(ny)])  3.26 us
    add_any x3, other arithmetic, collide(): density = jnp.sum(field, axis=0)  3.12 us
    dot_general x3, matrix products, exchange(): jnp.einsum('kx,nx->kn', pick, g.reshape(rows, width), precision=HI, prefe...  2.96 us
  transfers between devices with their start and end apart: 16, of which 4 were waited for; matrix products, arithmetic and copies ran while one was open for 23% of the time, Pallas kernels for 0%

profile of v1, /device:TPU:121, one launch (start us, length us, event | category | flops | bytes accessed | tf_op | source)
XLA Modules:
  0.0 93.3 jit_solution(10504282647982293302)
XLA Ops:
  0.7 0.9 select_reduce_fusion.3
  1.6 0.7 select_reduce_fusion.1
  2.4 1.7 %multiply_reduce_fusion.12 = (f32[4,32,128]{2,1,0:T(8,128)S(1)}, f32[4,32,128]{2,1,0:T(8,128)S(1)}, f32[4,32,128]{2,1,0:T(8,128)S(1)}, f32[4,32,128]{2,1,0:T(8,128)S(1)}) fusion(f32[19,4,32,128]{3,2,1,0:T(8,128)} %param.30, f32[19]{0:T(128)} %constant.47, f32[19]{0:T(128)} %constant.48, f32[19]{0:T(128)} %constant.49), kind=kLoop, calls=%fused_computation.57 | loop fusion | flops 2113536 | bytes 1507556 | tf_op jit(solution)/shard_map/reduce_sum | solution.py:22
  4.3 0.5 copy-done.3
  4.9 1.3 %fusion.2 = f32[19,4,32,128]{3,2,1,0:T(8,128)S(1)} fusion(f32[19,4,32,128]{3,2,1,0:T(8,128)S(1)} %copy-done, f32[4,32,128]{2,1,0:T(8,128)S(1)} %get-tuple-element.50, f32[4,32,128]{2,1,0:T(8,128)S(1)} %get-tuple-element.53, f32[19]{0:T(128)S(1)} %copy-done.11, f32[4,32,128]{2,1,0:T(8,128)S(1)} %get-tuple-element.52, f32[19]{0:T(128)S(1)} %copy-done.8, ...), kind=kLoop, calls=%fused_computation.14 | loop fusion | flops 4980736 | bytes 2818352 | tf_op jit(solution)/shard_map/sub | solution.py:28
  6.2 1.2 %fusion.68 = f32[2,2432]{1,0:T(2,128)S(1)} fusion(f32[2,128]{1,0:T(2,128)S(1)} %copy-done.14, f32[2432,128]{1,0:T(8,128)S(1)} %bitcast.442), kind=kOutput, calls=%fused_computation.332 | convolution fusion | flops 7471104 | bytes 1265664 | tf_op jit(solution)/shard_map/kx,nx->kn/dot_general | solution.py:58
  7.4 0.6 fusion.69
  8.1 0.6 pad_maximum_fusion.23
  8.7 1.2 %collective-permute-start = (f32[2,2432]{1,0:T(2,128)}, f32[2,2432]{1,0:T(2,128)}, u32[]{:S(2)}, u32[]{:S(2)}) collective-permute-start(f32[2,2432]{1,0:T(2,128)} %pad_maximum_fusion.23), channel_id=1, source_target_pairs={{0,32},{32,64},{64,96},{96,128},{128,160},{160,192},{192,224},{224... | collective-permute-start | bytes 58376 | tf_op jit(solution)/shard_map/ppermute | solution.py:76
  9.9 0.6 pad_maximum_fusion.24
  10.5 3.9 %collective-permute-start.1 = (f32[2,2432]{1,0:T(2,128)}, f32[2,2432]{1,0:T(2,128)}, u32[]{:S(2)}, u32[]{:S(2)}) collective-permute-start(f32[2,2432]{1,0:T(2,128)} %pad_maximum_fusion.24), channel_id=1, source_target_pairs={{0,224},{32,0},{64,32},{96,64},{128,96},{160,128},{192,160},{224,1... | collective-permute-start | bytes 58376 | tf_op jit(solution)/shard_map/ppermute | solution.py:76
  14.6 0.7 fusion.63
  15.4 0.7 fusion.64
  16.2 0.6 pad_maximum_fusion.29
  16.8 1.5 %collective-permute-start.5 = (f32[2,19,4]{1,2,0:T(4,128)}, f32[2,19,4]{1,2,0:T(4,128)}, u32[]{:S(2)}, u32[]{:S(2)}) collective-permute-start(f32[2,19,4]{1,2,0:T(4,128)} %pad_maximum_fusion.29), channel_id=1, source_target_pairs={{0,33},{1,34},{2,35},{3,36},{4,37},{5,38},{6,39},{7,40},{8,41},{9,... | collective-permute-start | bytes 1832 | tf_op jit(solution)/shard_map/ppermute | solution.py:83
  18.5 0.6 pad_maximum_fusion.30
  19.1 6.3 %collective-permute-start.7 = (f32[2,19,4]{1,2,0:T(4,128)}, f32[2,19,4]{1,2,0:T(4,128)}, u32[]{:S(2)}, u32[]{:S(2)}) collective-permute-start(f32[2,19,4]{1,2,0:T(4,128)} %pad_maximum_fusion.30), channel_id=1, source_target_pairs={{0,225},{1,226},{2,227},{3,228},{4,229},{5,230},{6,231},{7,232},{8... | collective-permute-start | bytes 1832 | tf_op jit(solution)/shard_map/ppermute | solution.py:83
  25.4 0.7 fusion.61
  26.1 0.3 copy_convert_fusion
  26.4 1.6 %collective-permute-start.6 = (f32[2,19,4,128]{3,2,1,0:T(4,128)S(1)}, f32[2,19,4,128]{3,2,1,0:T(4,128)S(1)}, u32[]{:S(2)}, u32[]{:S(2)}) collective-permute-start(f32[2,19,4,128]{3,2,1,0:T(4,128)S(1)} %pad_maximum_fusion.1), channel_id=1, source_target_pairs={{0,1},{1,2},{2,3},{3,4},{4,5},{5,6},{6,7},{7,8},{8,9},{9,10},{10,1... | collective-permute-start | bytes 233480 | tf_op jit(solution)/shard_map/ppermute | solution.py:79
  28.0 0.9 copy.152
  28.9 0.9 copy.153
  29.9 0.9 copy.156
  30.8 0.8 pad_maximum_fusion
  31.6 1.2 %copy.166 = f32[19,4,32,128]{3,2,1,0:T(8,128)} copy(f32[19,4,32,128]{3,1,0,2:T(4,128)S(1)} %copy_convert_fusion) | data formatting | bytes 2490368
  33.4 0.7 slice_bitcast_fusion.45
  34.1 4.6 %collective-permute-start.4 = (f32[2,19,4]{1,2,0:T(4,128)S(1)}, f32[2,19,4]{1,2,0:T(4,128)S(1)}, u32[]{:S(2)}, u32[]{:S(2)}) collective-permute-start(f32[2,19,4]{1,2,0:T(4,128)S(1)} %pad_maximum_fusion.28), channel_id=1, source_target_pairs={{0,255},{1,224},{2,225},{3,226},{4,227},{5,228},{6,229},{7,230},{8... | collective-permute-start | bytes 1832 | tf_op jit(solution)/shard_map/ppermute | solution.py:83
  38.8 0.7 slice_bitcast_fusion.44
  39.4 2.5 %collective-permute-done.2 = f32[2,19,4]{1,2,0:T(4,128)S(1)} collective-permute-done((f32[2,19,4]{1,2,0:T(4,128)S(1)}, f32[2,19,4]{1,2,0:T(4,128)S(1)}, u32[]{:S(2)}, u32[]{:S(2)}) %collective-permute-start.2) | collective-permute-done | bytes 640 | tf_op jit(solution)/shard_map/ppermute | solution.py:83
  42.9 0.9 slice_reduce_fusion.1
  43.7 0.9 slice_reduce_fusion
  44.6 2.0 %multiply_add_fusion.1 = (f32[2432,130]{1,0:T(8,128)S(1)}, f32[2432,130]{1,0:T(8,128)S(1)}) fusion(f32[2432]{0:T(1024)S(1)} %get-tuple-element.21, f32[2432]{0:T(1024)S(1)} %get-tuple-element.19, f32[130]{0:T(256)} %constant.53, f32[130]{0:T(256)} %constant.51, f32[2432]{0:T(1024)S(1)} %get-tuple-element.22, f32[2432]{0:T(1024)S(1)} %get-tuple-element.20), kind=kLoop, calls=%fused_computation.2 | loop fusion | flops 1896960 | bytes 2569232 | tf_op jit(solution)/shard_map/kn,kx->nx/dot_general | solution.py:98
  46.7 0.8 pad_add_fusion.2
  47.6 0.3 copy-done.1
  48.0 0.7 pad_add_fusion
  49.1 0.2 maximum_bitcast_fusion
  49.4 0.2 maximum_bitcast_fusion.27
  50.0 0.2 fusion.40
  50.9 0.4 copy-done.10
  51.4 0.3 multiply_reduce_fusion.9
  52.2 0.2 fusion.45
  52.6 0.2 copy-done.17
  52.8 1.3 %fusion.20 = (f32[4,32,128]{2,1,0:T(8,128)S(1)}, f32[4,32,128]{2,1,0:T(8,128)S(1)}, f32[4,32,128]{2,1,0:T(8,128)S(1)}, f32[4,32,128]{2,1,0:T(8,128)S(1)}, f32[4,32,128]{2,1,0:T(8,128)S(1)}) fusion(f32[19,4,32,128]{3,2,1,0:T(8,128)S(1)} %constant_dynamic-update-slice_fusion, f32[4,32,128]{2,1,0:T(8,128)S(1)} %bitcast.447, f32[19]{0:T(128)S(1)} %copy-done.17, ...), kind=kLoop, calls=%fused_computation.58 | loop fusion | flops 9879552 | bytes 1900848 | tf_op jit(solution)/shard_map/transpose(jvp())/reduce_sum | solution.py:27
  54.3 0.1 negate_add_fusion.1
  54.4 0.5 add_add_fusion.1
  54.9 1.0 %bitcast_add_fusion = f32[2432,128]{1,0:T(8,128)S(1)} fusion(f32[19,4,32,128]{3,2,1,0:T(8,128)S(1)} %constant_dynamic-update-slice_fusion, f32[2432]{0:T(1024)S(1)} %mul.899, f32[2432]{0:T(1024)S(1)} %mul.895, f32[2432]{0:T(1024)S(1)} %mul.891, f32[4,32,128]{2,1,0:T(8,128)S(1)} %get-tuple-element.33, f32[4,32,128]{2,1,0:T(8,128)S(1)} %get-tuple-element.133, ...), kind=kLoop, calls=%fused_computation.26 | loop fusion | flops 3112960 | bytes 2781696 | tf_op jit(solution)/shard_map/transpose(jvp())/add_any | solution.py:20
  56.0 1.2 %fusion.70 = f32[2,2432]{1,0:T(2,128)S(1)} fusion(f32[2,128]{1,0:T(2,128)S(1)} %copy-done.15, f32[2432,128]{1,0:T(8,128)S(1)} %bitcast_add_fusion), kind=kOutput, calls=%fused_computation.334 | convolution fusion | flops 7471104 | bytes 1265664 | tf_op jit(solution)/shard_map/kx,nx->kn/dot_general | solution.py:58
  57.4 3.9 %collective-permute-start.14 = (f32[1,19,4,128]{3,2,1,0:T(4,128)S(1)}, f32[1,19,4,128]{3,2,1,0:T(4,128)S(1)}, u32[]{:S(2)}, u32[]{:S(2)}) collective-permute-start(f32[1,19,4,128]{3,2,1,0:T(4,128)S(1)} %bitcast.451), channel_id=1, source_target_pairs={{0,1},{1,2},{2,3},{3,4},{4,5},{5,6},{6,7},{7,8},{8,9},{9,10},{10,1... | collective-permute-start | bytes 116744 | tf_op jit(solution)/shard_map/ppermute | solution.py:79
  61.4 5.1 %collective-permute-start.9 = (f32[1,2432]{1,0:T(1,128)S(1)}, f32[1,2432]{1,0:T(1,128)S(1)}, u32[]{:S(2)}, u32[]{:S(2)}) collective-permute-start(f32[1,2432]{1,0:T(1,128)S(1)} %get-tuple-element.157), channel_id=1, source_target_pairs={{0,224},{32,0},{64,32},{96,64},{128,96},{160,128},{192,160},{224,1... | collective-permute-start | bytes 29192 | tf_op jit(solution)/shard_map/ppermute | solution.py:76
  66.6 0.2 collective-permute-start.13
  67.0 3.3 %collective-permute-start.15 = (f32[1,19,4]{1,2,0:T(4,128)S(1)}, f32[1,19,4]{1,2,0:T(4,128)S(1)}, u32[]{:S(2)}, u32[]{:S(2)}) collective-permute-start(f32[1,19,4]{1,2,0:T(4,128)S(1)} %bitcast.467), channel_id=1, source_target_pairs={{0,225},{1,226},{2,227},{3,228},{4,229},{5,230},{6,231},{7,232},{8... | collective-permute-start | bytes 920 | tf_op jit(solution)/shard_map/ppermute | solution.py:83
  70.5 3.0 %collective-permute-done.13 = f32[1,19,4]{1,2,0:T(4,128)S(1)} collective-permute-done((f32[1,19,4]{1,2,0:T(4,128)S(1)}, f32[1,19,4]{1,2,0:T(4,128)S(1)}, u32[]{:S(2)}, u32[]{:S(2)}) %collective-permute-start.13) | collective-permute-done | bytes 336 | tf_op jit(solution)/shard_map/ppermute | solution.py:83
  73.6 3.8 %collective-permute-start.12 = (f32[1,19,4]{1,2,0:T(4,128)S(1)}, f32[1,19,4]{1,2,0:T(4,128)S(1)}, u32[]{:S(2)}, u32[]{:S(2)}) collective-permute-start(f32[1,19,4]{1,2,0:T(4,128)S(1)} %bitcast.462), channel_id=1, source_target_pairs={{0,255},{1,224},{2,225},{3,226},{4,227},{5,228},{6,229},{7,230},{8... | collective-permute-start | bytes 920 | tf_op jit(solution)/shard_map/ppermute | solution.py:83
  77.6 4.4 %collective-permute-done.10 = f32[1,19,4]{1,2,0:T(4,128)S(1)} collective-permute-done((f32[1,19,4]{1,2,0:T(4,128)S(1)}, f32[1,19,4]{1,2,0:T(4,128)S(1)}, u32[]{:S(2)}, u32[]{:S(2)}) %collective-permute-start.10) | collective-permute-done | bytes 336 | tf_op jit(solution)/shard_map/ppermute | solution.py:83
  82.3 0.7 multiply_add_fusion
  83.0 0.8 pad_add_fusion.1
  84.2 3.3 %collective-permute-done.11 = f32[1,19,4,128]{3,2,1,0:T(4,128)S(1)} collective-permute-done((f32[1,19,4,128]{3,2,1,0:T(4,128)S(1)}, f32[1,19,4,128]{3,2,1,0:T(4,128)S(1)}, u32[]{:S(2)}, u32[]{:S(2)}) %collective-permute-start.11) | collective-permute-done | bytes 38944 | tf_op jit(solution)/shard_map/ppermute | solution.py:79
  87.7 0.2 fusion.38
  88.6 0.7 copy-done.6
  89.2 1.3 %fusion.21 = (f32[4,32,128]{2,1,0:T(8,128)S(1)}, f32[4,32,128]{2,1,0:T(8,128)S(1)}, f32[4,32,128]{2,1,0:T(8,128)S(1)}, f32[4,32,128]{2,1,0:T(8,128)S(1)}, f32[4,32,128]{2,1,0:T(8,128)S(1)}) fusion(f32[19,4,32,128]{3,2,1,0:T(8,128)S(1)} %constant_dynamic-update-slice_fusion.38, f32[4,32,128]{2,1,0:T(8,128)S(1)} %get-tuple-element.17, f32[19]{0:T(128)S(1)} %copy-done.17, ...), kind=kLoop, calls=%fused_computation.59 | loop fusion | flops 9879552 | bytes 1900848 | tf_op jit(solution)/shard_map/transpose(jvp())/reduce_sum | solution.py:27
  90.6 0.2 add_reduce_fusion
  90.9 0.2 select_reduce_fusion
  91.1 0.6 select_reduce_fusion.2
  91.8 1.6 %add_add_fusion = f32[19,4,32,128]{3,2,1,0:T(8,128)} fusion(f32[19,4,32,128]{3,2,1,0:T(8,128)S(1)} %constant_dynamic-update-slice_fusion.38, f32[4,32,128]{2,1,0:T(8,128)S(1)} %negate_add_fusion, f32[4,32,128]{2,1,0:T(8,128)S(1)} %get-tuple-element.136, f32[4,32,128]{2,1,0:T(8,128)S(1)} %get-tuple-element.135, f32[4,32,128]{2,1,0:T(8,128)S(1)} %get-tuple-element.134, ...), kind=kLoop, calls=%fused_computation.37 | loop fusion | flops 3112960 | bytes 2752740 | tf_op jit(solution)/shard_map/transpose(jvp())/add_any | solution.py:20
  (177 shorter events, 7.7 us)
Async XLA Ops:
  0.6 4.3 %copy-start.7 = (f32[19]{0:T(128)S(1)}, f32[19]{0:T(128)}, u32[]{:S(2)}) copy-start(f32[19]{0:T(128)} %constant.47) | copy-start | bytes 232
  0.6 4.2 %copy-start.8 = (f32[19]{0:T(128)S(1)}, f32[19]{0:T(128)}, u32[]{:S(2)}) copy-start(f32[19]{0:T(128)} %constant.48) | copy-start | bytes 232
  0.7 4.2 %copy-start.11 = (f32[19]{0:T(128)S(1)}, f32[19]{0:T(128)}, u32[]{:S(2)}) copy-start(f32[19]{0:T(128)} %constant.49) | copy-start | bytes 232
  0.7 4.2 %copy-start.16 = (f32[19]{0:T(128)S(1)}, f32[19]{0:T(128)}, u32[]{:S(2)}) copy-start(f32[19]{0:T(128)} %constant.46) | copy-start | bytes 232
  0.7 4.2 %copy-start = (f32[19,4,32,128]{3,2,1,0:T(8,128)S(1)}, f32[19,4,32,128]{3,2,1,0:T(8,128)}, u32[]{:S(2)}) copy-start(f32[19,4,32,128]{3,2,1,0:T(8,128)} %param.30) | copy-start | bytes 3735556
  4.1 0.6 copy-start.3
  4.3 0.6 copy-start.5
  4.9 1.3 %copy-start.14 = (f32[2,128]{1,0:T(2,128)S(1)}, f32[2,128]{1,0:T(2,128)}, u32[]{:S(2)}) copy-start(f32[2,128]{1,0:T(2,128)} %constant.35.clone) | copy-start | bytes 3076
  6.2 1.2 %copy-start.2 = (bf16[19,4,32,128]{3,2,1,0:T(8,128)(2,1)S(1)}, bf16[19,4,32,128]{3,2,1,0:T(8,128)(2,1)}, u32[]{:S(2)}) copy-start(bf16[19,4,32,128]{3,2,1,0:T(8,128)(2,1)} %param.31) | copy-start | bytes 1867780
  8.7 34.2 %collective-permute-start = (f32[2,2432]{1,0:T(2,128)}, f32[2,2432]{1,0:T(2,128)}, u32[]{:S(2)}, u32[]{:S(2)}) collective-permute-start(f32[2,2432]{1,0:T(2,128)} %pad_maximum_fusion.23), channel_id=1, source_target_pairs={{0,32},{32,64},{64,96},{96,128},{128,160},{160,192},{192,224},{224... | collective-permute-start | bytes 58376 | tf_op jit(solution)/shard_map/ppermute | solution.py:76
  10.5 33.2 %collective-permute-start.1 = (f32[2,2432]{1,0:T(2,128)}, f32[2,2432]{1,0:T(2,128)}, u32[]{:S(2)}, u32[]{:S(2)}) collective-permute-start(f32[2,2432]{1,0:T(2,128)} %pad_maximum_fusion.24), channel_id=1, source_target_pairs={{0,224},{32,0},{64,32},{96,64},{128,96},{160,128},{192,160},{224,1... | collective-permute-start | bytes 58376 | tf_op jit(solution)/shard_map/ppermute | solution.py:76
  16.8 16.6 %collective-permute-start.5 = (f32[2,19,4]{1,2,0:T(4,128)}, f32[2,19,4]{1,2,0:T(4,128)}, u32[]{:S(2)}, u32[]{:S(2)}) collective-permute-start(f32[2,19,4]{1,2,0:T(4,128)} %pad_maximum_fusion.29), channel_id=1, source_target_pairs={{0,33},{1,34},{2,35},{3,36},{4,37},{5,38},{6,39},{7,40},{8,41},{9,... | collective-permute-start | bytes 1832 | tf_op jit(solution)/shard_map/ppermute | solution.py:83
  19.1 15.1 %collective-permute-start.7 = (f32[2,19,4]{1,2,0:T(4,128)}, f32[2,19,4]{1,2,0:T(4,128)}, u32[]{:S(2)}, u32[]{:S(2)}) collective-permute-start(f32[2,19,4]{1,2,0:T(4,128)} %pad_maximum_fusion.30), channel_id=1, source_target_pairs={{0,225},{1,226},{2,227},{3,228},{4,229},{5,230},{6,231},{7,232},{8... | collective-permute-start | bytes 1832 | tf_op jit(solution)/shard_map/ppermute | solution.py:83
  26.4 22.4 %collective-permute-start.6 = (f32[2,19,4,128]{3,2,1,0:T(4,128)S(1)}, f32[2,19,4,128]{3,2,1,0:T(4,128)S(1)}, u32[]{:S(2)}, u32[]{:S(2)}) collective-permute-start(f32[2,19,4,128]{3,2,1,0:T(4,128)S(1)} %pad_maximum_fusion.1), channel_id=1, source_target_pairs={{0,1},{1,2},{2,3},{3,4},{4,5},{5,6},{6,7},{7,8},{8,9},{9,10},{10,1... | collective-permute-start | bytes 233480 | tf_op jit(solution)/shard_map/ppermute | solution.py:79
  31.6 1.2 %copy-start.12 = (f32[19]{0:T(128)S(1)}, f32[19]{0:T(128)}, u32[]{:S(2)}) copy-start(f32[19]{0:T(128)} %constant.49) | copy-start | bytes 232
  31.6 1.4 %copy-start.9 = (f32[19]{0:T(128)S(1)}, f32[19]{0:T(128)}, u32[]{:S(2)}) copy-start(f32[19]{0:T(128)} %constant.48) | copy-start | bytes 232
  33.4 8.5 %collective-permute-start.2 = (f32[2,19,4]{1,2,0:T(4,128)S(1)}, f32[2,19,4]{1,2,0:T(4,128)S(1)}, u32[]{:S(2)}, u32[]{:S(2)}) collective-permute-start(f32[2,19,4]{1,2,0:T(4,128)S(1)} %pad_maximum_fusion.27), channel_id=1, source_target_pairs={{0,63},{1,32},{2,33},{3,34},{4,35},{5,36},{6,37},{7,38},{8,39},{9,... | collective-permute-start | bytes 1832 | tf_op jit(solution)/shard_map/ppermute | solution.py:83
  34.1 7.8 %collective-permute-start.4 = (f32[2,19,4]{1,2,0:T(4,128)S(1)}, f32[2,19,4]{1,2,0:T(4,128)S(1)}, u32[]{:S(2)}, u32[]{:S(2)}) collective-permute-start(f32[2,19,4]{1,2,0:T(4,128)S(1)} %pad_maximum_fusion.28), channel_id=1, source_target_pairs={{0,255},{1,224},{2,225},{3,226},{4,227},{5,228},{6,229},{7,230},{8... | collective-permute-start | bytes 1832 | tf_op jit(solution)/shard_map/ppermute | solution.py:83
  41.9 7.2 %collective-permute-start.3 = (f32[2,19,4,128]{3,2,1,0:T(4,128)S(1)}, f32[2,19,4,128]{3,2,1,0:T(4,128)S(1)}, u32[]{:S(2)}, u32[]{:S(2)}) collective-permute-start(f32[2,19,4,128]{3,2,1,0:T(4,128)S(1)} %pad_maximum_fusion), channel_id=1, source_target_pairs={{0,31},{1,0},{2,1},{3,2},{4,3},{5,4},{6,5},{7,6},{8,7},{9,8},{10,9... | collective-permute-start | bytes 233480 | tf_op jit(solution)/shard_map/ppermute | solution.py:79
  46.7 1.3 %copy-start.1 = (f32[19,4,32,128]{3,2,1,0:T(8,128)S(1)}, f32[19,4,32,128]{3,2,1,0:T(8,128)}, u32[]{:S(2)}) copy-start(f32[19,4,32,128]{3,2,1,0:T(8,128)} %copy.166) | copy-start | bytes 3735556
  50.7 0.7 copy-start.10
  50.7 0.7 copy-start.13
  52.1 0.7 copy-start.17
  54.9 1.1 %copy-start.15 = (f32[2,128]{1,0:T(2,128)S(1)}, f32[2,128]{1,0:T(2,128)}, u32[]{:S(2)}) copy-start(f32[2,128]{1,0:T(2,128)} %constant.35.clone) | copy-start | bytes 3076
  56.0 26.3 %copy-start.18 = (f32[130]{0:T(256)S(1)}, f32[130]{0:T(256)}, u32[]{:S(2)}) copy-start(f32[130]{0:T(256)} %constant.51) | copy-start | bytes 1564
  56.0 26.3 %copy-start.19 = (f32[130]{0:T(256)S(1)}, f32[130]{0:T(256)}, u32[]{:S(2)}) copy-start(f32[130]{0:T(256)} %constant.53) | copy-start | bytes 1564
  57.4 26.5 %collective-permute-start.14 = (f32[1,19,4,128]{3,2,1,0:T(4,128)S(1)}, f32[1,19,4,128]{3,2,1,0:T(4,128)S(1)}, u32[]{:S(2)}, u32[]{:S(2)}) collective-permute-start(f32[1,19,4,128]{3,2,1,0:T(4,128)S(1)} %bitcast.451), channel_id=1, source_target_pairs={{0,1},{1,2},{2,3},{3,4},{4,5},{5,6},{6,7},{7,8},{8,9},{9,10},{10,1... | collective-permute-start | bytes 116744 | tf_op jit(solution)/shard_map/ppermute | solution.py:79
  61.4 20.8 %collective-permute-start.8 = (f32[1,2432]{1,0:T(1,128)S(1)}, f32[1,2432]{1,0:T(1,128)S(1)}, u32[]{:S(2)}, u32[]{:S(2)}) collective-permute-start(f32[1,2432]{1,0:T(1,128)S(1)} %get-tuple-element.156), channel_id=1, source_target_pairs={{0,32},{32,64},{64,96},{96,128},{128,160},{160,192},{192,224},{224... | collective-permute-start | bytes 29192 | tf_op jit(solution)/shard_map/ppermute | solution.py:76
  61.4 20.9 %collective-permute-start.9 = (f32[1,2432]{1,0:T(1,128)S(1)}, f32[1,2432]{1,0:T(1,128)S(1)}, u32[]{:S(2)}, u32[]{:S(2)}) collective-permute-start(f32[1,2432]{1,0:T(1,128)S(1)} %get-tuple-element.157), channel_id=1, source_target_pairs={{0,224},{32,0},{64,32},{96,64},{128,96},{160,128},{192,160},{224,1... | collective-permute-start | bytes 29192 | tf_op jit(solution)/shard_map/ppermute | solution.py:76
  66.6 6.9 %collective-permute-start.13 = (f32[1,19,4]{1,2,0:T(4,128)S(1)}, f32[1,19,4]{1,2,0:T(4,128)S(1)}, u32[]{:S(2)}, u32[]{:S(2)}) collective-permute-start(f32[1,19,4]{1,2,0:T(4,128)S(1)} %bitcast.469), channel_id=1, source_target_pairs={{0,33},{1,34},{2,35},{3,36},{4,37},{5,38},{6,39},{7,40},{8,41},{9,... | collective-permute-start | bytes 920 | tf_op jit(solution)/shard_map/ppermute | solution.py:83
  67.0 6.6 %collective-permute-start.15 = (f32[1,19,4]{1,2,0:T(4,128)S(1)}, f32[1,19,4]{1,2,0:T(4,128)S(1)}, u32[]{:S(2)}, u32[]{:S(2)}) collective-permute-start(f32[1,19,4]{1,2,0:T(4,128)S(1)} %bitcast.467), channel_id=1, source_target_pairs={{0,225},{1,226},{2,227},{3,228},{4,229},{5,230},{6,231},{7,232},{8... | collective-permute-start | bytes 920 | tf_op jit(solution)/shard_map/ppermute | solution.py:83
  73.5 8.4 %collective-permute-start.10 = (f32[1,19,4]{1,2,0:T(4,128)S(1)}, f32[1,19,4]{1,2,0:T(4,128)S(1)}, u32[]{:S(2)}, u32[]{:S(2)}) collective-permute-start(f32[1,19,4]{1,2,0:T(4,128)S(1)} %bitcast.464), channel_id=1, source_target_pairs={{0,63},{1,32},{2,33},{3,34},{4,35},{5,36},{6,37},{7,38},{8,39},{9,... | collective-permute-start | bytes 920 | tf_op jit(solution)/shard_map/ppermute | solution.py:83
  73.6 8.4 %collective-permute-start.12 = (f32[1,19,4]{1,2,0:T(4,128)S(1)}, f32[1,19,4]{1,2,0:T(4,128)S(1)}, u32[]{:S(2)}, u32[]{:S(2)}) collective-permute-start(f32[1,19,4]{1,2,0:T(4,128)S(1)} %bitcast.462), channel_id=1, source_target_pairs={{0,255},{1,224},{2,225},{3,226},{4,227},{5,228},{6,229},{7,230},{8... | collective-permute-start | bytes 920 | tf_op jit(solution)/shard_map/ppermute | solution.py:83
  81.9 5.5 %collective-permute-start.11 = (f32[1,19,4,128]{3,2,1,0:T(4,128)S(1)}, f32[1,19,4,128]{3,2,1,0:T(4,128)S(1)}, u32[]{:S(2)}, u32[]{:S(2)}) collective-permute-start(f32[1,19,4,128]{3,2,1,0:T(4,128)S(1)} %bitcast.450), channel_id=1, source_target_pairs={{0,31},{1,0},{2,1},{3,2},{4,3},{5,4},{6,5},{7,6},{8,7},{9,8},{10,9... | collective-permute-start | bytes 116744 | tf_op jit(solution)/shard_map/ppermute | solution.py:79
  88.4 0.8 copy-start.6
  88.5 2.1 %copy-start.4 = (f32[4,32,128]{2,1,0:T(8,128)S(1)}, f32[4,32,128]{2,1,0:T(8,128)}, u32[]{:S(2)}) copy-start(f32[4,32,128]{2,1,0:T(8,128)} %copy-done.3) | copy-start | bytes 196612
  89.2 1.6 %copy-start.20 = (s32[1,1,64]{2,1,0:T(1,128)S(1)}, s32[1,1,64]{2,1,0:T(1,128)}, u32[]{:S(2)}) copy-start(s32[1,1,64]{2,1,0:T(1,128)} %param.33) | copy-start | bytes 772
  89.2 1.8 %copy-start.21 = (s32[1,1,64]{2,1,0:T(1,128)S(1)}, s32[1,1,64]{2,1,0:T(1,128)}, u32[]{:S(2)}) copy-start(s32[1,1,64]{2,1,0:T(1,128)} %param.34) | copy-start | bytes 772

commit v2 on v0

v2 whole, which is shorter than its diff:
```python
import jax
import jax.numpy as jnp
import numpy as np
from jax import lax
from jax.experimental import pallas as pl
from jax.experimental.pallas import tpu as pltpu
from jax.sharding import PartitionSpec as P

DIR_X = np.array([0, 1, -1, 0, 0, 0, 0, 1, -1, 1, -1, 1, -1, 1, -1, 0, 0, 0, 0])
DIR_Y = np.array([0, 0, 0, 1, -1, 0, 0, 1, 1, -1, -1, 0, 0, 0, 0, 1, -1, 1, -1])
DIR_Z = np.array([0, 0, 0, 0, 0, 1, -1, 0, 0, 0, 0, 1, 1, -1, -1, 1, 1, -1, -1])
WEIGHTS = np.array([1.0 / 3.0] + [1.0 / 18.0] * 6 + [1.0 / 36.0] * 12)
RELAX_RATE = 0.8

ROWS = 48
LANES = 256
TOP = 8


def collide(fields, solid):
    density = fields[0]
    for value in fields[1:]:
        density = density + value
    inverse = (1.0 - solid) / density
    moments = []
    for direction in (DIR_X, DIR_Y, DIR_Z):
        total = None
        for q in range(19):
            if direction[q] == 0:
                continue
            term = fields[q] if direction[q] > 0 else -fields[q]
            total = term if total is None else total + term
        moments.append(total * inverse)
    vel_x, vel_y, vel_z = moments
    square = vel_x * vel_x + vel_y * vel_y + vel_z * vel_z
    out = []
    for q in range(19):
        along = None
        for sign, vel in ((DIR_X[q], vel_x), (DIR_Y[q], vel_y), (DIR_Z[q], vel_z)):
            if sign == 0:
                continue
            term = vel if sign > 0 else -vel
            along = term if along is None else along + term
        if along is None:
            shape = 1.0 - 1.5 * square
        else:
            shape = 1.0 + 3.0 * along + 4.5 * along * along - 1.5 * square
        balance = float(WEIGHTS[q]) * density * shape
        out.append(fields[q] - RELAX_RATE * (fields[q] - balance))
    return out


def plane_list(q_count, layers):
    planes = [(0, q, z) for q in range(q_count) for z in range(layers)]
    planes += [(1, q, z) for q in range(q_count) for z in range(layers)]
    planes += [(2, 0, z) for z in range(layers)]
    return planes


def pack_kernel(f_ref, cot_ref, solid_ref, up_ref, dn_ref, to_right_ref, to_left_ref, tile_ref):
    q_count, layers, height, width = f_ref.shape
    lane = lax.broadcasted_iota(jnp.int32, (ROWS, width), 1)
    to_right_ref[...] = jnp.zeros(to_right_ref.shape, jnp.float32)
    to_left_ref[...] = jnp.zeros(to_left_ref.shape, jnp.float32)
    tile_ref[...] = jnp.zeros(tile_ref.shape, jnp.float32)
    for index, (field, q, z) in enumerate(plane_list(q_count, layers)):
        if field == 0:
            own = f_ref[q, z]
        elif field == 1:
            own = cot_ref[q, z].astype(jnp.float32)
        else:
            own = solid_ref[z]
        row_index = field * q_count + q
        tile_ref[TOP : TOP + height, :] = own
        tile_ref[TOP - 2 : TOP, :] = up_ref[row_index, z]
        tile_ref[TOP + height : TOP + height + 2, :] = dn_ref[row_index, z]
        tile = tile_ref[...]
        group, slot = divmod(index, width // 2)
        mine = (lane == 2 * slot) | (lane == 2 * slot + 1)
        moved = pltpu.roll(tile, (2 * slot - (width - 2)) % width, 1)
        to_right_ref[group] = jnp.where(mine, moved, to_right_ref[group])
        moved = pltpu.roll(tile, (2 * slot) % width, 1)
        to_left_ref[group] = jnp.where(mine, moved, to_left_ref[group])


def compute_kernel(f_ref, cot_ref, solid_ref, up_ref, dn_ref, from_left_ref, from_right_ref,
                   grad_ref, sbar_ref, ef, ec, es, cf, bo, sb2):
    q_count, layers, height, width = f_ref.shape
    lane = lax.broadcasted_iota(jnp.int32, (ROWS, width), 1)
    low_lanes = lane < 2
    high_lanes = lane >= width - 2
    tail = ROWS - (TOP + height + 2)

    def place(target, index, own, up_rows, dn_rows):
        group, slot = divmod(index, width // 2)
        from_r = pltpu.roll(from_right_ref[group], (-2 * slot) % width, 1)
        from_l = pltpu.roll(from_left_ref[group], (width - 2 - 2 * slot) % width, 1)
        target[:, width:LANES] = jnp.where(low_lanes, from_r, jnp.where(high_lanes, from_l, 0.0))
        target[0 : TOP - 2, 0:width] = jnp.zeros((TOP - 2, width), jnp.float32)
        target[TOP + height + 2 : ROWS, 0:width] = jnp.zeros((tail, width), jnp.float32)
        target[TOP - 2 : TOP, 0:width] = up_rows
        target[TOP : TOP + height, 0:width] = own
        target[TOP + height : TOP + height + 2, 0:width] = dn_rows

    for index, (field, q, z) in enumerate(plane_list(q_count, layers)):
        row_index = field * q_count + q
        if field == 0:
            place(ef.at[q, z], index, f_ref[q, z], up_ref[row_index, z], dn_ref[row_index, z])
        elif field == 1:
            place(ec.at[q, z], index, cot_ref[q, z].astype(jnp.float32), up_ref[row_index, z],
                  dn_ref[row_index, z])
        else:
            place(es.at[z], index, solid_ref[z], up_ref[row_index, z], dn_ref[row_index, z])

    def phase_one(z, carry):
        for k in range(ROWS // 8):
            rows = pl.ds(8 * k, 8)
            out = collide([ef[q, z, rows, :] for q in range(q_count)], es[z, rows, :])
            for q in range(q_count):
                cf[q, z, rows, :] = out[q]
        return carry

    lax.fori_loop(0, layers, phase_one, 0)

    def phase_two(z, carry):
        for k in range((ROWS - 8) // 8):
            start = TOP - 1 + 8 * k
            moved = []
            back = []
            for q in range(q_count):
                ex, ey, ez = int(DIR_X[q]), int(DIR_Y[q]), int(DIR_Z[q])
                src = cf[q, (z - ez + layers) % layers, pl.ds(start - ey, 8), :]
                moved.append(pltpu.roll(src, ex % LANES, 1) if ex else src)
                src = ec[q, (z + ez) % layers, pl.ds(start + ey, 8), :]
                back.append(pltpu.roll(src, (-ex) % LANES, 1) if ex else src)
            ignored, undo = jax.vjp(collide, moved, es[z, pl.ds(start, 8), :])
            grad_field, grad_solid = undo(back)
            for q in range(q_count):
                bo[q, z, pl.ds(8 * k, 8), :] = grad_field[q]
            sb2[z, pl.ds(8 * k, 8), :] = grad_solid
        return carry

    lax.fori_loop(0, layers, phase_two, 0)

    def phase_three(z, carry):
        for k in range(height // 8):
            rows = pl.ds(8 * k, 8)
            pulled = []
            for q in range(q_count):
                ex, ey, ez = int(DIR_X[q]), int(DIR_Y[q]), int(DIR_Z[q])
                src = bo[q, (z + ez) % layers, pl.ds(1 + ey + 8 * k, 8), :]
                if ex:
                    src = pltpu.roll(src, (-ex) % LANES, 1)
                pulled.append(src[:, 0:width])
            field = [f_ref[q, z, rows, :] for q in range(q_count)]
            ignored, undo = jax.vjp(collide, field, solid_ref[z, rows, :])
            grad_field, grad_solid = undo(pulled)
            for q in range(q_count):
                grad_ref[q, z, rows, :] = grad_field[q]
            sbar_ref[z, rows, :] = grad_solid + sb2[z, pl.ds(1 + 8 * k, 8), 0:width]
        return carry

    lax.fori_loop(0, layers, phase_three, 0)


def vmem_specs(count):
    return [pl.BlockSpec(memory_space=pltpu.VMEM) for _ in range(count)]


def on_device(f_start, cotangent, porosity, brick_ids, brick_slot):
    q_count, layers_dev, rows_dev, cols_dev = f_start.shape
    nx = lax.axis_size("gx")
    ny = lax.axis_size("gy")
    tile_count = cols_dev // 128
    brick_count = layers_dev * rows_dev * tile_count
    listed = brick_ids.reshape(-1)
    slots_of = brick_slot.reshape(-1)
    slot_table = porosity.reshape(-1)
    brick_hit = (listed[:, None] == jnp.arange(brick_count, dtype=jnp.int32)[None, :]).astype(
        jnp.float32
    )
    slot_hit = (
        slots_of[:, None] == jnp.arange(slot_table.shape[0], dtype=jnp.int32)[None, :]
    ).astype(jnp.float32)
    brick_value = jnp.sum(slot_hit * slot_table[None, :], axis=1)
    tile_value = jnp.sum(brick_hit * brick_value[:, None], axis=0)
    solid = jnp.broadcast_to(
        tile_value.reshape(layers_dev, rows_dev, tile_count, 1),
        (layers_dev, rows_dev, tile_count, 128),
    ).reshape(layers_dev, rows_dev, cols_dev)

    def shift(value, axis, size, step):
        return lax.ppermute(value, axis, [(i, (i + step) % size) for i in range(size)])

    cot32 = cotangent.astype(jnp.float32)
    first_rows = jnp.concatenate([f_start[:, :, 0:2], cot32[:, :, 0:2], solid[None, :, 0:2]], axis=0)
    last_rows = jnp.concatenate(
        [f_start[:, :, rows_dev - 2 :], cot32[:, :, rows_dev - 2 :], solid[None, :, rows_dev - 2 :]],
        axis=0,
    )
    up_rows = shift(last_rows, "gy", ny, 1)
    dn_rows = shift(first_rows, "gy", ny, -1)
    plane_count = (2 * q_count + 1) * layers_dev
    groups = -(-plane_count // (cols_dev // 2))
    buffer = jax.ShapeDtypeStruct((groups, ROWS, cols_dev), jnp.float32)
    to_right, to_left = pl.pallas_call(
        pack_kernel,
        out_shape=(buffer, buffer),
        in_specs=vmem_specs(5),
        out_specs=tuple(vmem_specs(2)),
        scratch_shapes=[pltpu.VMEM((ROWS, cols_dev), jnp.float32)],
    )(f_start, cotangent, solid, up_rows, dn_rows)
    from_left = shift(to_right, "gx", nx, 1)
    from_right = shift(to_left, "gx", nx, -1)
    big = pltpu.VMEM((q_count, layers_dev, ROWS, LANES), jnp.float32)
    start_grad, solid_bar = pl.pallas_call(
        compute_kernel,
        out_shape=(
            jax.ShapeDtypeStruct(f_start.shape, jnp.float32),
            jax.ShapeDtypeStruct(solid.shape, jnp.float32),
        ),
        in_specs=vmem_specs(7),
        out_specs=tuple(vmem_specs(2)),
        scratch_shapes=[
            big,
            big,
            pltpu.VMEM((layers_dev, ROWS, LANES), jnp.float32),
            big,
            pltpu.VMEM((q_count, layers_dev, ROWS - 8, LANES), jnp.float32),
            pltpu.VMEM((layers_dev, ROWS - 8, LANES), jnp.float32),
        ],
        compiler_params=pltpu.CompilerParams(vmem_limit_bytes=48 * 1024 * 1024),
    )(f_start, cotangent, solid, up_rows, dn_rows, from_left, from_right)
    tile_sums = jnp.sum(solid_bar.reshape(brick_count, 128), axis=1)
    brick_sum = jnp.sum(brick_hit * tile_sums[None, :], axis=1)
    slot_grad = jnp.sum(slot_hit * brick_sum[:, None], axis=0)
    return (start_grad, slot_grad.reshape(porosity.shape))


def solution(mesh):
    return jax.shard_map(
        on_device,
        mesh=mesh,
        in_specs=(
            P(None, None, "gy", "gx"),
            P(None, None, "gy", "gx"),
            P("gx", "gy", None),
            P("gx", "gy", None),
            P("gx", "gy", None),
        ),
        out_specs=(P(None, None, "gy", "gx"), P("gx", "gy", None)),
        check_vma=False,
    )
```

time: 90.5 us -> 47.7 us (0.53)
  the two profiles are of different devices: /device:TPU:0 before, /device:TPU:6 now
where the time goes in v2:
time: 47.7 us; the launch traced here: 47.5 us
  Pallas kernels  19.8 us (42%)
  waiting for transfers between devices  11 us (23%)
  starting transfers between devices  9.28 us (19%)
  local copies, waits for them, and re-layouts  4.23 us (9%)
  other arithmetic  2.55 us (5%)
  between operations  0.69 us (1%)
    pallas_call x1, Pallas kernels, on_device(): pl.pallas_call(compute_kernel, out_shape=(jax.ShapeDtypeStruct(f_start.sh...  15.4 us
    ppermute x4, waiting for transfers between devices, shift(): lax.ppermute(value, axis, [(i, (i + step) % size) for i in range(size)])  11 us
    ppermute x4, starting transfers between devices, shift(): lax.ppermute(value, axis, [(i, (i + step) % size) for i in range(size)])  9.28 us
    pallas_call x1, Pallas kernels, on_device(): pl.pallas_call(pack_kernel, out_shape=(buffer, buffer), in_specs=vmem_spe...  4.39 us
    unnamed x18, local copies, waits for them, and re-layouts  1.85 us
    slice x1, local copies, waits for them, and re-layouts, on_device(): f_start[:, :, 0:2]  1.28 us
  transfers between devices with their start and end apart: 4, of which 4 were waited for; matrix products, arithmetic and copies ran while one was open for 0% of the time, Pallas kernels for 0%

profile of v2, /device:TPU:6, one launch (start us, length us, event | category | flops | bytes accessed | tf_op | source)
XLA Modules:
  0.0 47.5 jit_solution(12537144038845160088)
XLA Ops:
  0.6 0.8 %select_reduce_fusion.3 = f32[64]{0:T(128)S(1)} fusion(f32[16]{0:T(128)} %bitcast.4, s32[64]{0:T(128)} %bitcast.7), kind=kLoop, calls=%fused_computation.6 | loop fusion | flops 3008 | bytes 576 | tf_op jit(solution)/shard_map/reduce_sum | solution.py:185
  1.4 0.7 %select_reduce_fusion.1 = f32[128]{0:T(128)S(1)} fusion(f32[64]{0:T(128)S(1)} %select_reduce_fusion.3, s32[64]{0:T(128)} %bitcast.5), kind=kLoop, calls=%fused_computation.3 | loop fusion | flops 24448 | bytes 1024 | tf_op jit(solution)/shard_map/reduce_sum | solution.py:186
  2.1 0.1 broadcast_in_dim.6
  2.2 0.1 fusion.2
  2.3 1.3 %fusion = (f32[19,4,2,128]{3,2,1,0:T(2,128)S(1)}, f32[19,4,2,128]{3,2,1,0:T(2,128)S(1)}, f32[19,4,2,128]{3,2,1,0:T(2,128)S(1)}, f32[19,4,2,128]{3,2,1,0:T(2,128)S(1)}) fusion(f32[19,4,32,128]{3,2,1,0:T(8,128)} %f_ref.3, bf16[19,4,32,128]{3,2,1,0:T(8,128)(2,1)} %cot_ref.3), kind=kLoop, calls=%fused_computation.8 | loop fusion | bytes 622592 | tf_op jit(solution)/shard_map/slice | solution.py:196
  3.6 0.1 broadcast_in_dim.7
  3.7 0.1 pad_maximum_fusion
  3.7 0.1 collective-permute-start
  3.8 0.1 broadcast_in_dim.8
  3.9 0.0 copy-start
  3.9 0.0 copy-start.1
  3.9 0.1 pad_maximum_fusion.1
  4.0 6.4 %collective-permute-start.1 = (f32[39,4,2,128]{3,2,1,0:T(2,128)S(1)}, f32[39,4,2,128]{3,2,1,0:T(2,128)S(1)}, u32[]{:S(2)}, u32[]{:S(2)}) collective-permute-start(f32[39,4,2,128]{3,2,1,0:T(2,128)S(1)} %pad_maximum_fusion.1), channel_id=1, source_target_pairs={{0,31},{1,0},{2,1},{3,2},{4,3},{5,4},{6,5},{7,6},{8,7},{9,8},{10,9... | collective-permute-start | bytes 479240 | tf_op jit(solution)/shard_map/ppermute | solution.py:193
  10.4 2.7 %collective-permute-done.up_ref = f32[39,4,2,128]{3,2,1,0:T(2,128)S(1)} collective-permute-done((f32[39,4,2,128]{3,2,1,0:T(2,128)S(1)}, f32[39,4,2,128]{3,2,1,0:T(2,128)S(1)}, u32[]{:S(2)}, u32[]{:S(2)}) %collective-permute-start) | collective-permute-done | bytes 159776 | tf_op jit(solution)/shard_map/ppermute | solution.py:193
  13.1 0.0 copy-start.2
  13.1 0.1 collective-permute-done.1.dn_ref
  13.2 0.0 copy-start.4
  13.2 0.7 %reshape.23.solid_ref = f32[4,32,128]{2,1,0:T(8,128)} broadcast(f32[4,32]{1,0:T(4,128)S(1)} %broadcast_in_dim.6), dimensions={0,1} | broadcast | bytes 66048 | tf_op jit(solution)/shard_map/reshape | solution.py:190
  13.9 0.0 copy-done.2
  13.9 0.0 copy-done.4
  13.9 0.0 copy-start.6
  13.9 4.4 %shard_map.68 = (f32[3,48,128]{2,1,0:T(8,128)}, f32[3,48,128]{2,1,0:T(8,128)}) custom-call(f32[19,4,32,128]{3,2,1,0:T(8,128)} %f_ref.3, bf16[19,4,32,128]{3,2,1,0:T(8,128)(2,1)} %cot_ref.3, f32[4,32,128]{2,1,0:T(8,128)} %reshape.23.solid_ref, f32[39,4,2,128]{3,2,1,0:T(2,128)} %copy-done.2, f32[39,4,2,128]{3,2,1,0:T(2,128)} %copy-done.4), custom_call_target="tpu_custom_call" | custom-call | tf_op jit(solution)/shard_map/pallas_call | solution.py:206
  18.3 0.0 copy-start.7
  18.3 0.0 copy-start.8
  18.3 2.8 %collective-permute-start.2 = (f32[3,48,128]{2,1,0:T(8,128)}, f32[3,48,128]{2,1,0:T(8,128)S(1)}, u32[]{:S(2)}, u32[]{:S(2)}) collective-permute-start(f32[3,48,128]{2,1,0:T(8,128)} %get-tuple-element.6), channel_id=1, source_target_pairs={{0,32},{32,64},{64,96},{96,128},{128,160},{160,192},{192,224},{224... | collective-permute-start | bytes 221192 | tf_op jit(solution)/shard_map/ppermute | solution.py:193
  21.1 0.0 collective-permute-start.3
  21.1 2.3 %collective-permute-done.2.from_left_ref = f32[3,48,128]{2,1,0:T(8,128)S(1)} collective-permute-done((f32[3,48,128]{2,1,0:T(8,128)}, f32[3,48,128]{2,1,0:T(8,128)S(1)}, u32[]{:S(2)}, u32[]{:S(2)}) %collective-permute-start.2) | collective-permute-done | bytes 73760 | tf_op jit(solution)/shard_map/ppermute | solution.py:193
  23.4 5.9 %collective-permute-done.3.from_right_ref = f32[3,48,128]{2,1,0:T(8,128)S(1)} collective-permute-done((f32[3,48,128]{2,1,0:T(8,128)}, f32[3,48,128]{2,1,0:T(8,128)S(1)}, u32[]{:S(2)}, u32[]{:S(2)}) %collective-permute-start.3) | collective-permute-done | bytes 73760 | tf_op jit(solution)/shard_map/ppermute | solution.py:193
  29.3 0.0 copy-done
  29.3 0.0 copy-done.1
  29.3 0.0 copy-done.6
  29.3 0.0 copy-start.3
  29.3 0.9 %copy-done.3 = f32[39,4,2,128]{3,2,1,0:T(2,128)S(1)} copy-done((f32[39,4,2,128]{3,2,1,0:T(2,128)S(1)}, f32[39,4,2,128]{3,2,1,0:T(2,128)}, u32[]{:S(2)}) %copy-start.3) | copy-done | bytes 159768
  30.2 0.0 copy-start.5
  30.2 0.9 %copy-done.5 = f32[39,4,2,128]{3,2,1,0:T(2,128)S(1)} copy-done((f32[39,4,2,128]{3,2,1,0:T(2,128)S(1)}, f32[39,4,2,128]{3,2,1,0:T(2,128)}, u32[]{:S(2)}) %copy-start.5) | copy-done | bytes 159768
  31.1 15.4 %shard_map.69 = (f32[19,4,32,128]{3,2,1,0:T(8,128)}, f32[4,32,128]{2,1,0:T(8,128)S(1)}) custom-call(f32[19,4,32,128]{3,2,1,0:T(8,128)S(1)} %copy-done, bf16[19,4,32,128]{3,2,1,0:T(8,128)(2,1)S(1)} %copy-done.1, f32[4,32,128]{2,1,0:T(8,128)S(1)} %copy-done.6, f32[39,4,2,128]{3,2,1,0:T(2,128)S(1)} %copy-done.3, f32[39,4,2,128]{3,2,1,0:T(2,128)S(1)} %copy-done.5, ...), custom_call_target="tpu_custom_call" | custom-call | tf_op jit(solution)/shard_map/pallas_call | solution.py:216
  46.5 0.1 reduce_sum.47
  46.6 0.1 mul.41
  46.7 0.0 copy-done.7
  46.7 0.2 select_reduce_fusion
  46.9 0.0 copy-done.8
  46.9 0.6 %select_reduce_fusion.2 = f32[16]{0:T(128)} fusion(f32[64]{0:T(128)S(1)} %select_reduce_fusion, s32[64]{0:T(128)S(1)} %bitcast.8), kind=kLoop, calls=%fused_computation.5 | loop fusion | flops 3056 | bytes 576 | tf_op jit(solution)/shard_map/reduce_sum | solution.py:236
Async XLA Ops:
  3.7 9.3 %collective-permute-start = (f32[39,4,2,128]{3,2,1,0:T(2,128)S(1)}, f32[39,4,2,128]{3,2,1,0:T(2,128)S(1)}, u32[]{:S(2)}, u32[]{:S(2)}) collective-permute-start(f32[39,4,2,128]{3,2,1,0:T(2,128)S(1)} %pad_maximum_fusion), channel_id=1, source_target_pairs={{0,1},{1,2},{2,3},{3,4},{4,5},{5,6},{6,7},{7,8},{8,9},{9,10},{10,1... | collective-permute-start | bytes 479240 | tf_op jit(solution)/shard_map/ppermute | solution.py:193
  3.9 25.4 %copy-start = (f32[19,4,32,128]{3,2,1,0:T(8,128)S(1)}, f32[19,4,32,128]{3,2,1,0:T(8,128)}, u32[]{:S(2)}) copy-start(f32[19,4,32,128]{3,2,1,0:T(8,128)} %f_ref.3) | copy-start | bytes 3735556
  3.9 25.4 %copy-start.1 = (bf16[19,4,32,128]{3,2,1,0:T(8,128)(2,1)S(1)}, bf16[19,4,32,128]{3,2,1,0:T(8,128)(2,1)}, u32[]{:S(2)}) copy-start(bf16[19,4,32,128]{3,2,1,0:T(8,128)(2,1)} %cot_ref.3) | copy-start | bytes 1867780
  4.0 9.2 %collective-permute-start.1 = (f32[39,4,2,128]{3,2,1,0:T(2,128)S(1)}, f32[39,4,2,128]{3,2,1,0:T(2,128)S(1)}, u32[]{:S(2)}, u32[]{:S(2)}) collective-permute-start(f32[39,4,2,128]{3,2,1,0:T(2,128)S(1)} %pad_maximum_fusion.1), channel_id=1, source_target_pairs={{0,31},{1,0},{2,1},{3,2},{4,3},{5,4},{6,5},{7,6},{8,7},{9,8},{10,9... | collective-permute-start | bytes 479240 | tf_op jit(solution)/shard_map/ppermute | solution.py:193
  13.1 0.8 %copy-start.2 = (f32[39,4,2,128]{3,2,1,0:T(2,128)}, f32[39,4,2,128]{3,2,1,0:T(2,128)S(1)}, u32[]{:S(2)}) copy-start(f32[39,4,2,128]{3,2,1,0:T(2,128)S(1)} %collective-permute-done.up_ref) | copy-start | bytes 479236
  13.2 0.7 %copy-start.4 = (f32[39,4,2,128]{3,2,1,0:T(2,128)}, f32[39,4,2,128]{3,2,1,0:T(2,128)S(1)}, u32[]{:S(2)}) copy-start(f32[39,4,2,128]{3,2,1,0:T(2,128)S(1)} %collective-permute-done.1.dn_ref) | copy-start | bytes 479236
  13.9 15.4 %copy-start.6 = (f32[4,32,128]{2,1,0:T(8,128)S(1)}, f32[4,32,128]{2,1,0:T(8,128)}, u32[]{:S(2)}) copy-start(f32[4,32,128]{2,1,0:T(8,128)} %reshape.23.solid_ref) | copy-start | bytes 196612
  18.3 28.5 %copy-start.7 = (s32[1,1,64]{2,1,0:T(1,128)S(1)}, s32[1,1,64]{2,1,0:T(1,128)}, u32[]{:S(2)}) copy-start(s32[1,1,64]{2,1,0:T(1,128)} %param.8) | copy-start | bytes 772
  18.3 28.6 %copy-start.8 = (s32[1,1,64]{2,1,0:T(1,128)S(1)}, s32[1,1,64]{2,1,0:T(1,128)}, u32[]{:S(2)}) copy-start(s32[1,1,64]{2,1,0:T(1,128)} %param.9) | copy-start | bytes 772
  18.3 5.1 %collective-permute-start.2 = (f32[3,48,128]{2,1,0:T(8,128)}, f32[3,48,128]{2,1,0:T(8,128)S(1)}, u32[]{:S(2)}, u32[]{:S(2)}) collective-permute-start(f32[3,48,128]{2,1,0:T(8,128)} %get-tuple-element.6), channel_id=1, source_target_pairs={{0,32},{32,64},{64,96},{96,128},{128,160},{160,192},{192,224},{224... | collective-permute-start | bytes 221192 | tf_op jit(solution)/shard_map/ppermute | solution.py:193
  21.1 8.2 %collective-permute-start.3 = (f32[3,48,128]{2,1,0:T(8,128)}, f32[3,48,128]{2,1,0:T(8,128)S(1)}, u32[]{:S(2)}, u32[]{:S(2)}) collective-permute-start(f32[3,48,128]{2,1,0:T(8,128)} %get-tuple-element.7), channel_id=1, source_target_pairs={{0,224},{32,0},{64,32},{96,64},{128,96},{160,128},{192,160},{224,1... | collective-permute-start | bytes 221192 | tf_op jit(solution)/shard_map/ppermute | solution.py:193
  29.3 0.9 %copy-start.3 = (f32[39,4,2,128]{3,2,1,0:T(2,128)S(1)}, f32[39,4,2,128]{3,2,1,0:T(2,128)}, u32[]{:S(2)}) copy-start(f32[39,4,2,128]{3,2,1,0:T(2,128)} %copy-done.2) | copy-start | bytes 479236
  30.2 0.9 %copy-start.5 = (f32[39,4,2,128]{3,2,1,0:T(2,128)S(1)}, f32[39,4,2,128]{3,2,1,0:T(2,128)}, u32[]{:S(2)}) copy-start(f32[39,4,2,128]{3,2,1,0:T(2,128)} %copy-done.4) | copy-start | bytes 479236

commit v3 on v2

--- a/solution.py
+++ b/solution.py
@@ -14,7 +14,7 @@
 
 ROWS = 48
 LANES = 256
-TOP = 8
+TOP = 2
 
 
 def collide(fields, solid):
@@ -57,12 +57,15 @@
     return planes
 
 
-def pack_kernel(f_ref, cot_ref, solid_ref, up_ref, dn_ref, to_right_ref, to_left_ref, tile_ref):
+def pack_kernel(f_ref, cot_ref, solid_ref, up_ref, dn_ref, to_right_ref, to_left_ref):
     q_count, layers, height, width = f_ref.shape
-    lane = lax.broadcasted_iota(jnp.int32, (ROWS, width), 1)
-    to_right_ref[...] = jnp.zeros(to_right_ref.shape, jnp.float32)
-    to_left_ref[...] = jnp.zeros(to_left_ref.shape, jnp.float32)
-    tile_ref[...] = jnp.zeros(tile_ref.shape, jnp.float32)
+    groups = to_right_ref.shape[0]
+    lane_own = lax.broadcasted_iota(jnp.int32, (height, width), 1)
+    lane_edge = lax.broadcasted_iota(jnp.int32, (2, width), 1)
+    zero_own = jnp.zeros((height, width), jnp.float32)
+    zero_edge = jnp.zeros((2, width), jnp.float32)
+    acc = {(side, part, g): (zero_own if part == 1 else zero_edge)
+           for side in range(2) for part in range(3) for g in range(groups)}
     for index, (field, q, z) in enumerate(plane_list(q_count, layers)):
         if field == 0:
             own = f_ref[q, z]
@@ -71,16 +74,21 @@
         else:
             own = solid_ref[z]
         row_index = field * q_count + q
-        tile_ref[TOP : TOP + height, :] = own
-        tile_ref[TOP - 2 : TOP, :] = up_ref[row_index, z]
-        tile_ref[TOP + height : TOP + height + 2, :] = dn_ref[row_index, z]
-        tile = tile_ref[...]
+        parts = (up_ref[row_index, z], own, dn_ref[row_index, z])
         group, slot = divmod(index, width // 2)
-        mine = (lane == 2 * slot) | (lane == 2 * slot + 1)
-        moved = pltpu.roll(tile, (2 * slot - (width - 2)) % width, 1)
-        to_right_ref[group] = jnp.where(mine, moved, to_right_ref[group])
-        moved = pltpu.roll(tile, (2 * slot) % width, 1)
-        to_left_ref[group] = jnp.where(mine, moved, to_left_ref[group])
+        for side, shift in ((0, (2 * slot - (width - 2)) % width), (1, (2 * slot) % width)):
+            for part, value in enumerate(parts):
+                lane = lane_own if part == 1 else lane_edge
+                mine = (lane == 2 * slot) | (lane == 2 * slot + 1)
+                key = (side, part, group)
+                acc[key] = jnp.where(mine, pltpu.roll(value, shift, 1), acc[key])
+    zero_tail = jnp.zeros((ROWS - TOP - height - 2, width), jnp.float32)
+    for side, out in ((0, to_right_ref), (1, to_left_ref)):
+        for g in range(groups):
+            out[g, 0:TOP] = acc[(side, 0, g)]
+            out[g, TOP : TOP + height] = acc[(side, 1, g)]
+            out[g, TOP + height : TOP + height + 2] = acc[(side, 2, g)]
+            out[g, TOP + height + 2 : ROWS] = zero_tail
 
 
 def compute_kernel(f_ref, cot_ref, solid_ref, up_ref, dn_ref, from_left_ref, from_right_ref,
@@ -96,7 +104,6 @@
         from_r = pltpu.roll(from_right_ref[group], (-2 * slot) % width, 1)
         from_l = pltpu.roll(from_left_ref[group], (width - 2 - 2 * slot) % width, 1)
         target[:, width:LANES] = jnp.where(low_lanes, from_r, jnp.where(high_lanes, from_l, 0.0))
-        target[0 : TOP - 2, 0:width] = jnp.zeros((TOP - 2, width), jnp.float32)
         target[TOP + height + 2 : ROWS, 0:width] = jnp.zeros((tail, width), jnp.float32)
         target[TOP - 2 : TOP, 0:width] = up_rows
         target[TOP : TOP + height, 0:width] = own
@@ -113,7 +120,7 @@
             place(es.at[z], index, solid_ref[z], up_ref[row_index, z], dn_ref[row_index, z])
 
     def phase_one(z, carry):
-        for k in range(ROWS // 8):
+        for k in range((TOP + height + 2 + 7) // 8):
             rows = pl.ds(8 * k, 8)
             out = collide([ef[q, z, rows, :] for q in range(q_count)], es[z, rows, :])
             for q in range(q_count):
@@ -208,7 +215,6 @@
         out_shape=(buffer, buffer),
         in_specs=vmem_specs(5),
         out_specs=tuple(vmem_specs(2)),
-        scratch_shapes=[pltpu.VMEM((ROWS, cols_dev), jnp.float32)],
     )(f_start, cotangent, solid, up_rows, dn_rows)
     from_left = shift(to_right, "gx", nx, 1)
     from_right = shift(to_left, "gx", nx, -1)

time: 47.7 us -> 46 us (0.964)
  Pallas kernels: 19.8 us -> 18.1 us
    pallas_call x1, Pallas kernels: 15.4 us -> 14.1 us  [on_device(): pl.pallas_call(compute_kernel, out_shape=(jax.ShapeDtypeStruct(f_start.sh...]
where the time goes in v3:
time: 46 us; the launch traced here: 45.8 us
  Pallas kernels  18.1 us (39%)
  waiting for transfers between devices  11 us (24%)
  starting transfers between devices  9.28 us (20%)
  local copies, waits for them, and re-layouts  4.23 us (9%)
  other arithmetic  2.55 us (6%)
  between operations  0.69 us (2%)
    pallas_call x1, Pallas kernels, on_device(): pl.pallas_call(compute_kernel, out_shape=(jax.ShapeDtypeStruct(f_start.sh...  14.1 us
    ppermute x4, waiting for transfers between devices, shift(): lax.ppermute(value, axis, [(i, (i + step) % size) for i in range(size)])  11 us
    ppermute x4, starting transfers between devices, shift(): lax.ppermute(value, axis, [(i, (i + step) % size) for i in range(size)])  9.28 us
    pallas_call x1, Pallas kernels, on_device(): pl.pallas_call(pack_kernel, out_shape=(buffer, buffer), in_specs=vmem_spe...  3.98 us
    unnamed x18, local copies, waits for them, and re-layouts  1.85 us
    slice x1, local copies, waits for them, and re-layouts, on_device(): f_start[:, :, 0:2]  1.28 us
  transfers between devices with their start and end apart: 4, of which 4 were waited for; matrix products, arithmetic and copies ran while one was open for 0% of the time, Pallas kernels for 0%

profile of v3, /device:TPU:6, one launch (start us, length us, event | category | flops | bytes accessed | tf_op | source)
XLA Modules:
  0.0 45.8 jit_solution(13843489758005255890)
XLA Ops:
  0.6 0.8 %select_reduce_fusion.3 = f32[64]{0:T(128)S(1)} fusion(f32[16]{0:T(128)} %bitcast.4, s32[64]{0:T(128)} %bitcast.7), kind=kLoop, calls=%fused_computation.6 | loop fusion | flops 3008 | bytes 576 | tf_op jit(solution)/shard_map/reduce_sum | solution.py:192
  1.4 0.7 %select_reduce_fusion.1 = f32[128]{0:T(128)S(1)} fusion(f32[64]{0:T(128)S(1)} %select_reduce_fusion.3, s32[64]{0:T(128)} %bitcast.5), kind=kLoop, calls=%fused_computation.3 | loop fusion | flops 24448 | bytes 1024 | tf_op jit(solution)/shard_map/reduce_sum | solution.py:193
  2.1 0.1 broadcast_in_dim.6
  2.2 0.1 fusion.2
  2.3 1.3 %fusion = (f32[19,4,2,128]{3,2,1,0:T(2,128)S(1)}, f32[19,4,2,128]{3,2,1,0:T(2,128)S(1)}, f32[19,4,2,128]{3,2,1,0:T(2,128)S(1)}, f32[19,4,2,128]{3,2,1,0:T(2,128)S(1)}) fusion(f32[19,4,32,128]{3,2,1,0:T(8,128)} %f_ref.3, bf16[19,4,32,128]{3,2,1,0:T(8,128)(2,1)} %cot_ref.3), kind=kLoop, calls=%fused_computation.8 | loop fusion | bytes 622592 | tf_op jit(solution)/shard_map/slice | solution.py:203
  3.6 0.1 broadcast_in_dim.7
  3.7 0.1 pad_maximum_fusion
  3.7 0.1 collective-permute-start
  3.8 0.1 broadcast_in_dim.8
  3.9 0.0 copy-start
  3.9 0.0 copy-start.1
  3.9 0.1 pad_maximum_fusion.1
  4.0 6.4 %collective-permute-start.1 = (f32[39,4,2,128]{3,2,1,0:T(2,128)S(1)}, f32[39,4,2,128]{3,2,1,0:T(2,128)S(1)}, u32[]{:S(2)}, u32[]{:S(2)}) collective-permute-start(f32[39,4,2,128]{3,2,1,0:T(2,128)S(1)} %pad_maximum_fusion.1), channel_id=1, source_target_pairs={{0,31},{1,0},{2,1},{3,2},{4,3},{5,4},{6,5},{7,6},{8,7},{9,8},{10,9... | collective-permute-start | bytes 479240 | tf_op jit(solution)/shard_map/ppermute | solution.py:200
  10.4 2.7 %collective-permute-done.up_ref = f32[39,4,2,128]{3,2,1,0:T(2,128)S(1)} collective-permute-done((f32[39,4,2,128]{3,2,1,0:T(2,128)S(1)}, f32[39,4,2,128]{3,2,1,0:T(2,128)S(1)}, u32[]{:S(2)}, u32[]{:S(2)}) %collective-permute-start) | collective-permute-done | bytes 159776 | tf_op jit(solution)/shard_map/ppermute | solution.py:200
  13.1 0.0 copy-start.2
  13.1 0.1 collective-permute-done.1.dn_ref
  13.2 0.0 copy-start.4
  13.2 0.7 %reshape.23.solid_ref = f32[4,32,128]{2,1,0:T(8,128)} broadcast(f32[4,32]{1,0:T(4,128)S(1)} %broadcast_in_dim.6), dimensions={0,1} | broadcast | bytes 66048 | tf_op jit(solution)/shard_map/reshape | solution.py:197
  13.9 0.0 copy-done.2
  13.9 0.0 copy-done.4
  13.9 0.0 copy-start.6
  13.9 4.0 %shard_map.68 = (f32[3,48,128]{2,1,0:T(8,128)}, f32[3,48,128]{2,1,0:T(8,128)}) custom-call(f32[19,4,32,128]{3,2,1,0:T(8,128)} %f_ref.3, bf16[19,4,32,128]{3,2,1,0:T(8,128)(2,1)} %cot_ref.3, f32[4,32,128]{2,1,0:T(8,128)} %reshape.23.solid_ref, f32[39,4,2,128]{3,2,1,0:T(2,128)} %copy-done.2, f32[39,4,2,128]{3,2,1,0:T(2,128)} %copy-done.4), custom_call_target="tpu_custom_call" | custom-call | tf_op jit(solution)/shard_map/pallas_call | solution.py:213
  17.9 0.0 copy-start.7
  17.9 0.0 copy-start.8
  17.9 2.8 %collective-permute-start.2 = (f32[3,48,128]{2,1,0:T(8,128)}, f32[3,48,128]{2,1,0:T(8,128)S(1)}, u32[]{:S(2)}, u32[]{:S(2)}) collective-permute-start(f32[3,48,128]{2,1,0:T(8,128)} %get-tuple-element.6), channel_id=1, source_target_pairs={{0,32},{32,64},{64,96},{96,128},{128,160},{160,192},{192,224},{224... | collective-permute-start | bytes 221192 | tf_op jit(solution)/shard_map/ppermute | solution.py:200
  20.7 0.0 collective-permute-start.3
  20.7 2.3 %collective-permute-done.2.from_left_ref = f32[3,48,128]{2,1,0:T(8,128)S(1)} collective-permute-done((f32[3,48,128]{2,1,0:T(8,128)}, f32[3,48,128]{2,1,0:T(8,128)S(1)}, u32[]{:S(2)}, u32[]{:S(2)}) %collective-permute-start.2) | collective-permute-done | bytes 73760 | tf_op jit(solution)/shard_map/ppermute | solution.py:200
  23.0 5.9 %collective-permute-done.3.from_right_ref = f32[3,48,128]{2,1,0:T(8,128)S(1)} collective-permute-done((f32[3,48,128]{2,1,0:T(8,128)}, f32[3,48,128]{2,1,0:T(8,128)S(1)}, u32[]{:S(2)}, u32[]{:S(2)}) %collective-permute-start.3) | collective-permute-done | bytes 73760 | tf_op jit(solution)/shard_map/ppermute | solution.py:200
  28.8 0.0 copy-done
  28.9 0.0 copy-done.1
  28.9 0.0 copy-done.6
  28.9 0.0 copy-start.3
  28.9 0.9 %copy-done.3 = f32[39,4,2,128]{3,2,1,0:T(2,128)S(1)} copy-done((f32[39,4,2,128]{3,2,1,0:T(2,128)S(1)}, f32[39,4,2,128]{3,2,1,0:T(2,128)}, u32[]{:S(2)}) %copy-start.3) | copy-done | bytes 159768
  29.8 0.0 copy-start.5
  29.8 0.9 %copy-done.5 = f32[39,4,2,128]{3,2,1,0:T(2,128)S(1)} copy-done((f32[39,4,2,128]{3,2,1,0:T(2,128)S(1)}, f32[39,4,2,128]{3,2,1,0:T(2,128)}, u32[]{:S(2)}) %copy-start.5) | copy-done | bytes 159768
  30.7 14.1 %shard_map.69 = (f32[19,4,32,128]{3,2,1,0:T(8,128)}, f32[4,32,128]{2,1,0:T(8,128)S(1)}) custom-call(f32[19,4,32,128]{3,2,1,0:T(8,128)S(1)} %copy-done, bf16[19,4,32,128]{3,2,1,0:T(8,128)(2,1)S(1)} %copy-done.1, f32[4,32,128]{2,1,0:T(8,128)S(1)} %copy-done.6, f32[39,4,2,128]{3,2,1,0:T(2,128)S(1)} %copy-done.3, f32[39,4,2,128]{3,2,1,0:T(2,128)S(1)} %copy-done.5, ...), custom_call_target="tpu_custom_call" | custom-call | tf_op jit(solution)/shard_map/pallas_call | solution.py:222
  44.8 0.1 reduce_sum.47
  44.9 0.1 mul.41
  45.0 0.0 copy-done.7
  45.0 0.2 select_reduce_fusion
  45.2 0.0 copy-done.8
  45.2 0.6 %select_reduce_fusion.2 = f32[16]{0:T(128)} fusion(f32[64]{0:T(128)S(1)} %select_reduce_fusion, s32[64]{0:T(128)S(1)} %bitcast.8), kind=kLoop, calls=%fused_computation.5 | loop fusion | flops 3056 | bytes 576 | tf_op jit(solution)/shard_map/reduce_sum | solution.py:242
Async XLA Ops:
  3.7 9.3 %collective-permute-start = (f32[39,4,2,128]{3,2,1,0:T(2,128)S(1)}, f32[39,4,2,128]{3,2,1,0:T(2,128)S(1)}, u32[]{:S(2)}, u32[]{:S(2)}) collective-permute-start(f32[39,4,2,128]{3,2,1,0:T(2,128)S(1)} %pad_maximum_fusion), channel_id=1, source_target_pairs={{0,1},{1,2},{2,3},{3,4},{4,5},{5,6},{6,7},{7,8},{8,9},{9,10},{10,1... | collective-permute-start | bytes 479240 | tf_op jit(solution)/shard_map/ppermute | solution.py:200
  3.9 25.0 %copy-start = (f32[19,4,32,128]{3,2,1,0:T(8,128)S(1)}, f32[19,4,32,128]{3,2,1,0:T(8,128)}, u32[]{:S(2)}) copy-start(f32[19,4,32,128]{3,2,1,0:T(8,128)} %f_ref.3) | copy-start | bytes 3735556
  3.9 25.0 %copy-start.1 = (bf16[19,4,32,128]{3,2,1,0:T(8,128)(2,1)S(1)}, bf16[19,4,32,128]{3,2,1,0:T(8,128)(2,1)}, u32[]{:S(2)}) copy-start(bf16[19,4,32,128]{3,2,1,0:T(8,128)(2,1)} %cot_ref.3) | copy-start | bytes 1867780
  4.0 9.2 %collective-permute-start.1 = (f32[39,4,2,128]{3,2,1,0:T(2,128)S(1)}, f32[39,4,2,128]{3,2,1,0:T(2,128)S(1)}, u32[]{:S(2)}, u32[]{:S(2)}) collective-permute-start(f32[39,4,2,128]{3,2,1,0:T(2,128)S(1)} %pad_maximum_fusion.1), channel_id=1, source_target_pairs={{0,31},{1,0},{2,1},{3,2},{4,3},{5,4},{6,5},{7,6},{8,7},{9,8},{10,9... | collective-permute-start | bytes 479240 | tf_op jit(solution)/shard_map/ppermute | solution.py:200
  13.1 0.8 %copy-start.2 = (f32[39,4,2,128]{3,2,1,0:T(2,128)}, f32[39,4,2,128]{3,2,1,0:T(2,128)S(1)}, u32[]{:S(2)}) copy-start(f32[39,4,2,128]{3,2,1,0:T(2,128)S(1)} %collective-permute-done.up_ref) | copy-start | bytes 479236
  13.2 0.7 %copy-start.4 = (f32[39,4,2,128]{3,2,1,0:T(2,128)}, f32[39,4,2,128]{3,2,1,0:T(2,128)S(1)}, u32[]{:S(2)}) copy-start(f32[39,4,2,128]{3,2,1,0:T(2,128)S(1)} %collective-permute-done.1.dn_ref) | copy-start | bytes 479236
  13.9 15.0 %copy-start.6 = (f32[4,32,128]{2,1,0:T(8,128)S(1)}, f32[4,32,128]{2,1,0:T(8,128)}, u32[]{:S(2)}) copy-start(f32[4,32,128]{2,1,0:T(8,128)} %reshape.23.solid_ref) | copy-start | bytes 196612
  17.9 27.2 %copy-start.7 = (s32[1,1,64]{2,1,0:T(1,128)S(1)}, s32[1,1,64]{2,1,0:T(1,128)}, u32[]{:S(2)}) copy-start(s32[1,1,64]{2,1,0:T(1,128)} %param.8) | copy-start | bytes 772
  17.9 27.4 %copy-start.8 = (s32[1,1,64]{2,1,0:T(1,128)S(1)}, s32[1,1,64]{2,1,0:T(1,128)}, u32[]{:S(2)}) copy-start(s32[1,1,64]{2,1,0:T(1,128)} %param.9) | copy-start | bytes 772
  17.9 5.1 %collective-permute-start.2 = (f32[3,48,128]{2,1,0:T(8,128)}, f32[3,48,128]{2,1,0:T(8,128)S(1)}, u32[]{:S(2)}, u32[]{:S(2)}) collective-permute-start(f32[3,48,128]{2,1,0:T(8,128)} %get-tuple-element.6), channel_id=1, source_target_pairs={{0,32},{32,64},{64,96},{96,128},{128,160},{160,192},{192,224},{224... | collective-permute-start | bytes 221192 | tf_op jit(solution)/shard_map/ppermute | solution.py:200
  20.7 8.2 %collective-permute-start.3 = (f32[3,48,128]{2,1,0:T(8,128)}, f32[3,48,128]{2,1,0:T(8,128)S(1)}, u32[]{:S(2)}, u32[]{:S(2)}) collective-permute-start(f32[3,48,128]{2,1,0:T(8,128)} %get-tuple-element.7), channel_id=1, source_target_pairs={{0,224},{32,0},{64,32},{96,64},{128,96},{160,128},{192,160},{224,1... | collective-permute-start | bytes 221192 | tf_op jit(solution)/shard_map/ppermute | solution.py:200
  28.9 0.9 %copy-start.3 = (f32[39,4,2,128]{3,2,1,0:T(2,128)S(1)}, f32[39,4,2,128]{3,2,1,0:T(2,128)}, u32[]{:S(2)}) copy-start(f32[39,4,2,128]{3,2,1,0:T(2,128)} %copy-done.2) | copy-start | bytes 479236
  29.8 0.9 %copy-start.5 = (f32[39,4,2,128]{3,2,1,0:T(2,128)S(1)}, f32[39,4,2,128]{3,2,1,0:T(2,128)}, u32[]{:S(2)}) copy-start(f32[39,4,2,128]{3,2,1,0:T(2,128)} %copy-done.4) | copy-start | bytes 479236

commit v4 on v3

--- a/solution.py
+++ b/solution.py
@@ -57,15 +57,12 @@
     return planes
 
 
-def pack_kernel(f_ref, cot_ref, solid_ref, up_ref, dn_ref, to_right_ref, to_left_ref):
+def pack_own_kernel(f_ref, cot_ref, solid_ref, to_right_ref, to_left_ref):
     q_count, layers, height, width = f_ref.shape
     groups = to_right_ref.shape[0]
-    lane_own = lax.broadcasted_iota(jnp.int32, (height, width), 1)
-    lane_edge = lax.broadcasted_iota(jnp.int32, (2, width), 1)
-    zero_own = jnp.zeros((height, width), jnp.float32)
-    zero_edge = jnp.zeros((2, width), jnp.float32)
-    acc = {(side, part, g): (zero_own if part == 1 else zero_edge)
-           for side in range(2) for part in range(3) for g in range(groups)}
+    lane = lax.broadcasted_iota(jnp.int32, (height, width), 1)
+    zero = jnp.zeros((height, width), jnp.float32)
+    acc = {(side, g): zero for side in range(2) for g in range(groups)}
     for index, (field, q, z) in enumerate(plane_list(q_count, layers)):
         if field == 0:
             own = f_ref[q, z]
@@ -73,51 +70,76 @@
             own = cot_ref[q, z].astype(jnp.float32)
         else:
             own = solid_ref[z]
+        group, slot = divmod(index, width // 2)
+        mine = (lane == 2 * slot) | (lane == 2 * slot + 1)
+        for side, shift in ((0, (2 * slot - (width - 2)) % width), (1, (2 * slot) % width)):
+            acc[(side, group)] = jnp.where(mine, pltpu.roll(own, shift, 1), acc[(side, group)])
+    for side, out in ((0, to_right_ref), (1, to_left_ref)):
+        for g in range(groups):
+            out[g] = acc[(side, g)]
+
+
+def pack_edge_kernel(own_right_ref, own_left_ref, up_ref, dn_ref, to_right_ref, to_left_ref):
+    groups, height, width = own_right_ref.shape
+    planes = plane_list((up_ref.shape[0] - 1) // 2, up_ref.shape[1])
+    q_count = (up_ref.shape[0] - 1) // 2
+    lane = lax.broadcasted_iota(jnp.int32, (2, width), 1)
+    zero = jnp.zeros((2, width), jnp.float32)
+    acc = {(side, part, g): zero for side in range(2) for part in range(2) for g in range(groups)}
+    for index, (field, q, z) in enumerate(planes):
         row_index = field * q_count + q
-        parts = (up_ref[row_index, z], own, dn_ref[row_index, z])
         group, slot = divmod(index, width // 2)
+        mine = (lane == 2 * slot) | (lane == 2 * slot + 1)
         for side, shift in ((0, (2 * slot - (width - 2)) % width), (1, (2 * slot) % width)):
-            for part, value in enumerate(parts):
-                lane = lane_own if part == 1 else lane_edge
-                mine = (lane == 2 * slot) | (lane == 2 * slot + 1)
+            for part, value in enumerate((up_ref[row_index, z], dn_ref[row_index, z])):
                 key = (side, part, group)
                 acc[key] = jnp.where(mine, pltpu.roll(value, shift, 1), acc[key])
     zero_tail = jnp.zeros((ROWS - TOP - height - 2, width), jnp.float32)
-    for side, out in ((0, to_right_ref), (1, to_left_ref)):
+    for side, own, out in ((0, own_right_ref, to_right_ref), (1, own_left_ref, to_left_ref)):
         for g in range(groups):
             out[g, 0:TOP] = acc[(side, 0, g)]
-            out[g, TOP : TOP + height] = acc[(side, 1, g)]
-            out[g, TOP + height : TOP + height + 2] = acc[(side, 2, g)]
+            out[g, TOP : TOP + height] = own[g]
+            out[g, TOP + height : TOP + height + 2] = acc[(side, 1, g)]
             out[g, TOP + height + 2 : ROWS] = zero_tail
 
 
-def compute_kernel(f_ref, cot_ref, solid_ref, up_ref, dn_ref, from_left_ref, from_right_ref,
-                   grad_ref, sbar_ref, ef, ec, es, cf, bo, sb2):
+def compute_kernel(f_hbm, cot_hbm, solid_ref, up_ref, dn_ref, from_left_ref, from_right_ref,
+                   grad_ref, sbar_ref, ef, ec, es, cf, bo, sb2, f_ref, cot_ref, sems):
     q_count, layers, height, width = f_ref.shape
+    f_copy = pltpu.make_async_copy(f_hbm, f_ref, sems.at[0])
+    cot_copy = pltpu.make_async_copy(cot_hbm, cot_ref, sems.at[1])
+    f_copy.start()
+    cot_copy.start()
     lane = lax.broadcasted_iota(jnp.int32, (ROWS, width), 1)
     low_lanes = lane < 2
     high_lanes = lane >= width - 2
     tail = ROWS - (TOP + height + 2)
 
-    def place(target, index, own, up_rows, dn_rows):
+    def place_halo(target, index, up_rows, dn_rows):
         group, slot = divmod(index, width // 2)
         from_r = pltpu.roll(from_right_ref[group], (-2 * slot) % width, 1)
         from_l = pltpu.roll(from_left_ref[group], (width - 2 - 2 * slot) % width, 1)
         target[:, width:LANES] = jnp.where(low_lanes, from_r, jnp.where(high_lanes, from_l, 0.0))
         target[TOP + height + 2 : ROWS, 0:width] = jnp.zeros((tail, width), jnp.float32)
         target[TOP - 2 : TOP, 0:width] = up_rows
-        target[TOP : TOP + height, 0:width] = own
         target[TOP + height : TOP + height + 2, 0:width] = dn_rows
 
+    targets = []
     for index, (field, q, z) in enumerate(plane_list(q_count, layers)):
         row_index = field * q_count + q
+        target = (ef.at[q, z], ec.at[q, z], es.at[z])[field]
+        place_halo(target, index, up_ref[row_index, z], dn_ref[row_index, z])
+        targets.append((field, q, z, target))
+    f_copy.wait()
+    cot_copy.wait()
+    for field, q, z, target in targets:
         if field == 0:
-            place(ef.at[q, z], index, f_ref[q, z], up_ref[row_index, z], dn_ref[row_index, z])
+            own = f_ref[q, z]
         elif field == 1:
-            place(ec.at[q, z], index, cot_ref[q, z].astype(jnp.float32), up_ref[row_index, z],
-                  dn_ref[row_index, z])
+            own = cot_ref[q, z].astype(jnp.float32)
         else:
-            place(es.at[z], index, solid_ref[z], up_ref[row_index, z], dn_ref[row_index, z])
+            own = solid_ref[z]
+        target[TOP : TOP + height, 0:width] = own
 
     def phase_one(z, carry):
         for k in range((TOP + height + 2 + 7) // 8):
@@ -210,12 +232,19 @@
     plane_count = (2 * q_count + 1) * layers_dev
     groups = -(-plane_count // (cols_dev // 2))
     buffer = jax.ShapeDtypeStruct((groups, ROWS, cols_dev), jnp.float32)
+    own_buffer = jax.ShapeDtypeStruct((groups, rows_dev, cols_dev), jnp.float32)
+    own_right, own_left = pl.pallas_call(
+        pack_own_kernel,
+        out_shape=(own_buffer, own_buffer),
+        in_specs=vmem_specs(3),
+        out_specs=tuple(vmem_specs(2)),
+    )(f_start, cotangent, solid)
     to_right, to_left = pl.pallas_call(
-        pack_kernel,
+        pack_edge_kernel,
         out_shape=(buffer, buffer),
-        in_specs=vmem_specs(5),
+        in_specs=vmem_specs(4),
         out_specs=tuple(vmem_specs(2)),
-    )(f_start, cotangent, solid, up_rows, dn_rows)
+    )(own_right, own_left, up_rows, dn_rows)
     from_left = shift(to_right, "gx", nx, 1)
     from_right = shift(to_left, "gx", nx, -1)
     big = pltpu.VMEM((q_count, layers_dev, ROWS, LANES), jnp.float32)
@@ -225,7 +254,7 @@
             jax.ShapeDtypeStruct(f_start.shape, jnp.float32),
             jax.ShapeDtypeStruct(solid.shape, jnp.float32),
         ),
-        in_specs=vmem_specs(7),
+        in_specs=[pl.BlockSpec(memory_space=pl.ANY)] * 2 + vmem_specs(5),
         out_specs=tuple(vmem_specs(2)),
         scratch_shapes=[
             big,
@@ -234,6 +263,9 @@
             big,
             pltpu.VMEM((q_count, layers_dev, ROWS - 8, LANES), jnp.float32),
             pltpu.VMEM((layers_dev, ROWS - 8, LANES), jnp.float32),
+            pltpu.VMEM(f_start.shape, jnp.float32),
+            pltpu.VMEM(cotangent.shape, cotangent.dtype),
+            pltpu.SemaphoreType.DMA((2,)),
         ],
         compiler_params=pltpu.CompilerParams(vmem_limit_bytes=48 * 1024 * 1024),
     )(f_start, cotangent, solid, up_rows, dn_rows, from_left, from_right)

time: 46 us -> 46.2 us (level)
  waiting for transfers between devices: 11 us -> 8.18 us
  Pallas kernels: 18.1 us -> 20.3 us
  local copies, waits for them, and re-layouts: 4.23 us -> 4.9 us
    ppermute x4, waiting for transfers between devices: 11 us -> 8.18 us  [shift(): lax.ppermute(value, axis, [(i, (i + step) % size) for i in range(size)])]
    pallas_call x1 -> x2, Pallas kernels: 3.98 us -> 5.66 us  [the longest x1 3.22 us: on_device(): pl.pallas_call(pack_own_kernel, out_shape=(own_buffer, own_buffer), in_sp...]
    unnamed x18, local copies, waits for them, and re-layouts: 1.85 us -> 2.54 us
    pallas_call x1, Pallas kernels: 14.1 us -> 14.6 us  [on_device(): pl.pallas_call(compute_kernel, out_shape=(jax.ShapeDtypeStruct(f_start.sh...]
  transfers between devices with their start and end apart: 4 -> 4, of which waited for: 4 -> 2; matrix products, arithmetic and copies ran while one was open for 0% -> 2% of each run, Pallas kernels for 0% -> 7%
where the time goes in v4:
time: 46.2 us; the launch traced here: 45.9 us
  Pallas kernels  20.3 us (44%)
  starting transfers between devices  9.28 us (20%)
  waiting for transfers between devices  8.18 us (18%)
  local copies, waits for them, and re-layouts  4.9 us (11%)
  other arithmetic  2.55 us (6%)
  between operations  0.73 us (2%)
    pallas_call x1, Pallas kernels, on_device(): pl.pallas_call(compute_kernel, out_shape=(jax.ShapeDtypeStruct(f_start.sh...  14.6 us
    ppermute x4, starting transfers between devices, shift(): lax.ppermute(value, axis, [(i, (i + step) % size) for i in range(size)])  9.28 us
    ppermute x4, waiting for transfers between devices, shift(): lax.ppermute(value, axis, [(i, (i + step) % size) for i in range(size)])  8.18 us
    pallas_call x1, Pallas kernels, on_device(): pl.pallas_call(pack_own_kernel, out_shape=(own_buffer, own_buffer), in_sp...  3.22 us
    unnamed x18, local copies, waits for them, and re-layouts  2.54 us
    pallas_call x1, Pallas kernels, on_device(): pl.pallas_call(pack_edge_kernel, out_shape=(buffer, buffer), in_specs=vme...  2.44 us
    slice x1, local copies, waits for them, and re-layouts, on_device(): f_start[:, :, 0:2]  1.28 us
  transfers between devices with their start and end apart: 4, of which 2 were waited for; matrix products, arithmetic and copies ran while one was open for 2% of the time, Pallas kernels for 7%

profile of v4, /device:TPU:6, one launch (start us, length us, event | category | flops | bytes accessed | tf_op | source)
XLA Modules:
  0.0 45.9 jit_solution(7321501973637249193)
XLA Ops:
  0.6 0.8 %select_reduce_fusion.3 = f32[64]{0:T(128)S(1)} fusion(f32[16]{0:T(128)} %bitcast.4, s32[64]{0:T(128)} %bitcast.7), kind=kLoop, calls=%fused_computation.6 | loop fusion | flops 3008 | bytes 576 | tf_op jit(solution)/shard_map/reduce_sum | solution.py:214
  1.4 0.7 %select_reduce_fusion.1 = f32[128]{0:T(128)S(1)} fusion(f32[64]{0:T(128)S(1)} %select_reduce_fusion.3, s32[64]{0:T(128)} %bitcast.5), kind=kLoop, calls=%fused_computation.3 | loop fusion | flops 24448 | bytes 1024 | tf_op jit(solution)/shard_map/reduce_sum | solution.py:215
  2.1 0.1 broadcast_in_dim.6
  2.2 0.1 fusion.2
  2.3 1.3 %fusion = (f32[19,4,2,128]{3,2,1,0:T(2,128)S(1)}, f32[19,4,2,128]{3,2,1,0:T(2,128)S(1)}, f32[19,4,2,128]{3,2,1,0:T(2,128)S(1)}, f32[19,4,2,128]{3,2,1,0:T(2,128)S(1)}) fusion(f32[19,4,32,128]{3,2,1,0:T(8,128)} %f_hbm.1, bf16[19,4,32,128]{3,2,1,0:T(8,128)(2,1)} %cot_hbm.1), kind=kLoop, calls=%fused_computation.8 | loop fusion | bytes 622592 | tf_op jit(solution)/shard_map/slice | solution.py:225
  3.6 0.1 broadcast_in_dim.7
  3.7 0.1 pad_maximum_fusion
  3.7 0.1 collective-permute-start
  3.8 0.1 broadcast_in_dim.8
  3.9 0.1 pad_maximum_fusion.1
  4.0 0.0 copy-start
  4.0 0.0 copy-start.1
  4.0 6.4 %collective-permute-start.1 = (f32[39,4,2,128]{3,2,1,0:T(2,128)S(1)}, f32[39,4,2,128]{3,2,1,0:T(2,128)S(1)}, u32[]{:S(2)}, u32[]{:S(2)}) collective-permute-start(f32[39,4,2,128]{3,2,1,0:T(2,128)S(1)} %pad_maximum_fusion.1), channel_id=1, source_target_pairs={{0,31},{1,0},{2,1},{3,2},{4,3},{5,4},{6,5},{7,6},{8,7},{9,8},{10,9... | collective-permute-start | bytes 479240 | tf_op jit(solution)/shard_map/ppermute | solution.py:222
  10.4 0.7 %reshape.23.solid_ref = f32[4,32,128]{2,1,0:T(8,128)} broadcast(f32[4,32]{1,0:T(4,128)S(1)} %broadcast_in_dim.6), dimensions={0,1} | broadcast | bytes 66048 | tf_op jit(solution)/shard_map/reshape | solution.py:219
  11.1 0.0 copy-start.6
  11.1 3.2 %shard_map.68 = (f32[3,32,128]{2,1,0:T(8,128)}, f32[3,32,128]{2,1,0:T(8,128)}) custom-call(f32[19,4,32,128]{3,2,1,0:T(8,128)} %f_hbm.1, bf16[19,4,32,128]{3,2,1,0:T(8,128)(2,1)} %cot_hbm.1, f32[4,32,128]{2,1,0:T(8,128)} %reshape.23.solid_ref), custom_call_target="tpu_custom_call" | custom-call | tf_op jit(solution)/shard_map/pallas_call | solution.py:236
  14.3 0.0 collective-permute-done.up_ref
  14.3 0.0 copy-start.2
  14.3 0.0 collective-permute-done.1.dn_ref
  14.3 0.0 copy-start.4
  14.3 0.6 %copy-done.2 = f32[39,4,2,128]{3,2,1,0:T(2,128)} copy-done((f32[39,4,2,128]{3,2,1,0:T(2,128)}, f32[39,4,2,128]{3,2,1,0:T(2,128)S(1)}, u32[]{:S(2)}) %copy-start.2) | copy-done | bytes 159768
  15.0 0.0 copy-done.4
  15.0 2.4 %shard_map.69 = (f32[3,48,128]{2,1,0:T(8,128)}, f32[3,48,128]{2,1,0:T(8,128)}) custom-call(f32[3,32,128]{2,1,0:T(8,128)} %get-tuple-element.8.own_right_ref, f32[3,32,128]{2,1,0:T(8,128)} %get-tuple-element.9.own_left_ref, f32[39,4,2,128]{3,2,1,0:T(2,128)} %copy-done.2, f32[39,4,2,128]{3,2,1,0:T(2,128)} %copy-done.4), custom_call_target="tpu_custom_call" | custom-call | tf_op jit(solution)/shard_map/pallas_call | solution.py:242
  17.5 0.0 copy-start.7
  17.5 0.0 copy-start.8
  17.5 2.8 %collective-permute-start.2 = (f32[3,48,128]{2,1,0:T(8,128)}, f32[3,48,128]{2,1,0:T(8,128)S(1)}, u32[]{:S(2)}, u32[]{:S(2)}) collective-permute-start(f32[3,48,128]{2,1,0:T(8,128)} %get-tuple-element.10), channel_id=1, source_target_pairs={{0,32},{32,64},{64,96},{96,128},{128,160},{160,192},{192,224},{224... | collective-permute-start | bytes 221192 | tf_op jit(solution)/shard_map/ppermute | solution.py:222
  20.3 0.0 collective-permute-start.3
  20.3 2.3 %collective-permute-done.2.from_left_ref = f32[3,48,128]{2,1,0:T(8,128)S(1)} collective-permute-done((f32[3,48,128]{2,1,0:T(8,128)}, f32[3,48,128]{2,1,0:T(8,128)S(1)}, u32[]{:S(2)}, u32[]{:S(2)}) %collective-permute-start.2) | collective-permute-done | bytes 73760 | tf_op jit(solution)/shard_map/ppermute | solution.py:222
  22.6 5.9 %collective-permute-done.3.from_right_ref = f32[3,48,128]{2,1,0:T(8,128)S(1)} collective-permute-done((f32[3,48,128]{2,1,0:T(8,128)}, f32[3,48,128]{2,1,0:T(8,128)S(1)}, u32[]{:S(2)}, u32[]{:S(2)}) %collective-permute-start.3) | collective-permute-done | bytes 73760 | tf_op jit(solution)/shard_map/ppermute | solution.py:222
  28.4 0.0 copy-done
  28.5 0.0 copy-done.1
  28.5 0.0 copy-done.6
  28.5 0.0 copy-start.3
  28.5 0.9 %copy-done.3 = f32[39,4,2,128]{3,2,1,0:T(2,128)S(1)} copy-done((f32[39,4,2,128]{3,2,1,0:T(2,128)S(1)}, f32[39,4,2,128]{3,2,1,0:T(2,128)}, u32[]{:S(2)}) %copy-start.3) | copy-done | bytes 159768
  29.4 0.0 copy-start.5
  29.4 0.9 %copy-done.5 = f32[39,4,2,128]{3,2,1,0:T(2,128)S(1)} copy-done((f32[39,4,2,128]{3,2,1,0:T(2,128)S(1)}, f32[39,4,2,128]{3,2,1,0:T(2,128)}, u32[]{:S(2)}) %copy-start.5) | copy-done | bytes 159768
  30.3 14.6 %shard_map.70 = (f32[19,4,32,128]{3,2,1,0:T(8,128)}, f32[4,32,128]{2,1,0:T(8,128)S(1)}) custom-call(f32[19,4,32,128]{3,2,1,0:T(8,128)S(1)} %copy-done, bf16[19,4,32,128]{3,2,1,0:T(8,128)(2,1)S(1)} %copy-done.1, f32[4,32,128]{2,1,0:T(8,128)S(1)} %copy-done.6, f32[39,4,2,128]{3,2,1,0:T(2,128)S(1)} %copy-done.3, f32[39,4,2,128]{3,2,1,0:T(2,128)S(1)} %copy-done.5, ...), custom_call_target="tpu_custom_call" | custom-call | tf_op jit(solution)/shard_map/pallas_call | solution.py:251
  44.9 0.1 reduce_sum.47
  45.0 0.1 mul.41
  45.1 0.0 copy-done.7
  45.1 0.2 select_reduce_fusion
  45.3 0.0 copy-done.8
  45.3 0.6 %select_reduce_fusion.2 = f32[16]{0:T(128)} fusion(f32[64]{0:T(128)S(1)} %select_reduce_fusion, s32[64]{0:T(128)S(1)} %bitcast.8), kind=kLoop, calls=%fused_computation.5 | loop fusion | flops 3056 | bytes 576 | tf_op jit(solution)/shard_map/reduce_sum | solution.py:274
Async XLA Ops:
  3.7 10.6 %collective-permute-start = (f32[39,4,2,128]{3,2,1,0:T(2,128)S(1)}, f32[39,4,2,128]{3,2,1,0:T(2,128)S(1)}, u32[]{:S(2)}, u32[]{:S(2)}) collective-permute-start(f32[39,4,2,128]{3,2,1,0:T(2,128)S(1)} %pad_maximum_fusion), channel_id=1, source_target_pairs={{0,1},{1,2},{2,3},{3,4},{4,5},{5,6},{6,7},{7,8},{8,9},{9,10},{10,1... | collective-permute-start | bytes 479240 | tf_op jit(solution)/shard_map/ppermute | solution.py:222
  4.0 24.5 %copy-start = (f32[19,4,32,128]{3,2,1,0:T(8,128)S(1)}, f32[19,4,32,128]{3,2,1,0:T(8,128)}, u32[]{:S(2)}) copy-start(f32[19,4,32,128]{3,2,1,0:T(8,128)} %f_hbm.1) | copy-start | bytes 3735556
  4.0 24.5 %copy-start.1 = (bf16[19,4,32,128]{3,2,1,0:T(8,128)(2,1)S(1)}, bf16[19,4,32,128]{3,2,1,0:T(8,128)(2,1)}, u32[]{:S(2)}) copy-start(bf16[19,4,32,128]{3,2,1,0:T(8,128)(2,1)} %cot_hbm.1) | copy-start | bytes 1867780
  4.0 10.3 %collective-permute-start.1 = (f32[39,4,2,128]{3,2,1,0:T(2,128)S(1)}, f32[39,4,2,128]{3,2,1,0:T(2,128)S(1)}, u32[]{:S(2)}, u32[]{:S(2)}) collective-permute-start(f32[39,4,2,128]{3,2,1,0:T(2,128)S(1)} %pad_maximum_fusion.1), channel_id=1, source_target_pairs={{0,31},{1,0},{2,1},{3,2},{4,3},{5,4},{6,5},{7,6},{8,7},{9,8},{10,9... | collective-permute-start | bytes 479240 | tf_op jit(solution)/shard_map/ppermute | solution.py:222
  11.1 17.4 %copy-start.6 = (f32[4,32,128]{2,1,0:T(8,128)S(1)}, f32[4,32,128]{2,1,0:T(8,128)}, u32[]{:S(2)}) copy-start(f32[4,32,128]{2,1,0:T(8,128)} %reshape.23.solid_ref) | copy-start | bytes 196612
  14.3 0.7 %copy-start.2 = (f32[39,4,2,128]{3,2,1,0:T(2,128)}, f32[39,4,2,128]{3,2,1,0:T(2,128)S(1)}, u32[]{:S(2)}) copy-start(f32[39,4,2,128]{3,2,1,0:T(2,128)S(1)} %collective-permute-done.up_ref) | copy-start | bytes 479236
  14.3 0.7 %copy-start.4 = (f32[39,4,2,128]{3,2,1,0:T(2,128)}, f32[39,4,2,128]{3,2,1,0:T(2,128)S(1)}, u32[]{:S(2)}) copy-start(f32[39,4,2,128]{3,2,1,0:T(2,128)S(1)} %collective-permute-done.1.dn_ref) | copy-start | bytes 479236
  17.5 27.7 %copy-start.7 = (s32[1,1,64]{2,1,0:T(1,128)S(1)}, s32[1,1,64]{2,1,0:T(1,128)}, u32[]{:S(2)}) copy-start(s32[1,1,64]{2,1,0:T(1,128)} %param.8) | copy-start | bytes 772
  17.5 27.9 %copy-start.8 = (s32[1,1,64]{2,1,0:T(1,128)S(1)}, s32[1,1,64]{2,1,0:T(1,128)}, u32[]{:S(2)}) copy-start(s32[1,1,64]{2,1,0:T(1,128)} %param.9) | copy-start | bytes 772
  17.5 5.1 %collective-permute-start.2 = (f32[3,48,128]{2,1,0:T(8,128)}, f32[3,48,128]{2,1,0:T(8,128)S(1)}, u32[]{:S(2)}, u32[]{:S(2)}) collective-permute-start(f32[3,48,128]{2,1,0:T(8,128)} %get-tuple-element.10), channel_id=1, source_target_pairs={{0,32},{32,64},{64,96},{96,128},{128,160},{160,192},{192,224},{224... | collective-permute-start | bytes 221192 | tf_op jit(solution)/shard_map/ppermute | solution.py:222
  20.3 8.2 %collective-permute-start.3 = (f32[3,48,128]{2,1,0:T(8,128)}, f32[3,48,128]{2,1,0:T(8,128)S(1)}, u32[]{:S(2)}, u32[]{:S(2)}) collective-permute-start(f32[3,48,128]{2,1,0:T(8,128)} %get-tuple-element.11), channel_id=1, source_target_pairs={{0,224},{32,0},{64,32},{96,64},{128,96},{160,128},{192,160},{224,1... | collective-permute-start | bytes 221192 | tf_op jit(solution)/shard_map/ppermute | solution.py:222
  28.5 0.9 %copy-start.3 = (f32[39,4,2,128]{3,2,1,0:T(2,128)S(1)}, f32[39,4,2,128]{3,2,1,0:T(2,128)}, u32[]{:S(2)}) copy-start(f32[39,4,2,128]{3,2,1,0:T(2,128)} %copy-done.2) | copy-start | bytes 479236
  29.4 0.9 %copy-start.5 = (f32[39,4,2,128]{3,2,1,0:T(2,128)S(1)}, f32[39,4,2,128]{3,2,1,0:T(2,128)}, u32[]{:S(2)}) copy-start(f32[39,4,2,128]{3,2,1,0:T(2,128)} %copy-done.4) | copy-start | bytes 479236

commit v5 on v4

--- a/solution.py
+++ b/solution.py
@@ -79,9 +79,16 @@
             out[g] = acc[(side, g)]
 
 
-def pack_edge_kernel(own_right_ref, own_left_ref, up_ref, dn_ref, to_right_ref, to_left_ref):
+def pack_edge_kernel(own_right_ref, own_left_ref, up_hbm, dn_hbm, to_right_ref, to_left_ref, up_ref, dn_ref,
+                     sems):
     groups, height, width = own_right_ref.shape
-    planes = plane_list((up_ref.shape[0] - 1) // 2, up_ref.shape[1])
+    up_copy = pltpu.make_async_copy(up_hbm, up_ref, sems.at[0])
+    dn_copy = pltpu.make_async_copy(dn_hbm, dn_ref, sems.at[1])
+    up_copy.start()
+    dn_copy.start()
+    up_copy.wait()
+    dn_copy.wait()
+    planes = plane_list((up_ref.shape[0] - 1) // 2, up_ref.shape[1] // 2)
     q_count = (up_ref.shape[0] - 1) // 2
     lane = lax.broadcasted_iota(jnp.int32, (2, width), 1)
     zero = jnp.zeros((2, width), jnp.float32)
@@ -91,7 +98,7 @@
         group, slot = divmod(index, width // 2)
         mine = (lane == 2 * slot) | (lane == 2 * slot + 1)
         for side, shift in ((0, (2 * slot - (width - 2)) % width), (1, (2 * slot) % width)):
-            for part, value in enumerate((up_ref[row_index, z], dn_ref[row_index, z])):
+            for part, value in enumerate((up_ref[row_index, 2 * z : 2 * z + 2], dn_ref[row_index, 2 * z : 2 * z + 2])):
                 key = (side, part, group)
                 acc[key] = jnp.where(mine, pltpu.roll(value, shift, 1), acc[key])
     zero_tail = jnp.zeros((ROWS - TOP - height - 2, width), jnp.float32)
@@ -103,11 +110,15 @@
             out[g, TOP + height + 2 : ROWS] = zero_tail
 
 
-def compute_kernel(f_hbm, cot_hbm, solid_ref, up_ref, dn_ref, from_left_ref, from_right_ref,
-                   grad_ref, sbar_ref, ef, ec, es, cf, bo, sb2, f_ref, cot_ref, sems):
+def compute_kernel(f_hbm, cot_hbm, solid_ref, up_hbm, dn_hbm, from_left_ref, from_right_ref,
+                   grad_ref, sbar_ref, ef, ec, es, cf, bo, sb2, f_ref, cot_ref, up_ref, dn_ref, sems):
     q_count, layers, height, width = f_ref.shape
+    up_copy = pltpu.make_async_copy(up_hbm, up_ref, sems.at[2])
+    dn_copy = pltpu.make_async_copy(dn_hbm, dn_ref, sems.at[3])
     f_copy = pltpu.make_async_copy(f_hbm, f_ref, sems.at[0])
     cot_copy = pltpu.make_async_copy(cot_hbm, cot_ref, sems.at[1])
+    up_copy.start()
+    dn_copy.start()
     f_copy.start()
     cot_copy.start()
     lane = lax.broadcasted_iota(jnp.int32, (ROWS, width), 1)
@@ -125,10 +136,12 @@
         target[TOP + height : TOP + height + 2, 0:width] = dn_rows
 
     targets = []
+    up_copy.wait()
+    dn_copy.wait()
     for index, (field, q, z) in enumerate(plane_list(q_count, layers)):
         row_index = field * q_count + q
         target = (ef.at[q, z], ec.at[q, z], es.at[z])[field]
-        place_halo(target, index, up_ref[row_index, z], dn_ref[row_index, z])
+        place_halo(target, index, up_ref[row_index, 2 * z : 2 * z + 2], dn_ref[row_index, 2 * z : 2 * z + 2])
         targets.append((field, q, z, target))
     f_copy.wait()
     cot_copy.wait()
@@ -222,11 +235,12 @@
         return lax.ppermute(value, axis, [(i, (i + step) % size) for i in range(size)])
 
     cot32 = cotangent.astype(jnp.float32)
-    first_rows = jnp.concatenate([f_start[:, :, 0:2], cot32[:, :, 0:2], solid[None, :, 0:2]], axis=0)
-    last_rows = jnp.concatenate(
-        [f_start[:, :, rows_dev - 2 :], cot32[:, :, rows_dev - 2 :], solid[None, :, rows_dev - 2 :]],
-        axis=0,
-    )
+    def edge_rows(chosen):
+        rows = jnp.concatenate([f_start[:, :, chosen], cot32[:, :, chosen], solid[None, :, chosen]], axis=0)
+        return rows.reshape(rows.shape[0], 2 * layers_dev, cols_dev)
+
+    first_rows = edge_rows(slice(0, 2))
+    last_rows = edge_rows(slice(rows_dev - 2, rows_dev))
     up_rows = shift(last_rows, "gy", ny, 1)
     dn_rows = shift(first_rows, "gy", ny, -1)
     plane_count = (2 * q_count + 1) * layers_dev
@@ -242,8 +256,13 @@
     to_right, to_left = pl.pallas_call(
         pack_edge_kernel,
         out_shape=(buffer, buffer),
-        in_specs=vmem_specs(4),
+        in_specs=vmem_specs(2) + [pl.BlockSpec(memory_space=pltpu.HBM)] * 2,
         out_specs=tuple(vmem_specs(2)),
+        scratch_shapes=[
+            pltpu.VMEM(up_rows.shape, jnp.float32),
+            pltpu.VMEM(dn_rows.shape, jnp.float32),
+            pltpu.SemaphoreType.DMA((2,)),
+        ],
     )(own_right, own_left, up_rows, dn_rows)
     from_left = shift(to_right, "gx", nx, 1)
     from_right = shift(to_left, "gx", nx, -1)
@@ -254,7 +273,8 @@
             jax.ShapeDtypeStruct(f_start.shape, jnp.float32),
             jax.ShapeDtypeStruct(solid.shape, jnp.float32),
         ),
-        in_specs=[pl.BlockSpec(memory_space=pl.ANY)] * 2 + vmem_specs(5),
+        in_specs=[pl.BlockSpec(memory_space=pltpu.HBM)] * 2 + vmem_specs(1)
+        + [pl.BlockSpec(memory_space=pltpu.HBM)] * 2 + vmem_specs(2),
         out_specs=tuple(vmem_specs(2)),
         scratch_shapes=[
             big,
@@ -265,9 +285,11 @@
             pltpu.VMEM((layers_dev, ROWS - 8, LANES), jnp.float32),
             pltpu.VMEM(f_start.shape, jnp.float32),
             pltpu.VMEM(cotangent.shape, cotangent.dtype),
-            pltpu.SemaphoreType.DMA((2,)),
+            pltpu.VMEM(up_rows.shape, jnp.float32),
+            pltpu.VMEM(dn_rows.shape, jnp.float32),
+            pltpu.SemaphoreType.DMA((4,)),
         ],
-        compiler_params=pltpu.CompilerParams(vmem_limit_bytes=48 * 1024 * 1024),
+        compiler_params=pltpu.CompilerParams(vmem_limit_bytes=28 * 1024 * 1024),
     )(f_start, cotangent, solid, up_rows, dn_rows, from_left, from_right)
     tile_sums = jnp.sum(solid_bar.reshape(brick_count, 128), axis=1)
     brick_sum = jnp.sum(brick_hit * tile_sums[None, :], axis=1)

time: 46.2 us -> 49 us (1.061)
  other arithmetic: 2.55 us -> 3.91 us
  Pallas kernels: 20.3 us -> 21.5 us
    convert_element_type x0 -> x1, other arithmetic: none -> 1.45 us  [on_device(): cot32 = cotangent.astype(jnp.float32)]
    pallas_call x1, Pallas kernels: 2.44 us -> 3.23 us  [on_device(): pl.pallas_call(pack_edge_kernel, out_shape=(buffer, buffer), in_specs=vme...]
    slice x2 -> x3, local copies, waits for them, and re-layouts: 1.35 us -> 1.22 us  [the longest x1 1.13 us: edge_rows(): f_start[:, :, chosen]]
    unnamed x18 -> x20, local copies, waits for them, and re-layouts: 2.54 us -> 2.55 us
where the time goes in v5:
time: 49 us; the launch traced here: 48.7 us
  Pallas kernels  21.5 us (44%)
  starting transfers between devices  9.36 us (19%)
  waiting for transfers between devices  8.18 us (17%)
  local copies, waits for them, and re-layouts  4.95 us (10%)
  other arithmetic  3.91 us (8%)
  between operations  0.79 us (2%)
    pallas_call x1, Pallas kernels, on_device(): pl.pallas_call(compute_kernel, out_shape=(jax.ShapeDtypeStruct(f_start.sh...  15 us
    ppermute x4, starting transfers between devices, shift(): lax.ppermute(value, axis, [(i, (i + step) % size) for i in range(size)])  9.36 us
    ppermute x4, waiting for transfers between devices, shift(): lax.ppermute(value, axis, [(i, (i + step) % size) for i in range(size)])  8.18 us
    pallas_call x1, Pallas kernels, on_device(): pl.pallas_call(pack_edge_kernel, out_shape=(buffer, buffer), in_specs=vme...  3.23 us
    pallas_call x1, Pallas kernels, on_device(): pl.pallas_call(pack_own_kernel, out_shape=(own_buffer, own_buffer), in_sp...  3.21 us
    unnamed x20, local copies, waits for them, and re-layouts  2.55 us
    convert_element_type x1, other arithmetic, on_device(): cot32 = cotangent.astype(jnp.float32)  1.45 us
    slice x1, local copies, waits for them, and re-layouts, edge_rows(): f_start[:, :, chosen]  1.13 us
  transfers between devices with their start and end apart: 4, of which 2 were waited for; matrix products, arithmetic and copies ran while one was open for 2% of the time, Pallas kernels for 7%

profile of v5, /device:TPU:6, one launch (start us, length us, event | category | flops | bytes accessed | tf_op | source)
XLA Modules:
  0.0 48.7 jit_solution(9746440484469181265)
XLA Ops:
  0.6 0.8 %select_reduce_fusion.3 = f32[64]{0:T(128)S(1)} fusion(f32[16]{0:T(128)} %bitcast.8, s32[64]{0:T(128)} %bitcast.11), kind=kLoop, calls=%fused_computation.7 | loop fusion | flops 3008 | bytes 576 | tf_op jit(solution)/shard_map/reduce_sum | solution.py:227
  1.4 0.7 %select_reduce_fusion.1 = f32[128]{0:T(128)S(1)} fusion(f32[64]{0:T(128)S(1)} %select_reduce_fusion.3, s32[64]{0:T(128)} %bitcast.9), kind=kLoop, calls=%fused_computation.4 | loop fusion | flops 24448 | bytes 1024 | tf_op jit(solution)/shard_map/reduce_sum | solution.py:228
  2.1 0.1 broadcast_in_dim.6
  2.2 0.1 fusion.2
  2.3 1.5 %copy_convert_fusion = f32[19,4,32,128]{3,0,2,1:T(8,128)S(1)} fusion(bf16[19,4,32,128]{3,2,1,0:T(8,128)(2,1)} %cot_hbm.1), kind=kLoop, calls=%fused_computation | loop fusion | flops 311296 | bytes 1867776 | tf_op jit(solution)/shard_map/convert_element_type | solution.py:237
  3.8 1.1 %fusion.1 = (f32[19,4,2,128]{3,2,1,0:T(2,128)S(1)}, f32[19,4,2,128]{3,2,1,0:T(2,128)S(1)}) fusion(f32[19,4,32,128]{3,2,1,0:T(8,128)} %f_hbm.1), kind=kLoop, calls=%fused_computation.10 | loop fusion | bytes 311296 | tf_op jit(solution)/shard_map/slice | solution.py:239
  5.0 0.1 broadcast_in_dim.7
  5.0 0.1 broadcast_in_dim.8
  5.2 0.0 copy-start
  5.2 0.0 copy-start.1
  5.2 0.1 copy.14
  5.3 0.1 collective-permute-start
  5.4 0.1 copy.16
  5.5 6.4 %collective-permute-start.1 = (f32[39,8,128]{2,1,0:T(8,128)S(1)}, f32[39,8,128]{2,1,0:T(8,128)S(1)}, u32[]{:S(2)}, u32[]{:S(2)}) collective-permute-start(f32[39,8,128]{2,1,0:T(8,128)S(1)} %bitcast.7), channel_id=1, source_target_pairs={{0,31},{1,0},{2,1},{3,2},{4,3},{5,4},{6,5},{7,6},{8,7},{9,8},{10,9... | collective-permute-start | bytes 479240 | tf_op jit(solution)/shard_map/ppermute | solution.py:235
  11.8 0.7 %reshape.29.solid_ref = f32[4,32,128]{2,1,0:T(8,128)} broadcast(f32[4,32]{1,0:T(4,128)S(1)} %broadcast_in_dim.6), dimensions={0,1} | broadcast | bytes 66048 | tf_op jit(solution)/shard_map/reshape | solution.py:232
  12.5 0.0 copy-start.6
  12.5 3.2 %shard_map.68 = (f32[3,32,128]{2,1,0:T(8,128)}, f32[3,32,128]{2,1,0:T(8,128)}) custom-call(f32[19,4,32,128]{3,2,1,0:T(8,128)} %f_hbm.1, bf16[19,4,32,128]{3,2,1,0:T(8,128)(2,1)} %cot_hbm.1, f32[4,32,128]{2,1,0:T(8,128)} %reshape.29.solid_ref), custom_call_target="tpu_custom_call" | custom-call | tf_op jit(solution)/shard_map/pallas_call | solution.py:250
  15.8 0.0 copy-start.7
  15.8 0.0 copy-start.8
  15.8 0.0 collective-permute-done.up_hbm
  15.8 0.0 copy-start.2
  15.8 0.0 collective-permute-done.1.dn_hbm
  15.8 0.0 copy-start.4
  15.8 0.6 %copy-done.2 = f32[39,8,128]{2,1,0:T(8,128)} copy-done((f32[39,8,128]{2,1,0:T(8,128)}, f32[39,8,128]{2,1,0:T(8,128)S(1)}, u32[]{:S(2)}) %copy-start.2) | copy-done | bytes 159768
  16.4 0.0 copy-done.4
  16.5 3.2 %shard_map.69 = (f32[3,48,128]{2,1,0:T(8,128)}, f32[3,48,128]{2,1,0:T(8,128)}) custom-call(f32[3,32,128]{2,1,0:T(8,128)} %get-tuple-element.8.own_right_ref, f32[3,32,128]{2,1,0:T(8,128)} %get-tuple-element.9.own_left_ref, f32[39,8,128]{2,1,0:T(8,128)} %copy-done.2, f32[39,8,128]{2,1,0:T(8,128)} %copy-done.4), custom_call_target="tpu_custom_call" | custom-call | tf_op jit(solution)/shard_map/pallas_call | solution.py:256
  19.7 2.9 %collective-permute-start.2 = (f32[3,48,128]{2,1,0:T(8,128)}, f32[3,48,128]{2,1,0:T(8,128)S(1)}, u32[]{:S(2)}, u32[]{:S(2)}) collective-permute-start(f32[3,48,128]{2,1,0:T(8,128)} %get-tuple-element.10), channel_id=1, source_target_pairs={{0,32},{32,64},{64,96},{96,128},{128,160},{160,192},{192,224},{224... | collective-permute-start | bytes 221192 | tf_op jit(solution)/shard_map/ppermute | solution.py:235
  22.6 0.0 collective-permute-start.3
  22.6 2.3 %collective-permute-done.2.from_left_ref = f32[3,48,128]{2,1,0:T(8,128)S(1)} collective-permute-done((f32[3,48,128]{2,1,0:T(8,128)}, f32[3,48,128]{2,1,0:T(8,128)S(1)}, u32[]{:S(2)}, u32[]{:S(2)}) %collective-permute-start.2) | collective-permute-done | bytes 73760 | tf_op jit(solution)/shard_map/ppermute | solution.py:235
  24.9 5.9 %collective-permute-done.3.from_right_ref = f32[3,48,128]{2,1,0:T(8,128)S(1)} collective-permute-done((f32[3,48,128]{2,1,0:T(8,128)}, f32[3,48,128]{2,1,0:T(8,128)S(1)}, u32[]{:S(2)}, u32[]{:S(2)}) %collective-permute-start.3) | collective-permute-done | bytes 73760 | tf_op jit(solution)/shard_map/ppermute | solution.py:235
  30.8 0.0 copy-done
  30.8 0.0 copy-done.1
  30.8 0.0 copy-done.6
  30.8 0.0 copy-start.3
  30.8 0.9 %copy-done.3 = f32[39,8,128]{2,1,0:T(8,128)S(1)} copy-done((f32[39,8,128]{2,1,0:T(8,128)S(1)}, f32[39,8,128]{2,1,0:T(8,128)}, u32[]{:S(2)}) %copy-start.3) | copy-done | bytes 159768
  31.7 0.0 copy-start.5
  31.7 0.9 %copy-done.5 = f32[39,8,128]{2,1,0:T(8,128)S(1)} copy-done((f32[39,8,128]{2,1,0:T(8,128)S(1)}, f32[39,8,128]{2,1,0:T(8,128)}, u32[]{:S(2)}) %copy-start.5) | copy-done | bytes 159768
  32.6 15.0 %shard_map.70 = (f32[19,4,32,128]{3,2,1,0:T(8,128)}, f32[4,32,128]{2,1,0:T(8,128)S(1)}) custom-call(f32[19,4,32,128]{3,2,1,0:T(8,128)S(1)} %copy-done, bf16[19,4,32,128]{3,2,1,0:T(8,128)(2,1)S(1)} %copy-done.1, f32[4,32,128]{2,1,0:T(8,128)S(1)} %copy-done.6, f32[39,8,128]{2,1,0:T(8,128)S(1)} %copy-done.3, f32[39,8,128]{2,1,0:T(8,128)S(1)} %copy-done.5, ...), custom_call_target="tpu_custom_call" | custom-call | tf_op jit(solution)/shard_map/pallas_call | solution.py:270
  47.7 0.1 reduce_sum.47
  47.8 0.1 mul.41
  47.8 0.0 copy-done.7
  47.8 0.2 select_reduce_fusion
  48.0 0.0 copy-done.8
  48.0 0.6 %select_reduce_fusion.2 = f32[16]{0:T(128)} fusion(f32[64]{0:T(128)S(1)} %select_reduce_fusion, s32[64]{0:T(128)S(1)} %bitcast.12), kind=kLoop, calls=%fused_computation.6 | loop fusion | flops 3056 | bytes 576 | tf_op jit(solution)/shard_map/reduce_sum | solution.py:296
  (4 shorter events, 0.1 us)
Async XLA Ops:
  5.2 25.6 %copy-start = (f32[19,4,32,128]{3,2,1,0:T(8,128)S(1)}, f32[19,4,32,128]{3,2,1,0:T(8,128)}, u32[]{:S(2)}) copy-start(f32[19,4,32,128]{3,2,1,0:T(8,128)} %f_hbm.1) | copy-start | bytes 3735556
  5.2 25.6 %copy-start.1 = (bf16[19,4,32,128]{3,2,1,0:T(8,128)(2,1)S(1)}, bf16[19,4,32,128]{3,2,1,0:T(8,128)(2,1)}, u32[]{:S(2)}) copy-start(bf16[19,4,32,128]{3,2,1,0:T(8,128)(2,1)} %cot_hbm.1) | copy-start | bytes 1867780
  5.3 10.5 %collective-permute-start = (f32[39,8,128]{2,1,0:T(8,128)S(1)}, f32[39,8,128]{2,1,0:T(8,128)S(1)}, u32[]{:S(2)}, u32[]{:S(2)}) collective-permute-start(f32[39,8,128]{2,1,0:T(8,128)S(1)} %bitcast.6), channel_id=1, source_target_pairs={{0,1},{1,2},{2,3},{3,4},{4,5},{5,6},{6,7},{7,8},{8,9},{9,10},{10,1... | collective-permute-start | bytes 479240 | tf_op jit(solution)/shard_map/ppermute | solution.py:235
  5.5 10.3 %collective-permute-start.1 = (f32[39,8,128]{2,1,0:T(8,128)S(1)}, f32[39,8,128]{2,1,0:T(8,128)S(1)}, u32[]{:S(2)}, u32[]{:S(2)}) collective-permute-start(f32[39,8,128]{2,1,0:T(8,128)S(1)} %bitcast.7), channel_id=1, source_target_pairs={{0,31},{1,0},{2,1},{3,2},{4,3},{5,4},{6,5},{7,6},{8,7},{9,8},{10,9... | collective-permute-start | bytes 479240 | tf_op jit(solution)/shard_map/ppermute | solution.py:235
  12.5 18.2 %copy-start.6 = (f32[4,32,128]{2,1,0:T(8,128)S(1)}, f32[4,32,128]{2,1,0:T(8,128)}, u32[]{:S(2)}) copy-start(f32[4,32,128]{2,1,0:T(8,128)} %reshape.29.solid_ref) | copy-start | bytes 196612
  15.8 32.1 %copy-start.7 = (s32[1,1,64]{2,1,0:T(1,128)S(1)}, s32[1,1,64]{2,1,0:T(1,128)}, u32[]{:S(2)}) copy-start(s32[1,1,64]{2,1,0:T(1,128)} %param.8) | copy-start | bytes 772
  15.8 32.3 %copy-start.8 = (s32[1,1,64]{2,1,0:T(1,128)S(1)}, s32[1,1,64]{2,1,0:T(1,128)}, u32[]{:S(2)}) copy-start(s32[1,1,64]{2,1,0:T(1,128)} %param.9) | copy-start | bytes 772
  15.8 0.7 %copy-start.2 = (f32[39,8,128]{2,1,0:T(8,128)}, f32[39,8,128]{2,1,0:T(8,128)S(1)}, u32[]{:S(2)}) copy-start(f32[39,8,128]{2,1,0:T(8,128)S(1)} %collective-permute-done.up_hbm) | copy-start | bytes 479236
  15.8 0.7 %copy-start.4 = (f32[39,8,128]{2,1,0:T(8,128)}, f32[39,8,128]{2,1,0:T(8,128)S(1)}, u32[]{:S(2)}) copy-start(f32[39,8,128]{2,1,0:T(8,128)S(1)} %collective-permute-done.1.dn_hbm) | copy-start | bytes 479236
  19.7 5.2 %collective-permute-start.2 = (f32[3,48,128]{2,1,0:T(8,128)}, f32[3,48,128]{2,1,0:T(8,128)S(1)}, u32[]{:S(2)}, u32[]{:S(2)}) collective-permute-start(f32[3,48,128]{2,1,0:T(8,128)} %get-tuple-element.10), channel_id=1, source_target_pairs={{0,32},{32,64},{64,96},{96,128},{128,160},{160,192},{192,224},{224... | collective-permute-start | bytes 221192 | tf_op jit(solution)/shard_map/ppermute | solution.py:235
  22.6 8.2 %collective-permute-start.3 = (f32[3,48,128]{2,1,0:T(8,128)}, f32[3,48,128]{2,1,0:T(8,128)S(1)}, u32[]{:S(2)}, u32[]{:S(2)}) collective-permute-start(f32[3,48,128]{2,1,0:T(8,128)} %get-tuple-element.11), channel_id=1, source_target_pairs={{0,224},{32,0},{64,32},{96,64},{128,96},{160,128},{192,160},{224,1... | collective-permute-start | bytes 221192 | tf_op jit(solution)/shard_map/ppermute | solution.py:235
  30.8 0.9 %copy-start.3 = (f32[39,8,128]{2,1,0:T(8,128)S(1)}, f32[39,8,128]{2,1,0:T(8,128)}, u32[]{:S(2)}) copy-start(f32[39,8,128]{2,1,0:T(8,128)} %copy-done.2) | copy-start | bytes 479236
  31.7 0.9 %copy-start.5 = (f32[39,8,128]{2,1,0:T(8,128)S(1)}, f32[39,8,128]{2,1,0:T(8,128)}, u32[]{:S(2)}) copy-start(f32[39,8,128]{2,1,0:T(8,128)} %copy-done.4) | copy-start | bytes 479236

commit v6 on v4

--- a/solution.py
+++ b/solution.py
@@ -48,6 +48,62 @@
         balance = float(WEIGHTS[q]) * density * shape
         out.append(fields[q] - RELAX_RATE * (fields[q] - balance))
     return out
+
+
+def collide_vjp(fields, solid, cots):
+    density = fields[0]
+    for value in fields[1:]:
+        density = density + value
+    recip = 1.0 / density
+    scale = (1.0 - solid) * recip
+    moments = []
+    for direction in (DIR_X, DIR_Y, DIR_Z):
+        total = None
+        for q in range(19):
+            if direction[q] == 0:
+                continue
+            term = fields[q] if direction[q] > 0 else -fields[q]
+            total = term if total is None else total + term
+        moments.append(total)
+    vel = [m * scale for m in moments]
+    square = vel[0] * vel[0] + vel[1] * vel[1] + vel[2] * vel[2]
+    weighted_sum = None
+    density_part = None
+    dv = [None, None, None]
+    for q in range(19):
+        weighted = (RELAX_RATE * float(WEIGHTS[q])) * cots[q]
+        weighted_sum = weighted if weighted_sum is None else weighted_sum + weighted
+        along = None
+        for sign, v in zip((DIR_X[q], DIR_Y[q], DIR_Z[q]), vel):
+            if sign == 0:
+                continue
+            term = v if sign > 0 else -v
+            along = term if along is None else along + term
+        if along is None:
+            shape = 1.0 - 1.5 * square
+        else:
+            shape = 1.0 + along * (3.0 + 4.5 * along) - 1.5 * square
+            slope = weighted * (3.0 + 9.0 * along)
+            for axis, sign in enumerate((DIR_X[q], DIR_Y[q], DIR_Z[q])):
+                if sign == 0:
+                    continue
+                term = slope if sign > 0 else -slope
+                dv[axis] = term if dv[axis] is None else dv[axis] + term
+        part = weighted * shape
+        density_part = part if density_part is None else density_part + part
+    dv = [density * (d - 3.0 * v * weighted_sum) for d, v in zip(dv, vel)]
+    through = (moments[0] * dv[0] + moments[1] * dv[1] + moments[2] * dv[2]) * recip
+    common = density_part - scale * through
+    scaled = [scale * d for d in dv]
+    grads = []
+    for q in range(19):
+        grad = (1.0 - RELAX_RATE) * cots[q] + common
+        for sign, d in zip((DIR_X[q], DIR_Y[q], DIR_Z[q]), scaled):
+            if sign == 0:
+                continue
+            grad = grad + d if sign > 0 else grad - d
+        grads.append(grad)
+    return grads, -through
 
 
 def plane_list(q_count, layers):
@@ -162,8 +218,7 @@
                 moved.append(pltpu.roll(src, ex % LANES, 1) if ex else src)
                 src = ec[q, (z + ez) % layers, pl.ds(start + ey, 8), :]
                 back.append(pltpu.roll(src, (-ex) % LANES, 1) if ex else src)
-            ignored, undo = jax.vjp(collide, moved, es[z, pl.ds(start, 8), :])
-            grad_field, grad_solid = undo(back)
+            grad_field, grad_solid = collide_vjp(moved, es[z, pl.ds(start, 8), :], back)
             for q in range(q_count):
                 bo[q, z, pl.ds(8 * k, 8), :] = grad_field[q]
             sb2[z, pl.ds(8 * k, 8), :] = grad_solid
@@ -182,8 +237,7 @@
                     src = pltpu.roll(src, (-ex) % LANES, 1)
                 pulled.append(src[:, 0:width])
             field = [f_ref[q, z, rows, :] for q in range(q_count)]
-            ignored, undo = jax.vjp(collide, field, solid_ref[z, rows, :])
-            grad_field, grad_solid = undo(pulled)
+            grad_field, grad_solid = collide_vjp(field, solid_ref[z, rows, :], pulled)
             for q in range(q_count):
                 grad_ref[q, z, rows, :] = grad_field[q]
             sbar_ref[z, rows, :] = grad_solid + sb2[z, pl.ds(1 + 8 * k, 8), 0:width]

time: 46.2 us -> 43.5 us (0.942)
  Pallas kernels: 20.3 us -> 17.7 us
    pallas_call x1, Pallas kernels: 14.6 us -> 12 us  [on_device(): pl.pallas_call(compute_kernel, out_shape=(jax.ShapeDtypeStruct(f_start.sh...]
where the time goes in v6:
time: 43.5 us; the launch traced here: 43.3 us
  Pallas kernels  17.7 us (41%)
  starting transfers between devices  9.28 us (21%)
  waiting for transfers between devices  8.18 us (19%)
  local copies, waits for them, and re-layouts  4.9 us (11%)
  other arithmetic  2.55 us (6%)
  between operations  0.73 us (2%)
    pallas_call x1, Pallas kernels, on_device(): pl.pallas_call(compute_kernel, out_shape=(jax.ShapeDtypeStruct(f_start.sh...  12 us
    ppermute x4, starting transfers between devices, shift(): lax.ppermute(value, axis, [(i, (i + step) % size) for i in range(size)])  9.28 us
    ppermute x4, waiting for transfers between devices, shift(): lax.ppermute(value, axis, [(i, (i + step) % size) for i in range(size)])  8.18 us
    pallas_call x1, Pallas kernels, on_device(): pl.pallas_call(pack_own_kernel, out_shape=(own_buffer, own_buffer), in_sp...  3.22 us
    unnamed x18, local copies, waits for them, and re-layouts  2.54 us
    pallas_call x1, Pallas kernels, on_device(): pl.pallas_call(pack_edge_kernel, out_shape=(buffer, buffer), in_specs=vme...  2.44 us
    slice x1, local copies, waits for them, and re-layouts, on_device(): f_start[:, :, 0:2]  1.28 us
  transfers between devices with their start and end apart: 4, of which 2 were waited for; matrix products, arithmetic and copies ran while one was open for 2% of the time, Pallas kernels for 7%

profile of v6, /device:TPU:6, one launch (start us, length us, event | category | flops | bytes accessed | tf_op | source)
XLA Modules:
  0.0 43.3 jit_solution(8281014430484140145)
XLA Ops:
  0.6 0.8 %select_reduce_fusion.3 = f32[64]{0:T(128)S(1)} fusion(f32[16]{0:T(128)} %bitcast.4, s32[64]{0:T(128)} %bitcast.7), kind=kLoop, calls=%fused_computation.6 | loop fusion | flops 3008 | bytes 576 | tf_op jit(solution)/shard_map/reduce_sum | solution.py:268
  1.4 0.7 %select_reduce_fusion.1 = f32[128]{0:T(128)S(1)} fusion(f32[64]{0:T(128)S(1)} %select_reduce_fusion.3, s32[64]{0:T(128)} %bitcast.5), kind=kLoop, calls=%fused_computation.3 | loop fusion | flops 24448 | bytes 1024 | tf_op jit(solution)/shard_map/reduce_sum | solution.py:269
  2.1 0.1 broadcast_in_dim.6
  2.2 0.1 fusion.2
  2.3 1.3 %fusion = (f32[19,4,2,128]{3,2,1,0:T(2,128)S(1)}, f32[19,4,2,128]{3,2,1,0:T(2,128)S(1)}, f32[19,4,2,128]{3,2,1,0:T(2,128)S(1)}, f32[19,4,2,128]{3,2,1,0:T(2,128)S(1)}) fusion(f32[19,4,32,128]{3,2,1,0:T(8,128)} %f_hbm.1, bf16[19,4,32,128]{3,2,1,0:T(8,128)(2,1)} %cot_hbm.1), kind=kLoop, calls=%fused_computation.8 | loop fusion | bytes 622592 | tf_op jit(solution)/shard_map/slice | solution.py:279
  3.6 0.1 broadcast_in_dim.7
  3.7 0.1 pad_maximum_fusion
  3.7 0.1 collective-permute-start
  3.8 0.1 broadcast_in_dim.8
  3.9 0.1 pad_maximum_fusion.1
  4.0 0.0 copy-start
  4.0 0.0 copy-start.1
  4.0 6.4 %collective-permute-start.1 = (f32[39,4,2,128]{3,2,1,0:T(2,128)S(1)}, f32[39,4,2,128]{3,2,1,0:T(2,128)S(1)}, u32[]{:S(2)}, u32[]{:S(2)}) collective-permute-start(f32[39,4,2,128]{3,2,1,0:T(2,128)S(1)} %pad_maximum_fusion.1), channel_id=1, source_target_pairs={{0,31},{1,0},{2,1},{3,2},{4,3},{5,4},{6,5},{7,6},{8,7},{9,8},{10,9... | collective-permute-start | bytes 479240 | tf_op jit(solution)/shard_map/ppermute | solution.py:276
  10.4 0.7 %reshape.23.solid_ref = f32[4,32,128]{2,1,0:T(8,128)} broadcast(f32[4,32]{1,0:T(4,128)S(1)} %broadcast_in_dim.6), dimensions={0,1} | broadcast | bytes 66048 | tf_op jit(solution)/shard_map/reshape | solution.py:273
  11.1 0.0 copy-start.6
  11.1 3.2 %shard_map.68 = (f32[3,32,128]{2,1,0:T(8,128)}, f32[3,32,128]{2,1,0:T(8,128)}) custom-call(f32[19,4,32,128]{3,2,1,0:T(8,128)} %f_hbm.1, bf16[19,4,32,128]{3,2,1,0:T(8,128)(2,1)} %cot_hbm.1, f32[4,32,128]{2,1,0:T(8,128)} %reshape.23.solid_ref), custom_call_target="tpu_custom_call" | custom-call | tf_op jit(solution)/shard_map/pallas_call | solution.py:290
  14.3 0.0 collective-permute-done.up_ref
  14.3 0.0 copy-start.2
  14.3 0.0 collective-permute-done.1.dn_ref
  14.3 0.0 copy-start.4
  14.3 0.6 %copy-done.2 = f32[39,4,2,128]{3,2,1,0:T(2,128)} copy-done((f32[39,4,2,128]{3,2,1,0:T(2,128)}, f32[39,4,2,128]{3,2,1,0:T(2,128)S(1)}, u32[]{:S(2)}) %copy-start.2) | copy-done | bytes 159768
  15.0 0.0 copy-done.4
  15.0 2.4 %shard_map.69 = (f32[3,48,128]{2,1,0:T(8,128)}, f32[3,48,128]{2,1,0:T(8,128)}) custom-call(f32[3,32,128]{2,1,0:T(8,128)} %get-tuple-element.8.own_right_ref, f32[3,32,128]{2,1,0:T(8,128)} %get-tuple-element.9.own_left_ref, f32[39,4,2,128]{3,2,1,0:T(2,128)} %copy-done.2, f32[39,4,2,128]{3,2,1,0:T(2,128)} %copy-done.4), custom_call_target="tpu_custom_call" | custom-call | tf_op jit(solution)/shard_map/pallas_call | solution.py:296
  17.5 0.0 copy-start.7
  17.5 0.0 copy-start.8
  17.5 2.8 %collective-permute-start.2 = (f32[3,48,128]{2,1,0:T(8,128)}, f32[3,48,128]{2,1,0:T(8,128)S(1)}, u32[]{:S(2)}, u32[]{:S(2)}) collective-permute-start(f32[3,48,128]{2,1,0:T(8,128)} %get-tuple-element.10), channel_id=1, source_target_pairs={{0,32},{32,64},{64,96},{96,128},{128,160},{160,192},{192,224},{224... | collective-permute-start | bytes 221192 | tf_op jit(solution)/shard_map/ppermute | solution.py:276
  20.3 0.0 collective-permute-start.3
  20.3 2.3 %collective-permute-done.2.from_left_ref = f32[3,48,128]{2,1,0:T(8,128)S(1)} collective-permute-done((f32[3,48,128]{2,1,0:T(8,128)}, f32[3,48,128]{2,1,0:T(8,128)S(1)}, u32[]{:S(2)}, u32[]{:S(2)}) %collective-permute-start.2) | collective-permute-done | bytes 73760 | tf_op jit(solution)/shard_map/ppermute | solution.py:276
  22.6 5.9 %collective-permute-done.3.from_right_ref = f32[3,48,128]{2,1,0:T(8,128)S(1)} collective-permute-done((f32[3,48,128]{2,1,0:T(8,128)}, f32[3,48,128]{2,1,0:T(8,128)S(1)}, u32[]{:S(2)}, u32[]{:S(2)}) %collective-permute-start.3) | collective-permute-done | bytes 73760 | tf_op jit(solution)/shard_map/ppermute | solution.py:276
  28.4 0.0 copy-done
  28.5 0.0 copy-done.1
  28.5 0.0 copy-done.6
  28.5 0.0 copy-start.3
  28.5 0.9 %copy-done.3 = f32[39,4,2,128]{3,2,1,0:T(2,128)S(1)} copy-done((f32[39,4,2,128]{3,2,1,0:T(2,128)S(1)}, f32[39,4,2,128]{3,2,1,0:T(2,128)}, u32[]{:S(2)}) %copy-start.3) | copy-done | bytes 159768
  29.4 0.0 copy-start.5
  29.4 0.9 %copy-done.5 = f32[39,4,2,128]{3,2,1,0:T(2,128)S(1)} copy-done((f32[39,4,2,128]{3,2,1,0:T(2,128)S(1)}, f32[39,4,2,128]{3,2,1,0:T(2,128)}, u32[]{:S(2)}) %copy-start.5) | copy-done | bytes 159768
  30.3 12.0 %shard_map.70 = (f32[19,4,32,128]{3,2,1,0:T(8,128)}, f32[4,32,128]{2,1,0:T(8,128)S(1)}) custom-call(f32[19,4,32,128]{3,2,1,0:T(8,128)S(1)} %copy-done, bf16[19,4,32,128]{3,2,1,0:T(8,128)(2,1)S(1)} %copy-done.1, f32[4,32,128]{2,1,0:T(8,128)S(1)} %copy-done.6, f32[39,4,2,128]{3,2,1,0:T(2,128)S(1)} %copy-done.3, f32[39,4,2,128]{3,2,1,0:T(2,128)S(1)} %copy-done.5, ...), custom_call_target="tpu_custom_call" | custom-call | tf_op jit(solution)/shard_map/pallas_call | solution.py:305
  42.3 0.1 reduce_sum.47
  42.4 0.1 mul.41
  42.5 0.0 copy-done.7
  42.5 0.2 select_reduce_fusion
  42.7 0.0 copy-done.8
  42.7 0.6 %select_reduce_fusion.2 = f32[16]{0:T(128)} fusion(f32[64]{0:T(128)S(1)} %select_reduce_fusion, s32[64]{0:T(128)S(1)} %bitcast.8), kind=kLoop, calls=%fused_computation.5 | loop fusion | flops 3056 | bytes 576 | tf_op jit(solution)/shard_map/reduce_sum | solution.py:328
Async XLA Ops:
  3.7 10.6 %collective-permute-start = (f32[39,4,2,128]{3,2,1,0:T(2,128)S(1)}, f32[39,4,2,128]{3,2,1,0:T(2,128)S(1)}, u32[]{:S(2)}, u32[]{:S(2)}) collective-permute-start(f32[39,4,2,128]{3,2,1,0:T(2,128)S(1)} %pad_maximum_fusion), channel_id=1, source_target_pairs={{0,1},{1,2},{2,3},{3,4},{4,5},{5,6},{6,7},{7,8},{8,9},{9,10},{10,1... | collective-permute-start | bytes 479240 | tf_op jit(solution)/shard_map/ppermute | solution.py:276
  4.0 24.5 %copy-start = (f32[19,4,32,128]{3,2,1,0:T(8,128)S(1)}, f32[19,4,32,128]{3,2,1,0:T(8,128)}, u32[]{:S(2)}) copy-start(f32[19,4,32,128]{3,2,1,0:T(8,128)} %f_hbm.1) | copy-start | bytes 3735556
  4.0 24.5 %copy-start.1 = (bf16[19,4,32,128]{3,2,1,0:T(8,128)(2,1)S(1)}, bf16[19,4,32,128]{3,2,1,0:T(8,128)(2,1)}, u32[]{:S(2)}) copy-start(bf16[19,4,32,128]{3,2,1,0:T(8,128)(2,1)} %cot_hbm.1) | copy-start | bytes 1867780
  4.0 10.3 %collective-permute-start.1 = (f32[39,4,2,128]{3,2,1,0:T(2,128)S(1)}, f32[39,4,2,128]{3,2,1,0:T(2,128)S(1)}, u32[]{:S(2)}, u32[]{:S(2)}) collective-permute-start(f32[39,4,2,128]{3,2,1,0:T(2,128)S(1)} %pad_maximum_fusion.1), channel_id=1, source_target_pairs={{0,31},{1,0},{2,1},{3,2},{4,3},{5,4},{6,5},{7,6},{8,7},{9,8},{10,9... | collective-permute-start | bytes 479240 | tf_op jit(solution)/shard_map/ppermute | solution.py:276
  11.1 17.4 %copy-start.6 = (f32[4,32,128]{2,1,0:T(8,128)S(1)}, f32[4,32,128]{2,1,0:T(8,128)}, u32[]{:S(2)}) copy-start(f32[4,32,128]{2,1,0:T(8,128)} %reshape.23.solid_ref) | copy-start | bytes 196612
  14.3 0.7 %copy-start.2 = (f32[39,4,2,128]{3,2,1,0:T(2,128)}, f32[39,4,2,128]{3,2,1,0:T(2,128)S(1)}, u32[]{:S(2)}) copy-start(f32[39,4,2,128]{3,2,1,0:T(2,128)S(1)} %collective-permute-done.up_ref) | copy-start | bytes 479236
  14.3 0.7 %copy-start.4 = (f32[39,4,2,128]{3,2,1,0:T(2,128)}, f32[39,4,2,128]{3,2,1,0:T(2,128)S(1)}, u32[]{:S(2)}) copy-start(f32[39,4,2,128]{3,2,1,0:T(2,128)S(1)} %collective-permute-done.1.dn_ref) | copy-start | bytes 479236
  17.5 25.1 %copy-start.7 = (s32[1,1,64]{2,1,0:T(1,128)S(1)}, s32[1,1,64]{2,1,0:T(1,128)}, u32[]{:S(2)}) copy-start(s32[1,1,64]{2,1,0:T(1,128)} %param.8) | copy-start | bytes 772
  17.5 25.2 %copy-start.8 = (s32[1,1,64]{2,1,0:T(1,128)S(1)}, s32[1,1,64]{2,1,0:T(1,128)}, u32[]{:S(2)}) copy-start(s32[1,1,64]{2,1,0:T(1,128)} %param.9) | copy-start | bytes 772
  17.5 5.1 %collective-permute-start.2 = (f32[3,48,128]{2,1,0:T(8,128)}, f32[3,48,128]{2,1,0:T(8,128)S(1)}, u32[]{:S(2)}, u32[]{:S(2)}) collective-permute-start(f32[3,48,128]{2,1,0:T(8,128)} %get-tuple-element.10), channel_id=1, source_target_pairs={{0,32},{32,64},{64,96},{96,128},{128,160},{160,192},{192,224},{224... | collective-permute-start | bytes 221192 | tf_op jit(solution)/shard_map/ppermute | solution.py:276
  20.3 8.2 %collective-permute-start.3 = (f32[3,48,128]{2,1,0:T(8,128)}, f32[3,48,128]{2,1,0:T(8,128)S(1)}, u32[]{:S(2)}, u32[]{:S(2)}) collective-permute-start(f32[3,48,128]{2,1,0:T(8,128)} %get-tuple-element.11), channel_id=1, source_target_pairs={{0,224},{32,0},{64,32},{96,64},{128,96},{160,128},{192,160},{224,1... | collective-permute-start | bytes 221192 | tf_op jit(solution)/shard_map/ppermute | solution.py:276
  28.5 0.9 %copy-start.3 = (f32[39,4,2,128]{3,2,1,0:T(2,128)S(1)}, f32[39,4,2,128]{3,2,1,0:T(2,128)}, u32[]{:S(2)}) copy-start(f32[39,4,2,128]{3,2,1,0:T(2,128)} %copy-done.2) | copy-start | bytes 479236
  29.4 0.9 %copy-start.5 = (f32[39,4,2,128]{3,2,1,0:T(2,128)S(1)}, f32[39,4,2,128]{3,2,1,0:T(2,128)}, u32[]{:S(2)}) copy-start(f32[39,4,2,128]{3,2,1,0:T(2,128)} %copy-done.4) | copy-start | bytes 479236

commit v7 on v6

--- a/solution.py
+++ b/solution.py
@@ -113,12 +113,12 @@
     return planes
 
 
-def pack_own_kernel(f_ref, cot_ref, solid_ref, to_right_ref, to_left_ref):
+def pack_kernel(f_ref, cot_ref, solid_ref, packed_ref):
     q_count, layers, height, width = f_ref.shape
-    groups = to_right_ref.shape[0]
+    groups = packed_ref.shape[0]
     lane = lax.broadcasted_iota(jnp.int32, (height, width), 1)
     zero = jnp.zeros((height, width), jnp.float32)
-    acc = {(side, g): zero for side in range(2) for g in range(groups)}
+    acc = [zero for g in range(groups)]
     for index, (field, q, z) in enumerate(plane_list(q_count, layers)):
         if field == 0:
             own = f_ref[q, z]
@@ -126,65 +126,51 @@
             own = cot_ref[q, z].astype(jnp.float32)
         else:
             own = solid_ref[z]
-        group, slot = divmod(index, width // 2)
-        mine = (lane == 2 * slot) | (lane == 2 * slot + 1)
-        for side, shift in ((0, (2 * slot - (width - 2)) % width), (1, (2 * slot) % width)):
-            acc[(side, group)] = jnp.where(mine, pltpu.roll(own, shift, 1), acc[(side, group)])
-    for side, out in ((0, to_right_ref), (1, to_left_ref)):
-        for g in range(groups):
-            out[g] = acc[(side, g)]
-
-
-def pack_edge_kernel(own_right_ref, own_left_ref, up_ref, dn_ref, to_right_ref, to_left_ref):
-    groups, height, width = own_right_ref.shape
-    planes = plane_list((up_ref.shape[0] - 1) // 2, up_ref.shape[1])
-    q_count = (up_ref.shape[0] - 1) // 2
-    lane = lax.broadcasted_iota(jnp.int32, (2, width), 1)
-    zero = jnp.zeros((2, width), jnp.float32)
-    acc = {(side, part, g): zero for side in range(2) for part in range(2) for g in range(groups)}
-    for index, (field, q, z) in enumerate(planes):
-        row_index = field * q_count + q
-        group, slot = divmod(index, width // 2)
-        mine = (lane == 2 * slot) | (lane == 2 * slot + 1)
-        for side, shift in ((0, (2 * slot - (width - 2)) % width), (1, (2 * slot) % width)):
-            for part, value in enumerate((up_ref[row_index, z], dn_ref[row_index, z])):
-                key = (side, part, group)
-                acc[key] = jnp.where(mine, pltpu.roll(value, shift, 1), acc[key])
-    zero_tail = jnp.zeros((ROWS - TOP - height - 2, width), jnp.float32)
-    for side, own, out in ((0, own_right_ref, to_right_ref), (1, own_left_ref, to_left_ref)):
-        for g in range(groups):
-            out[g, 0:TOP] = acc[(side, 0, g)]
-            out[g, TOP : TOP + height] = own[g]
-            out[g, TOP + height : TOP + height + 2] = acc[(side, 1, g)]
-            out[g, TOP + height + 2 : ROWS] = zero_tail
+        group, slot = divmod(index, width // 4)
+        mine = (lane >= 4 * slot) & (lane < 4 * slot + 4)
+        acc[group] = jnp.where(mine, pltpu.roll(own, (4 * slot - (width - 2)) % width, 1), acc[group])
+    for g in range(groups):
+        packed_ref[g] = acc[g]
 
 
 def compute_kernel(f_hbm, cot_hbm, solid_ref, up_ref, dn_ref, from_left_ref, from_right_ref,
                    grad_ref, sbar_ref, ef, ec, es, cf, bo, sb2, f_ref, cot_ref, sems):
     q_count, layers, height, width = f_ref.shape
+    groups = from_left_ref.shape[0]
+    corner_base = (2 * q_count + 1) * layers * 2
     f_copy = pltpu.make_async_copy(f_hbm, f_ref, sems.at[0])
     cot_copy = pltpu.make_async_copy(cot_hbm, cot_ref, sems.at[1])
     f_copy.start()
     cot_copy.start()
-    lane = lax.broadcasted_iota(jnp.int32, (ROWS, width), 1)
-    low_lanes = lane < 2
-    high_lanes = lane >= width - 2
+    lane_own = lax.broadcasted_iota(jnp.int32, (height, width), 1)
+    lane_edge = lax.broadcasted_iota(jnp.int32, (2, width), 1)
     tail = ROWS - (TOP + height + 2)
 
-    def place_halo(target, index, up_rows, dn_rows):
-        group, slot = divmod(index, width // 2)
-        from_r = pltpu.roll(from_right_ref[group], (-2 * slot) % width, 1)
-        from_l = pltpu.roll(from_left_ref[group], (width - 2 - 2 * slot) % width, 1)
-        target[:, width:LANES] = jnp.where(low_lanes, from_r, jnp.where(high_lanes, from_l, 0.0))
-        target[TOP + height + 2 : ROWS, 0:width] = jnp.zeros((tail, width), jnp.float32)
-        target[TOP - 2 : TOP, 0:width] = up_rows
-        target[TOP + height : TOP + height + 2, 0:width] = dn_rows
+    def sides(left, right, slot, lane):
+        from_r = pltpu.roll(right, (-(4 * slot + 2)) % width, 1)
+        from_l = pltpu.roll(left, (width - 2 - 4 * slot) % width, 1)
+        return jnp.where(lane < 2, from_r, jnp.where(lane >= width - 2, from_l, 0.0))
+
+    def place_halo(target, index, row_index, z):
+        group, slot = divmod(index, width // 4)
+        base = (row_index * layers + z) * 2
+        left_rows = corner_base + 2 * group
+        right_rows = corner_base + 2 * (groups + group)
+        target[TOP : TOP + height, width:LANES] = sides(
+            from_left_ref[group], from_right_ref[group], slot, lane_own)
+        target[0:TOP, width:LANES] = sides(
+            up_ref[left_rows : left_rows + 2], up_ref[right_rows : right_rows + 2], slot, lane_edge)
+        target[TOP + height : TOP + height + 2, width:LANES] = sides(
+            dn_ref[left_rows : left_rows + 2], dn_ref[right_rows : right_rows + 2], slot, lane_edge)
+        target[TOP + height + 2 : ROWS, :] = jnp.zeros((tail, LANES), jnp.float32)
+        target[0:TOP, 0:width] = up_ref[base : base + 2]
+        target[TOP + height : TOP + height + 2, 0:width] = dn_ref[base : base + 2]
 
     targets = []
     for index, (field, q, z) in enumerate(plane_list(q_count, layers)):
         row_index = field * q_count + q
         target = (ef.at[q, z], ec.at[q, z], es.at[z])[field]
-        place_halo(target, index, up_ref[row_index, z], dn_ref[row_index, z])
+        place_halo(target, index, row_index, z)
         targets.append((field, q, z, target))
     f_copy.wait()
     cot_copy.wait()
@@ -276,31 +262,28 @@
         return lax.ppermute(value, axis, [(i, (i + step) % size) for i in range(size)])
 
     cot32 = cotangent.astype(jnp.float32)
-    first_rows = jnp.concatenate([f_start[:, :, 0:2], cot32[:, :, 0:2], solid[None, :, 0:2]], axis=0)
-    last_rows = jnp.concatenate(
-        [f_start[:, :, rows_dev - 2 :], cot32[:, :, rows_dev - 2 :], solid[None, :, rows_dev - 2 :]],
-        axis=0,
-    )
+    plane_count = (2 * q_count + 1) * layers_dev
+    groups = -(-plane_count // (cols_dev // 4))
+    packed = pl.pallas_call(
+        pack_kernel,
+        out_shape=jax.ShapeDtypeStruct((groups, rows_dev, cols_dev), jnp.float32),
+        in_specs=vmem_specs(3),
+        out_specs=vmem_specs(1)[0],
+    )(f_start, cotangent, solid)
+    from_left = shift(packed, "gx", nx, 1)
+    from_right = shift(packed, "gx", nx, -1)
+
+    def edge_rows(chosen):
+        rows = jnp.concatenate([f_start[:, :, chosen], cot32[:, :, chosen], solid[None, :, chosen]], axis=0)
+        corners = jnp.concatenate([from_left[:, chosen], from_right[:, chosen]], axis=0)
+        return jnp.concatenate(
+            [rows.reshape(-1, cols_dev), corners.reshape(-1, cols_dev)], axis=0
+        )
+
+    first_rows = edge_rows(slice(0, 2))
+    last_rows = edge_rows(slice(rows_dev - 2, rows_dev))
     up_rows = shift(last_rows, "gy", ny, 1)
     dn_rows = shift(first_rows, "gy", ny, -1)
-    plane_count = (2 * q_count + 1) * layers_dev
-    groups = -(-plane_count // (cols_dev // 2))
-    buffer = jax.ShapeDtypeStruct((groups, ROWS, cols_dev), jnp.float32)
-    own_buffer = jax.ShapeDtypeStruct((groups, rows_dev, cols_dev), jnp.float32)
-    own_right, own_left = pl.pallas_call(
-        pack_own_kernel,
-        out_shape=(own_buffer, own_buffer),
-        in_specs=vmem_specs(3),
-        out_specs=tuple(vmem_specs(2)),
-    )(f_start, cotangent, solid)
-    to_right, to_left = pl.pallas_call(
-        pack_edge_kernel,
-        out_shape=(buffer, buffer),
-        in_specs=vmem_specs(4),
-        out_specs=tuple(vmem_specs(2)),
-    )(own_right, own_left, up_rows, dn_rows)
-    from_left = shift(to_right, "gx", nx, 1)
-    from_right = shift(to_left, "gx", nx, -1)
     big = pltpu.VMEM((q_count, layers_dev, ROWS, LANES), jnp.float32)
     start_grad, solid_bar = pl.pallas_call(
         compute_kernel,

time: 43.5 us -> 43.2 us (level)
  the two profiles are of different devices: /device:TPU:6 before, /device:TPU:105 now
where the time goes in v7:
time: 43.2 us; the launch traced here: 43 us
  Pallas kernels  14.9 us (34%)
  waiting for transfers between devices  13 us (30%)
  starting transfers between devices  10 us (23%)
  other arithmetic  2.93 us (7%)
  local copies, waits for them, and re-layouts  1.42 us (3%)
  between operations  0.8 us (2%)
    ppermute x4, waiting for transfers between devices, shift(): lax.ppermute(value, axis, [(i, (i + step) % size) for i in range(size)])  13 us
    pallas_call x1, Pallas kernels, on_device(): pl.pallas_call(compute_kernel, out_shape=(jax.ShapeDtypeStruct(f_start.sh...  12.2 us
    ppermute x4, starting transfers between devices, shift(): lax.ppermute(value, axis, [(i, (i + step) % size) for i in range(size)])  10 us
    pallas_call x1, Pallas kernels, on_device(): pl.pallas_call(pack_kernel, out_shape=jax.ShapeDtypeStruct((groups, rows_...  2.7 us
  transfers between devices with their start and end apart: 4, of which 4 were waited for; matrix products, arithmetic and copies ran while one was open for 2% of the time, Pallas kernels for 0%

profile of v7, /device:TPU:105, one launch (start us, length us, event | category | flops | bytes accessed | tf_op | source)
XLA Modules:
  0.0 43.0 jit_solution(2695845988220722479)
XLA Ops:
  0.6 0.0 copy-start.1
  0.6 0.8 %select_reduce_fusion.3 = f32[64]{0:T(128)S(1)} fusion(f32[16]{0:T(128)} %bitcast.8, s32[64]{0:T(128)} %bitcast.11), kind=kLoop, calls=%fused_computation.11 | loop fusion | flops 3008 | bytes 576 | tf_op jit(solution)/shard_map/reduce_sum | solution.py:254
  1.5 0.7 %select_reduce_fusion.1 = f32[128]{0:T(128)S(1)} fusion(f32[64]{0:T(128)S(1)} %select_reduce_fusion.3, s32[64]{0:T(128)} %bitcast.9), kind=kLoop, calls=%fused_computation.6 | loop fusion | flops 24448 | bytes 1024 | tf_op jit(solution)/shard_map/reduce_sum | solution.py:255
  2.2 0.1 broadcast_in_dim.6
  2.3 0.7 %reshape.35.solid_ref = f32[4,32,128]{2,1,0:T(8,128)} broadcast(f32[4,32]{1,0:T(4,128)S(1)} %broadcast_in_dim.6), dimensions={0,1} | broadcast | bytes 66048 | tf_op jit(solution)/shard_map/reshape | solution.py:259
  3.0 2.7 %shard_map.68 = f32[5,32,128]{2,1,0:T(8,128)} custom-call(f32[19,4,32,128]{3,2,1,0:T(8,128)} %f_hbm.1, bf16[19,4,32,128]{3,2,1,0:T(8,128)(2,1)} %cot_hbm.1, f32[4,32,128]{2,1,0:T(8,128)} %reshape.35.solid_ref), custom_call_target="tpu_custom_call" | custom-call | tf_op jit(solution)/shard_map/pallas_call | solution.py:267
  5.7 0.0 copy-start
  5.7 4.2 %collective-permute-start.1 = (f32[5,32,128]{2,1,0:T(8,128)}, f32[5,32,128]{2,1,0:T(8,128)S(1)}, u32[]{:S(2)}, u32[]{:S(2)}) collective-permute-start(f32[5,32,128]{2,1,0:T(8,128)} %shard_map.68), channel_id=1, source_target_pairs={{0,224},{32,0},{64,32},{96,64},{128,96},{160,128},{192,160},{224,1... | collective-permute-start | bytes 245768 | tf_op jit(solution)/shard_map/ppermute | solution.py:262
  9.9 0.0 collective-permute-start
  9.9 0.1 fusion.4
  10.0 0.0 copy-done.1
  10.0 0.4 copy_convert_fusion
  10.4 0.0 copy-done
  10.4 0.0 copy-start.2
  10.4 0.1 fusion.1
  10.5 0.1 broadcast_in_dim.7
  10.6 0.1 broadcast_in_dim.8
  10.7 0.1 copy.14
  10.8 0.1 copy.16
  10.9 0.8 %collective-permute-done.1.from_right_ref = f32[5,32,128]{2,1,0:T(8,128)S(1)} collective-permute-done((f32[5,32,128]{2,1,0:T(8,128)}, f32[5,32,128]{2,1,0:T(8,128)S(1)}, u32[]{:S(2)}, u32[]{:S(2)}) %collective-permute-start.1) | collective-permute-done | bytes 81952 | tf_op jit(solution)/shard_map/ppermute | solution.py:262
  11.7 5.3 %collective-permute-done.from_left_ref = f32[5,32,128]{2,1,0:T(8,128)S(1)} collective-permute-done((f32[5,32,128]{2,1,0:T(8,128)}, f32[5,32,128]{2,1,0:T(8,128)S(1)}, u32[]{:S(2)}, u32[]{:S(2)}) %collective-permute-start) | collective-permute-done | bytes 81952 | tf_op jit(solution)/shard_map/ppermute | solution.py:262
  17.1 0.0 copy-start.3
  17.1 0.0 copy-start.4
  17.1 5.7 %collective-permute-start.2 = (f32[332,128]{1,0:T(8,128)S(1)}, f32[332,128]{1,0:T(8,128)S(1)}, u32[]{:S(2)}, u32[]{:S(2)}) collective-permute-start(f32[332,128]{1,0:T(8,128)S(1)} %pad_maximum_fusion), channel_id=1, source_target_pairs={{0,1},{1,2},{2,3},{3,4},{4,5},{5,6},{6,7},{7,8},{8,9},{9,10},{10,1... | collective-permute-start | bytes 509960 | tf_op jit(solution)/shard_map/ppermute | solution.py:262
  22.9 0.1 collective-permute-start.3
  22.9 2.2 %collective-permute-done.2.up_ref = f32[332,128]{1,0:T(8,128)S(1)} collective-permute-done((f32[332,128]{1,0:T(8,128)S(1)}, f32[332,128]{1,0:T(8,128)S(1)}, u32[]{:S(2)}, u32[]{:S(2)}) %collective-permute-start.2) | collective-permute-done | bytes 170016 | tf_op jit(solution)/shard_map/ppermute | solution.py:262
  25.2 4.7 %collective-permute-done.3.dn_ref = f32[332,128]{1,0:T(8,128)S(1)} collective-permute-done((f32[332,128]{1,0:T(8,128)S(1)}, f32[332,128]{1,0:T(8,128)S(1)}, u32[]{:S(2)}, u32[]{:S(2)}) %collective-permute-start.3) | collective-permute-done | bytes 170016 | tf_op jit(solution)/shard_map/ppermute | solution.py:262
  29.9 0.0 copy-done.2
  29.9 12.2 %shard_map.69 = (f32[19,4,32,128]{3,2,1,0:T(8,128)}, f32[4,32,128]{2,1,0:T(8,128)S(1)}) custom-call(f32[19,4,32,128]{3,2,1,0:T(8,128)S(1)} %copy-done, bf16[19,4,32,128]{3,2,1,0:T(8,128)(2,1)S(1)} %copy-done.1, f32[4,32,128]{2,1,0:T(8,128)S(1)} %copy-done.2, f32[332,128]{1,0:T(8,128)S(1)} %collective-permute-done.2.up_ref, ...), custom_call_target="tpu_custom_call" | custom-call | tf_op jit(solution)/shard_map/pallas_call | solution.py:288
  42.0 0.1 reduce_sum.47
  42.1 0.1 mul.41
  42.2 0.0 copy-done.3
  42.2 0.2 select_reduce_fusion
  42.4 0.0 copy-done.4
  42.4 0.6 %select_reduce_fusion.2 = f32[16]{0:T(128)} fusion(f32[64]{0:T(128)S(1)} %select_reduce_fusion, s32[64]{0:T(128)S(1)} %bitcast.12), kind=kLoop, calls=%fused_computation.10 | loop fusion | flops 3056 | bytes 576 | tf_op jit(solution)/shard_map/reduce_sum | solution.py:311
  (11 shorter events, 0.2 us)
Async XLA Ops:
  0.6 9.4 %copy-start.1 = (bf16[19,4,32,128]{3,2,1,0:T(8,128)(2,1)S(1)}, bf16[19,4,32,128]{3,2,1,0:T(8,128)(2,1)}, u32[]{:S(2)}) copy-start(bf16[19,4,32,128]{3,2,1,0:T(8,128)(2,1)} %cot_hbm.1) | copy-start | bytes 1867780
  5.7 4.7 %copy-start = (f32[19,4,32,128]{3,2,1,0:T(8,128)S(1)}, f32[19,4,32,128]{3,2,1,0:T(8,128)}, u32[]{:S(2)}) copy-start(f32[19,4,32,128]{3,2,1,0:T(8,128)} %f_hbm.1) | copy-start | bytes 3735556
  5.7 6.0 %collective-permute-start.1 = (f32[5,32,128]{2,1,0:T(8,128)}, f32[5,32,128]{2,1,0:T(8,128)S(1)}, u32[]{:S(2)}, u32[]{:S(2)}) collective-permute-start(f32[5,32,128]{2,1,0:T(8,128)} %shard_map.68), channel_id=1, source_target_pairs={{0,224},{32,0},{64,32},{96,64},{128,96},{160,128},{192,160},{224,1... | collective-permute-start | bytes 245768 | tf_op jit(solution)/shard_map/ppermute | solution.py:262
  9.9 7.1 %collective-permute-start = (f32[5,32,128]{2,1,0:T(8,128)}, f32[5,32,128]{2,1,0:T(8,128)S(1)}, u32[]{:S(2)}, u32[]{:S(2)}) collective-permute-start(f32[5,32,128]{2,1,0:T(8,128)} %shard_map.68), channel_id=1, source_target_pairs={{0,32},{32,64},{64,96},{96,128},{128,160},{160,192},{192,224},{224... | collective-permute-start | bytes 245768 | tf_op jit(solution)/shard_map/ppermute | solution.py:262
  10.4 19.5 %copy-start.2 = (f32[4,32,128]{2,1,0:T(8,128)S(1)}, f32[4,32,128]{2,1,0:T(8,128)}, u32[]{:S(2)}) copy-start(f32[4,32,128]{2,1,0:T(8,128)} %reshape.35.solid_ref) | copy-start | bytes 196612
  17.1 25.1 %copy-start.3 = (s32[1,1,64]{2,1,0:T(1,128)S(1)}, s32[1,1,64]{2,1,0:T(1,128)}, u32[]{:S(2)}) copy-start(s32[1,1,64]{2,1,0:T(1,128)} %param.8) | copy-start | bytes 772
  17.1 25.3 %copy-start.4 = (s32[1,1,64]{2,1,0:T(1,128)S(1)}, s32[1,1,64]{2,1,0:T(1,128)}, u32[]{:S(2)}) copy-start(s32[1,1,64]{2,1,0:T(1,128)} %param.9) | copy-start | bytes 772
  17.1 8.1 %collective-permute-start.2 = (f32[332,128]{1,0:T(8,128)S(1)}, f32[332,128]{1,0:T(8,128)S(1)}, u32[]{:S(2)}, u32[]{:S(2)}) collective-permute-start(f32[332,128]{1,0:T(8,128)S(1)} %pad_maximum_fusion), channel_id=1, source_target_pairs={{0,1},{1,2},{2,3},{3,4},{4,5},{5,6},{6,7},{7,8},{8,9},{9,10},{10,1... | collective-permute-start | bytes 509960 | tf_op jit(solution)/shard_map/ppermute | solution.py:262
  22.9 7.0 %collective-permute-start.3 = (f32[332,128]{1,0:T(8,128)S(1)}, f32[332,128]{1,0:T(8,128)S(1)}, u32[]{:S(2)}, u32[]{:S(2)}) collective-permute-start(f32[332,128]{1,0:T(8,128)S(1)} %pad_maximum_fusion.1), channel_id=1, source_target_pairs={{0,31},{1,0},{2,1},{3,2},{4,3},{5,4},{6,5},{7,6},{8,7},{9,8},{10,9... | collective-permute-start | bytes 509960 | tf_op jit(solution)/shard_map/ppermute | solution.py:262

commit v8 on v7

--- a/solution.py
+++ b/solution.py
@@ -113,9 +113,17 @@
     return planes
 
 
-def pack_kernel(f_ref, cot_ref, solid_ref, packed_ref):
+def pack_kernel(f_ref, cot_ref, porosity_ref, ids_ref, slot_ref, packed_ref, solid_ref, tile_ref):
     q_count, layers, height, width = f_ref.shape
     groups = packed_ref.shape[0]
+    for b in range(layers * height):
+        tile_ref[b] = jnp.float32(0.0)
+    for n in range(ids_ref.shape[0]):
+        brick = ids_ref[n]
+        tile_ref[brick] = tile_ref[brick] + porosity_ref[slot_ref[n]]
+    for z in range(layers):
+        for y in range(height):
+            solid_ref[z, y : y + 1, :] = jnp.full((1, width), tile_ref[z * height + y], jnp.float32)
     lane = lax.broadcasted_iota(jnp.int32, (height, width), 1)
     zero = jnp.zeros((height, width), jnp.float32)
     acc = [zero for g in range(groups)]
@@ -251,12 +259,6 @@
     slot_hit = (
         slots_of[:, None] == jnp.arange(slot_table.shape[0], dtype=jnp.int32)[None, :]
     ).astype(jnp.float32)
-    brick_value = jnp.sum(slot_hit * slot_table[None, :], axis=1)
-    tile_value = jnp.sum(brick_hit * brick_value[:, None], axis=0)
-    solid = jnp.broadcast_to(
-        tile_value.reshape(layers_dev, rows_dev, tile_count, 1),
-        (layers_dev, rows_dev, tile_count, 128),
-    ).reshape(layers_dev, rows_dev, cols_dev)
 
     def shift(value, axis, size, step):
         return lax.ppermute(value, axis, [(i, (i + step) % size) for i in range(size)])
@@ -264,12 +266,17 @@
     cot32 = cotangent.astype(jnp.float32)
     plane_count = (2 * q_count + 1) * layers_dev
     groups = -(-plane_count // (cols_dev // 4))
-    packed = pl.pallas_call(
+    smem = pl.BlockSpec(memory_space=pltpu.SMEM)
+    packed, solid = pl.pallas_call(
         pack_kernel,
-        out_shape=jax.ShapeDtypeStruct((groups, rows_dev, cols_dev), jnp.float32),
-        in_specs=vmem_specs(3),
-        out_specs=vmem_specs(1)[0],
-    )(f_start, cotangent, solid)
+        out_shape=(
+            jax.ShapeDtypeStruct((groups, rows_dev, cols_dev), jnp.float32),
+            jax.ShapeDtypeStruct((layers_dev, rows_dev, cols_dev), jnp.float32),
+        ),
+        in_specs=vmem_specs(2) + [smem, smem, smem],
+        out_specs=tuple(vmem_specs(2)),
+        scratch_shapes=[pltpu.SMEM((brick_count,), jnp.float32)],
+    )(f_start, cotangent, slot_table, listed, slots_of)
     from_left = shift(packed, "gx", nx, 1)
     from_right = shift(packed, "gx", nx, -1)
 

time: 43.2 us -> 40.3 us (0.933)
  the two profiles are of different devices: /device:TPU:105 before, /device:TPU:16 now
where the time goes in v8:
time: 40.3 us; the launch traced here: 40.2 us
  Pallas kernels  15 us (37%)
  waiting for transfers between devices  14.1 us (35%)
  starting transfers between devices  8.18 us (20%)
  other arithmetic  1.11 us (3%)
  local copies, waits for them, and re-layouts  0.99 us (2%)
  between operations  0.75 us (2%)
    ppermute x4, waiting for transfers between devices, shift(): lax.ppermute(value, axis, [(i, (i + step) % size) for i in range(size)])  14.1 us
    pallas_call x1, Pallas kernels, on_device(): pl.pallas_call(compute_kernel, out_shape=(jax.ShapeDtypeStruct(f_start.sh...  12.2 us
    ppermute x4, starting transfers between devices, shift(): lax.ppermute(value, axis, [(i, (i + step) % size) for i in range(size)])  8.18 us
    pallas_call x1, Pallas kernels, on_device(): pl.pallas_call(pack_kernel, out_shape=(jax.ShapeDtypeStruct((groups, rows...  2.85 us
  transfers between devices with their start and end apart: 4, of which 4 were waited for; matrix products, arithmetic and copies ran while one was open for 3% of the time, Pallas kernels for 0%

profile of v8, /device:TPU:16, one launch (start us, length us, event | category | flops | bytes accessed | tf_op | source)
XLA Modules:
  0.0 40.2 jit_solution(9402100123050384806)
XLA Ops:
  0.6 0.0 copy-start.1
  0.6 0.0 copy-start
  0.6 2.8 %shard_map.68 = (f32[5,32,128]{2,1,0:T(8,128)}, f32[4,32,128]{2,1,0:T(8,128)}) custom-call(f32[19,4,32,128]{3,2,1,0:T(8,128)} %f_hbm.1, bf16[19,4,32,128]{3,2,1,0:T(8,128)(2,1)} %cot_hbm.1, f32[16]{0:T(128)} %bitcast.12, s32[64]{0:T(128)} %bitcast.13, s32[64]{0:T(128)} %bitcast.15), custom_call_target="tpu_custom_call" | custom-call | tf_op jit(solution)/shard_map/pallas_call | solution.py:270
  3.5 0.0 copy-start.2
  3.5 2.5 %collective-permute-start.1 = (f32[5,32,128]{2,1,0:T(8,128)}, f32[5,32,128]{2,1,0:T(8,128)S(1)}, u32[]{:S(2)}, u32[]{:S(2)}) collective-permute-start(f32[5,32,128]{2,1,0:T(8,128)} %get-tuple-element.7), channel_id=1, source_target_pairs={{0,224},{32,0},{64,32},{96,64},{128,96},{160,128},{192,160},{224,1... | collective-permute-start | bytes 245768 | tf_op jit(solution)/shard_map/ppermute | solution.py:264
  6.0 0.0 collective-permute-start
  6.0 0.0 copy-done
  6.0 0.1 fusion
  6.1 0.0 copy-done.1
  6.1 0.1 fusion.1
  6.2 0.7 %slice_bitcast_fusion = (f32[1,4,2,128]{3,2,1,0:T(2,128)S(1)}, f32[1,4,2,128]{3,2,1,0:T(2,128)S(1)}) fusion(f32[4,32,128]{2,1,0:T(8,128)} %get-tuple-element.6.solid_ref), kind=kLoop, calls=%fused_computation.10 | loop fusion | bytes 16384 | tf_op jit(solution)/shard_map/broadcast_in_dim | solution.py:284
  6.9 0.2 pad_maximum_fusion.2
  7.1 1.3 %collective-permute-done.1.from_right_ref = f32[5,32,128]{2,1,0:T(8,128)S(1)} collective-permute-done((f32[5,32,128]{2,1,0:T(8,128)}, f32[5,32,128]{2,1,0:T(8,128)S(1)}, u32[]{:S(2)}, u32[]{:S(2)}) %collective-permute-start.1) | collective-permute-done | bytes 81952 | tf_op jit(solution)/shard_map/ppermute | solution.py:264
  8.4 5.9 %collective-permute-done.from_left_ref = f32[5,32,128]{2,1,0:T(8,128)S(1)} collective-permute-done((f32[5,32,128]{2,1,0:T(8,128)}, f32[5,32,128]{2,1,0:T(8,128)S(1)}, u32[]{:S(2)}, u32[]{:S(2)}) %collective-permute-start) | collective-permute-done | bytes 81952 | tf_op jit(solution)/shard_map/ppermute | solution.py:264
  14.4 5.6 %collective-permute-start.3 = (f32[332,128]{1,0:T(8,128)S(1)}, f32[332,128]{1,0:T(8,128)S(1)}, u32[]{:S(2)}, u32[]{:S(2)}) collective-permute-start(f32[332,128]{1,0:T(8,128)S(1)} %pad_maximum_fusion.1), channel_id=1, source_target_pairs={{0,31},{1,0},{2,1},{3,2},{4,3},{5,4},{6,5},{7,6},{8,7},{9,8},{10,9... | collective-permute-start | bytes 509960 | tf_op jit(solution)/shard_map/ppermute | solution.py:264
  20.0 0.0 copy-start.3
  20.0 0.0 copy-start.4
  20.0 0.1 collective-permute-start.2
  20.1 2.8 %collective-permute-done.3.dn_ref = f32[332,128]{1,0:T(8,128)S(1)} collective-permute-done((f32[332,128]{1,0:T(8,128)S(1)}, f32[332,128]{1,0:T(8,128)S(1)}, u32[]{:S(2)}, u32[]{:S(2)}) %collective-permute-start.3) | collective-permute-done | bytes 170016 | tf_op jit(solution)/shard_map/ppermute | solution.py:264
  22.9 4.1 %collective-permute-done.2.up_ref = f32[332,128]{1,0:T(8,128)S(1)} collective-permute-done((f32[332,128]{1,0:T(8,128)S(1)}, f32[332,128]{1,0:T(8,128)S(1)}, u32[]{:S(2)}, u32[]{:S(2)}) %collective-permute-start.2) | collective-permute-done | bytes 170016 | tf_op jit(solution)/shard_map/ppermute | solution.py:264
  27.0 0.0 copy-done.2
  27.0 12.2 %shard_map.69 = (f32[19,4,32,128]{3,2,1,0:T(8,128)}, f32[4,32,128]{2,1,0:T(8,128)S(1)}) custom-call(f32[19,4,32,128]{3,2,1,0:T(8,128)S(1)} %copy-done, bf16[19,4,32,128]{3,2,1,0:T(8,128)(2,1)S(1)} %copy-done.1, f32[4,32,128]{2,1,0:T(8,128)S(1)} %copy-done.2, f32[332,128]{1,0:T(8,128)S(1)} %collective-permute-done.2.up_ref, ...), custom_call_target="tpu_custom_call" | custom-call | tf_op jit(solution)/shard_map/pallas_call | solution.py:295
  39.2 0.1 reduce_sum.27
  39.3 0.1 mul.18
  39.3 0.0 copy-done.3
  39.3 0.2 select_reduce_fusion
  39.5 0.0 copy-done.4
  39.5 0.6 %select_reduce_fusion.1 = f32[16]{0:T(128)} fusion(f32[64]{0:T(128)S(1)} %select_reduce_fusion, s32[64]{0:T(128)S(1)} %bitcast.16), kind=kLoop, calls=%fused_computation.8 | loop fusion | flops 3056 | bytes 576 | tf_op jit(solution)/shard_map/reduce_sum | solution.py:318
  (7 shorter events, 0.1 us)
Async XLA Ops:
  0.6 5.5 %copy-start.1 = (bf16[19,4,32,128]{3,2,1,0:T(8,128)(2,1)S(1)}, bf16[19,4,32,128]{3,2,1,0:T(8,128)(2,1)}, u32[]{:S(2)}) copy-start(bf16[19,4,32,128]{3,2,1,0:T(8,128)(2,1)} %cot_hbm.1) | copy-start | bytes 1867780
  0.6 5.4 %copy-start = (f32[19,4,32,128]{3,2,1,0:T(8,128)S(1)}, f32[19,4,32,128]{3,2,1,0:T(8,128)}, u32[]{:S(2)}) copy-start(f32[19,4,32,128]{3,2,1,0:T(8,128)} %f_hbm.1) | copy-start | bytes 3735556
  3.5 23.5 %copy-start.2 = (f32[4,32,128]{2,1,0:T(8,128)S(1)}, f32[4,32,128]{2,1,0:T(8,128)}, u32[]{:S(2)}) copy-start(f32[4,32,128]{2,1,0:T(8,128)} %get-tuple-element.6.solid_ref) | copy-start | bytes 196612
  3.5 4.9 %collective-permute-start.1 = (f32[5,32,128]{2,1,0:T(8,128)}, f32[5,32,128]{2,1,0:T(8,128)S(1)}, u32[]{:S(2)}, u32[]{:S(2)}) collective-permute-start(f32[5,32,128]{2,1,0:T(8,128)} %get-tuple-element.7), channel_id=1, source_target_pairs={{0,224},{32,0},{64,32},{96,64},{128,96},{160,128},{192,160},{224,1... | collective-permute-start | bytes 245768 | tf_op jit(solution)/shard_map/ppermute | solution.py:264
  6.0 8.3 %collective-permute-start = (f32[5,32,128]{2,1,0:T(8,128)}, f32[5,32,128]{2,1,0:T(8,128)S(1)}, u32[]{:S(2)}, u32[]{:S(2)}) collective-permute-start(f32[5,32,128]{2,1,0:T(8,128)} %get-tuple-element.7), channel_id=1, source_target_pairs={{0,32},{32,64},{64,96},{96,128},{128,160},{160,192},{192,224},{224... | collective-permute-start | bytes 245768 | tf_op jit(solution)/shard_map/ppermute | solution.py:264
  14.4 8.5 %collective-permute-start.3 = (f32[332,128]{1,0:T(8,128)S(1)}, f32[332,128]{1,0:T(8,128)S(1)}, u32[]{:S(2)}, u32[]{:S(2)}) collective-permute-start(f32[332,128]{1,0:T(8,128)S(1)} %pad_maximum_fusion.1), channel_id=1, source_target_pairs={{0,31},{1,0},{2,1},{3,2},{4,3},{5,4},{6,5},{7,6},{8,7},{9,8},{10,9... | collective-permute-start | bytes 509960 | tf_op jit(solution)/shard_map/ppermute | solution.py:264
  20.0 19.4 %copy-start.3 = (s32[1,1,64]{2,1,0:T(1,128)S(1)}, s32[1,1,64]{2,1,0:T(1,128)}, u32[]{:S(2)}) copy-start(s32[1,1,64]{2,1,0:T(1,128)} %param.8) | copy-start | bytes 772
  20.0 19.6 %copy-start.4 = (s32[1,1,64]{2,1,0:T(1,128)S(1)}, s32[1,1,64]{2,1,0:T(1,128)}, u32[]{:S(2)}) copy-start(s32[1,1,64]{2,1,0:T(1,128)} %param.9) | copy-start | bytes 772
  20.0 7.0 %collective-permute-start.2 = (f32[332,128]{1,0:T(8,128)S(1)}, f32[332,128]{1,0:T(8,128)S(1)}, u32[]{:S(2)}, u32[]{:S(2)}) collective-permute-start(f32[332,128]{1,0:T(8,128)S(1)} %pad_maximum_fusion), channel_id=1, source_target_pairs={{0,1},{1,2},{2,3},{3,4},{4,5},{5,6},{6,7},{7,8},{8,9},{9,10},{10,1... | collective-permute-start | bytes 509960 | tf_op jit(solution)/shard_map/ppermute | solution.py:264

commit v9 on v8

--- a/solution.py
+++ b/solution.py
@@ -199,7 +199,7 @@
                 cf[q, z, rows, :] = out[q]
         return carry
 
-    lax.fori_loop(0, layers, phase_one, 0)
+    lax.fori_loop(0, layers, phase_one, 0, unroll=True)
 
     def phase_two(z, carry):
         for k in range((ROWS - 8) // 8):
@@ -218,7 +218,7 @@
             sb2[z, pl.ds(8 * k, 8), :] = grad_solid
         return carry
 
-    lax.fori_loop(0, layers, phase_two, 0)
+    lax.fori_loop(0, layers, phase_two, 0, unroll=True)
 
     def phase_three(z, carry):
         for k in range(height // 8):
@@ -237,7 +237,7 @@
             sbar_ref[z, rows, :] = grad_solid + sb2[z, pl.ds(1 + 8 * k, 8), 0:width]
         return carry
 
-    lax.fori_loop(0, layers, phase_three, 0)
+    lax.fori_loop(0, layers, phase_three, 0, unroll=True)
 
 
 def vmem_specs(count):

time: 40.3 us -> 40.7 us (level)
  no operation moved by 1% of the time
where the time goes in v9:
time: 40.7 us; the launch traced here: 40.6 us
  Pallas kernels  15.2 us (37%)
  waiting for transfers between devices  14.1 us (35%)
  starting transfers between devices  8.36 us (21%)
  other arithmetic  1.11 us (3%)
  local copies, waits for them, and re-layouts  0.99 us (2%)
  between operations  0.75 us (2%)
    ppermute x4, waiting for transfers between devices, shift(): lax.ppermute(value, axis, [(i, (i + step) % size) for i in range(size)])  14.1 us
    pallas_call x1, Pallas kernels, on_device(): pl.pallas_call(compute_kernel, out_shape=(jax.ShapeDtypeStruct(f_start.sh...  12.4 us
    ppermute x4, starting transfers between devices, shift(): lax.ppermute(value, axis, [(i, (i + step) % size) for i in range(size)])  8.36 us
    pallas_call x1, Pallas kernels, on_device(): pl.pallas_call(pack_kernel, out_shape=(jax.ShapeDtypeStruct((groups, rows...  2.85 us
  transfers between devices with their start and end apart: 4, of which 4 were waited for; matrix products, arithmetic and copies ran while one was open for 3% of the time, Pallas kernels for 0%

profile of v9, /device:TPU:16, one launch (start us, length us, event | category | flops | bytes accessed | tf_op | source)
XLA Modules:
  0.0 40.6 jit_solution(8435288357261721190)
XLA Ops:
  0.6 0.0 copy-start.1
  0.6 0.0 copy-start
  0.6 2.8 %shard_map.68 = (f32[5,32,128]{2,1,0:T(8,128)}, f32[4,32,128]{2,1,0:T(8,128)}) custom-call(f32[19,4,32,128]{3,2,1,0:T(8,128)} %f_hbm.1, bf16[19,4,32,128]{3,2,1,0:T(8,128)(2,1)} %cot_hbm.1, f32[16]{0:T(128)} %bitcast.12, s32[64]{0:T(128)} %bitcast.13, s32[64]{0:T(128)} %bitcast.15), custom_call_target="tpu_custom_call" | custom-call | tf_op jit(solution)/shard_map/pallas_call | solution.py:270
  3.5 0.0 copy-start.2
  3.5 2.5 %collective-permute-start.1 = (f32[5,32,128]{2,1,0:T(8,128)}, f32[5,32,128]{2,1,0:T(8,128)S(1)}, u32[]{:S(2)}, u32[]{:S(2)}) collective-permute-start(f32[5,32,128]{2,1,0:T(8,128)} %get-tuple-element.7), channel_id=1, source_target_pairs={{0,224},{32,0},{64,32},{96,64},{128,96},{160,128},{192,160},{224,1... | collective-permute-start | bytes 245768 | tf_op jit(solution)/shard_map/ppermute | solution.py:264
  6.0 0.0 collective-permute-start
  6.0 0.0 copy-done
  6.0 0.1 fusion
  6.1 0.0 copy-done.1
  6.1 0.1 fusion.1
  6.2 0.7 %slice_bitcast_fusion = (f32[1,4,2,128]{3,2,1,0:T(2,128)S(1)}, f32[1,4,2,128]{3,2,1,0:T(2,128)S(1)}) fusion(f32[4,32,128]{2,1,0:T(8,128)} %get-tuple-element.6.solid_ref), kind=kLoop, calls=%fused_computation.10 | loop fusion | bytes 16384 | tf_op jit(solution)/shard_map/broadcast_in_dim | solution.py:284
  6.9 0.2 pad_maximum_fusion.2
  7.1 1.3 %collective-permute-done.1.from_right_ref = f32[5,32,128]{2,1,0:T(8,128)S(1)} collective-permute-done((f32[5,32,128]{2,1,0:T(8,128)}, f32[5,32,128]{2,1,0:T(8,128)S(1)}, u32[]{:S(2)}, u32[]{:S(2)}) %collective-permute-start.1) | collective-permute-done | bytes 81952 | tf_op jit(solution)/shard_map/ppermute | solution.py:264
  8.4 5.9 %collective-permute-done.from_left_ref = f32[5,32,128]{2,1,0:T(8,128)S(1)} collective-permute-done((f32[5,32,128]{2,1,0:T(8,128)}, f32[5,32,128]{2,1,0:T(8,128)S(1)}, u32[]{:S(2)}, u32[]{:S(2)}) %collective-permute-start) | collective-permute-done | bytes 81952 | tf_op jit(solution)/shard_map/ppermute | solution.py:264
  14.4 5.6 %collective-permute-start.3 = (f32[332,128]{1,0:T(8,128)S(1)}, f32[332,128]{1,0:T(8,128)S(1)}, u32[]{:S(2)}, u32[]{:S(2)}) collective-permute-start(f32[332,128]{1,0:T(8,128)S(1)} %pad_maximum_fusion.1), channel_id=1, source_target_pairs={{0,31},{1,0},{2,1},{3,2},{4,3},{5,4},{6,5},{7,6},{8,7},{9,8},{10,9... | collective-permute-start | bytes 509960 | tf_op jit(solution)/shard_map/ppermute | solution.py:264
  20.0 0.0 copy-start.3
  20.0 0.0 copy-start.4
  20.0 0.3 collective-permute-start.2
  20.2 2.6 %collective-permute-done.3.dn_ref = f32[332,128]{1,0:T(8,128)S(1)} collective-permute-done((f32[332,128]{1,0:T(8,128)S(1)}, f32[332,128]{1,0:T(8,128)S(1)}, u32[]{:S(2)}, u32[]{:S(2)}) %collective-permute-start.3) | collective-permute-done | bytes 170016 | tf_op jit(solution)/shard_map/ppermute | solution.py:264
  22.9 4.3 %collective-permute-done.2.up_ref = f32[332,128]{1,0:T(8,128)S(1)} collective-permute-done((f32[332,128]{1,0:T(8,128)S(1)}, f32[332,128]{1,0:T(8,128)S(1)}, u32[]{:S(2)}, u32[]{:S(2)}) %collective-permute-start.2) | collective-permute-done | bytes 170016 | tf_op jit(solution)/shard_map/ppermute | solution.py:264
  27.2 0.0 copy-done.2
  27.2 12.4 %shard_map.69 = (f32[19,4,32,128]{3,2,1,0:T(8,128)}, f32[4,32,128]{2,1,0:T(8,128)S(1)}) custom-call(f32[19,4,32,128]{3,2,1,0:T(8,128)S(1)} %copy-done, bf16[19,4,32,128]{3,2,1,0:T(8,128)(2,1)S(1)} %copy-done.1, f32[4,32,128]{2,1,0:T(8,128)S(1)} %copy-done.2, f32[332,128]{1,0:T(8,128)S(1)} %collective-permute-done.2.up_ref, ...), custom_call_target="tpu_custom_call" | custom-call | tf_op jit(solution)/shard_map/pallas_call | solution.py:295
  39.6 0.1 reduce_sum.27
  39.7 0.1 mul.18
  39.7 0.0 copy-done.3
  39.7 0.2 select_reduce_fusion
  39.9 0.0 copy-done.4
  39.9 0.6 %select_reduce_fusion.1 = f32[16]{0:T(128)} fusion(f32[64]{0:T(128)S(1)} %select_reduce_fusion, s32[64]{0:T(128)S(1)} %bitcast.16), kind=kLoop, calls=%fused_computation.8 | loop fusion | flops 3056 | bytes 576 | tf_op jit(solution)/shard_map/reduce_sum | solution.py:318
  (7 shorter events, 0.1 us)
Async XLA Ops:
  0.6 5.5 %copy-start.1 = (bf16[19,4,32,128]{3,2,1,0:T(8,128)(2,1)S(1)}, bf16[19,4,32,128]{3,2,1,0:T(8,128)(2,1)}, u32[]{:S(2)}) copy-start(bf16[19,4,32,128]{3,2,1,0:T(8,128)(2,1)} %cot_hbm.1) | copy-start | bytes 1867780
  0.6 5.4 %copy-start = (f32[19,4,32,128]{3,2,1,0:T(8,128)S(1)}, f32[19,4,32,128]{3,2,1,0:T(8,128)}, u32[]{:S(2)}) copy-start(f32[19,4,32,128]{3,2,1,0:T(8,128)} %f_hbm.1) | copy-start | bytes 3735556
  3.5 23.7 %copy-start.2 = (f32[4,32,128]{2,1,0:T(8,128)S(1)}, f32[4,32,128]{2,1,0:T(8,128)}, u32[]{:S(2)}) copy-start(f32[4,32,128]{2,1,0:T(8,128)} %get-tuple-element.6.solid_ref) | copy-start | bytes 196612
  3.5 4.9 %collective-permute-start.1 = (f32[5,32,128]{2,1,0:T(8,128)}, f32[5,32,128]{2,1,0:T(8,128)S(1)}, u32[]{:S(2)}, u32[]{:S(2)}) collective-permute-start(f32[5,32,128]{2,1,0:T(8,128)} %get-tuple-element.7), channel_id=1, source_target_pairs={{0,224},{32,0},{64,32},{96,64},{128,96},{160,128},{192,160},{224,1... | collective-permute-start | bytes 245768 | tf_op jit(solution)/shard_map/ppermute | solution.py:264
  6.0 8.3 %collective-permute-start = (f32[5,32,128]{2,1,0:T(8,128)}, f32[5,32,128]{2,1,0:T(8,128)S(1)}, u32[]{:S(2)}, u32[]{:S(2)}) collective-permute-start(f32[5,32,128]{2,1,0:T(8,128)} %get-tuple-element.7), channel_id=1, source_target_pairs={{0,32},{32,64},{64,96},{96,128},{128,160},{160,192},{192,224},{224... | collective-permute-start | bytes 245768 | tf_op jit(solution)/shard_map/ppermute | solution.py:264
  14.4 8.5 %collective-permute-start.3 = (f32[332,128]{1,0:T(8,128)S(1)}, f32[332,128]{1,0:T(8,128)S(1)}, u32[]{:S(2)}, u32[]{:S(2)}) collective-permute-start(f32[332,128]{1,0:T(8,128)S(1)} %pad_maximum_fusion.1), channel_id=1, source_target_pairs={{0,31},{1,0},{2,1},{3,2},{4,3},{5,4},{6,5},{7,6},{8,7},{9,8},{10,9... | collective-permute-start | bytes 509960 | tf_op jit(solution)/shard_map/ppermute | solution.py:264
  20.0 19.8 %copy-start.3 = (s32[1,1,64]{2,1,0:T(1,128)S(1)}, s32[1,1,64]{2,1,0:T(1,128)}, u32[]{:S(2)}) copy-start(s32[1,1,64]{2,1,0:T(1,128)} %param.8) | copy-start | bytes 772
  20.0 20.0 %copy-start.4 = (s32[1,1,64]{2,1,0:T(1,128)S(1)}, s32[1,1,64]{2,1,0:T(1,128)}, u32[]{:S(2)}) copy-start(s32[1,1,64]{2,1,0:T(1,128)} %param.9) | copy-start | bytes 772
  20.0 7.2 %collective-permute-start.2 = (f32[332,128]{1,0:T(8,128)S(1)}, f32[332,128]{1,0:T(8,128)S(1)}, u32[]{:S(2)}, u32[]{:S(2)}) collective-permute-start(f32[332,128]{1,0:T(8,128)S(1)} %pad_maximum_fusion), channel_id=1, source_target_pairs={{0,1},{1,2},{2,3},{3,4},{4,5},{5,6},{6,7},{7,8},{8,9},{9,10},{10,1... | collective-permute-start | bytes 509960 | tf_op jit(solution)/shard_map/ppermute | solution.py:264

commit v10 on v8

--- a/solution.py
+++ b/solution.py
@@ -170,7 +170,6 @@
             up_ref[left_rows : left_rows + 2], up_ref[right_rows : right_rows + 2], slot, lane_edge)
         target[TOP + height : TOP + height + 2, width:LANES] = sides(
             dn_ref[left_rows : left_rows + 2], dn_ref[right_rows : right_rows + 2], slot, lane_edge)
-        target[TOP + height + 2 : ROWS, :] = jnp.zeros((tail, LANES), jnp.float32)
         target[0:TOP, 0:width] = up_ref[base : base + 2]
         target[TOP + height : TOP + height + 2, 0:width] = dn_ref[base : base + 2]
 

time: 40.3 us -> 40.1 us (level)
  no operation moved by 1% of the time
where the time goes in v10:
time: 40.1 us; the launch traced here: 40 us
  Pallas kernels  14.8 us (37%)
  waiting for transfers between devices  14.1 us (35%)
  starting transfers between devices  8.18 us (20%)
  other arithmetic  1.11 us (3%)
  local copies, waits for them, and re-layouts  0.99 us (2%)
  between operations  0.75 us (2%)
    ppermute x4, waiting for transfers between devices, shift(): lax.ppermute(value, axis, [(i, (i + step) % size) for i in range(size)])  14.1 us
    pallas_call x1, Pallas kernels, on_device(): pl.pallas_call(compute_kernel, out_shape=(jax.ShapeDtypeStruct(f_start.sh...  12 us
    ppermute x4, starting transfers between devices, shift(): lax.ppermute(value, axis, [(i, (i + step) % size) for i in range(size)])  8.18 us
    pallas_call x1, Pallas kernels, on_device(): pl.pallas_call(pack_kernel, out_shape=(jax.ShapeDtypeStruct((groups, rows...  2.85 us
  transfers between devices with their start and end apart: 4, of which 4 were waited for; matrix products, arithmetic and copies ran while one was open for 3% of the time, Pallas kernels for 0%

profile of v10, /device:TPU:16, one launch (start us, length us, event | category | flops | bytes accessed | tf_op | source)
XLA Modules:
  0.0 40.0 jit_solution(7841536610568285945)
XLA Ops:
  0.6 0.0 copy-start.1
  0.6 0.0 copy-start
  0.6 2.8 %shard_map.68 = (f32[5,32,128]{2,1,0:T(8,128)}, f32[4,32,128]{2,1,0:T(8,128)}) custom-call(f32[19,4,32,128]{3,2,1,0:T(8,128)} %f_hbm.1, bf16[19,4,32,128]{3,2,1,0:T(8,128)(2,1)} %cot_hbm.1, f32[16]{0:T(128)} %bitcast.12, s32[64]{0:T(128)} %bitcast.13, s32[64]{0:T(128)} %bitcast.15), custom_call_target="tpu_custom_call" | custom-call | tf_op jit(solution)/shard_map/pallas_call | solution.py:269
  3.5 0.0 copy-start.2
  3.5 2.5 %collective-permute-start.1 = (f32[5,32,128]{2,1,0:T(8,128)}, f32[5,32,128]{2,1,0:T(8,128)S(1)}, u32[]{:S(2)}, u32[]{:S(2)}) collective-permute-start(f32[5,32,128]{2,1,0:T(8,128)} %get-tuple-element.7), channel_id=1, source_target_pairs={{0,224},{32,0},{64,32},{96,64},{128,96},{160,128},{192,160},{224,1... | collective-permute-start | bytes 245768 | tf_op jit(solution)/shard_map/ppermute | solution.py:263
  6.0 0.0 collective-permute-start
  6.0 0.0 copy-done
  6.0 0.1 fusion
  6.1 0.0 copy-done.1
  6.1 0.1 fusion.1
  6.2 0.7 %slice_bitcast_fusion = (f32[1,4,2,128]{3,2,1,0:T(2,128)S(1)}, f32[1,4,2,128]{3,2,1,0:T(2,128)S(1)}) fusion(f32[4,32,128]{2,1,0:T(8,128)} %get-tuple-element.6.solid_ref), kind=kLoop, calls=%fused_computation.10 | loop fusion | bytes 16384 | tf_op jit(solution)/shard_map/broadcast_in_dim | solution.py:283
  6.9 0.2 pad_maximum_fusion.2
  7.1 1.3 %collective-permute-done.1.from_right_ref = f32[5,32,128]{2,1,0:T(8,128)S(1)} collective-permute-done((f32[5,32,128]{2,1,0:T(8,128)}, f32[5,32,128]{2,1,0:T(8,128)S(1)}, u32[]{:S(2)}, u32[]{:S(2)}) %collective-permute-start.1) | collective-permute-done | bytes 81952 | tf_op jit(solution)/shard_map/ppermute | solution.py:263
  8.4 5.9 %collective-permute-done.from_left_ref = f32[5,32,128]{2,1,0:T(8,128)S(1)} collective-permute-done((f32[5,32,128]{2,1,0:T(8,128)}, f32[5,32,128]{2,1,0:T(8,128)S(1)}, u32[]{:S(2)}, u32[]{:S(2)}) %collective-permute-start) | collective-permute-done | bytes 81952 | tf_op jit(solution)/shard_map/ppermute | solution.py:263
  14.4 5.6 %collective-permute-start.3 = (f32[332,128]{1,0:T(8,128)S(1)}, f32[332,128]{1,0:T(8,128)S(1)}, u32[]{:S(2)}, u32[]{:S(2)}) collective-permute-start(f32[332,128]{1,0:T(8,128)S(1)} %pad_maximum_fusion.1), channel_id=1, source_target_pairs={{0,31},{1,0},{2,1},{3,2},{4,3},{5,4},{6,5},{7,6},{8,7},{9,8},{10,9... | collective-permute-start | bytes 509960 | tf_op jit(solution)/shard_map/ppermute | solution.py:263
  20.0 0.0 copy-start.3
  20.0 0.0 copy-start.4
  20.0 0.1 collective-permute-start.2
  20.1 2.8 %collective-permute-done.3.dn_ref = f32[332,128]{1,0:T(8,128)S(1)} collective-permute-done((f32[332,128]{1,0:T(8,128)S(1)}, f32[332,128]{1,0:T(8,128)S(1)}, u32[]{:S(2)}, u32[]{:S(2)}) %collective-permute-start.3) | collective-permute-done | bytes 170016 | tf_op jit(solution)/shard_map/ppermute | solution.py:263
  22.9 4.1 %collective-permute-done.2.up_ref = f32[332,128]{1,0:T(8,128)S(1)} collective-permute-done((f32[332,128]{1,0:T(8,128)S(1)}, f32[332,128]{1,0:T(8,128)S(1)}, u32[]{:S(2)}, u32[]{:S(2)}) %collective-permute-start.2) | collective-permute-done | bytes 170016 | tf_op jit(solution)/shard_map/ppermute | solution.py:263
  27.0 0.0 copy-done.2
  27.0 12.0 %shard_map.69 = (f32[19,4,32,128]{3,2,1,0:T(8,128)}, f32[4,32,128]{2,1,0:T(8,128)S(1)}) custom-call(f32[19,4,32,128]{3,2,1,0:T(8,128)S(1)} %copy-done, bf16[19,4,32,128]{3,2,1,0:T(8,128)(2,1)S(1)} %copy-done.1, f32[4,32,128]{2,1,0:T(8,128)S(1)} %copy-done.2, f32[332,128]{1,0:T(8,128)S(1)} %collective-permute-done.2.up_ref, ...), custom_call_target="tpu_custom_call" | custom-call | tf_op jit(solution)/shard_map/pallas_call | solution.py:294
  39.0 0.1 reduce_sum.27
  39.1 0.1 mul.18
  39.2 0.0 copy-done.3
  39.2 0.2 select_reduce_fusion
  39.4 0.0 copy-done.4
  39.4 0.6 %select_reduce_fusion.1 = f32[16]{0:T(128)} fusion(f32[64]{0:T(128)S(1)} %select_reduce_fusion, s32[64]{0:T(128)S(1)} %bitcast.16), kind=kLoop, calls=%fused_computation.8 | loop fusion | flops 3056 | bytes 576 | tf_op jit(solution)/shard_map/reduce_sum | solution.py:317
  (7 shorter events, 0.1 us)
Async XLA Ops:
  0.6 5.5 %copy-start.1 = (bf16[19,4,32,128]{3,2,1,0:T(8,128)(2,1)S(1)}, bf16[19,4,32,128]{3,2,1,0:T(8,128)(2,1)}, u32[]{:S(2)}) copy-start(bf16[19,4,32,128]{3,2,1,0:T(8,128)(2,1)} %cot_hbm.1) | copy-start | bytes 1867780
  0.6 5.4 %copy-start = (f32[19,4,32,128]{3,2,1,0:T(8,128)S(1)}, f32[19,4,32,128]{3,2,1,0:T(8,128)}, u32[]{:S(2)}) copy-start(f32[19,4,32,128]{3,2,1,0:T(8,128)} %f_hbm.1) | copy-start | bytes 3735556
  3.5 23.5 %copy-start.2 = (f32[4,32,128]{2,1,0:T(8,128)S(1)}, f32[4,32,128]{2,1,0:T(8,128)}, u32[]{:S(2)}) copy-start(f32[4,32,128]{2,1,0:T(8,128)} %get-tuple-element.6.solid_ref) | copy-start | bytes 196612
  3.5 4.9 %collective-permute-start.1 = (f32[5,32,128]{2,1,0:T(8,128)}, f32[5,32,128]{2,1,0:T(8,128)S(1)}, u32[]{:S(2)}, u32[]{:S(2)}) collective-permute-start(f32[5,32,128]{2,1,0:T(8,128)} %get-tuple-element.7), channel_id=1, source_target_pairs={{0,224},{32,0},{64,32},{96,64},{128,96},{160,128},{192,160},{224,1... | collective-permute-start | bytes 245768 | tf_op jit(solution)/shard_map/ppermute | solution.py:263
  6.0 8.3 %collective-permute-start = (f32[5,32,128]{2,1,0:T(8,128)}, f32[5,32,128]{2,1,0:T(8,128)S(1)}, u32[]{:S(2)}, u32[]{:S(2)}) collective-permute-start(f32[5,32,128]{2,1,0:T(8,128)} %get-tuple-element.7), channel_id=1, source_target_pairs={{0,32},{32,64},{64,96},{96,128},{128,160},{160,192},{192,224},{224... | collective-permute-start | bytes 245768 | tf_op jit(solution)/shard_map/ppermute | solution.py:263
  14.4 8.5 %collective-permute-start.3 = (f32[332,128]{1,0:T(8,128)S(1)}, f32[332,128]{1,0:T(8,128)S(1)}, u32[]{:S(2)}, u32[]{:S(2)}) collective-permute-start(f32[332,128]{1,0:T(8,128)S(1)} %pad_maximum_fusion.1), channel_id=1, source_target_pairs={{0,31},{1,0},{2,1},{3,2},{4,3},{5,4},{6,5},{7,6},{8,7},{9,8},{10,9... | collective-permute-start | bytes 509960 | tf_op jit(solution)/shard_map/ppermute | solution.py:263
  20.0 19.2 %copy-start.3 = (s32[1,1,64]{2,1,0:T(1,128)S(1)}, s32[1,1,64]{2,1,0:T(1,128)}, u32[]{:S(2)}) copy-start(s32[1,1,64]{2,1,0:T(1,128)} %param.8) | copy-start | bytes 772
  20.0 19.4 %copy-start.4 = (s32[1,1,64]{2,1,0:T(1,128)S(1)}, s32[1,1,64]{2,1,0:T(1,128)}, u32[]{:S(2)}) copy-start(s32[1,1,64]{2,1,0:T(1,128)} %param.9) | copy-start | bytes 772
  20.0 7.0 %collective-permute-start.2 = (f32[332,128]{1,0:T(8,128)S(1)}, f32[332,128]{1,0:T(8,128)S(1)}, u32[]{:S(2)}, u32[]{:S(2)}) collective-permute-start(f32[332,128]{1,0:T(8,128)S(1)} %pad_maximum_fusion), channel_id=1, source_target_pairs={{0,1},{1,2},{2,3},{3,4},{4,5},{5,6},{6,7},{7,8},{8,9},{9,10},{10,1... | collective-permute-start | bytes 509960 | tf_op jit(solution)/shard_map/ppermute | solution.py:263
